TPU v7x, 128 devices: a whole 4x4x4 slice. The times are simulated.
128 devices in a mesh: srow: 8 (over y_lo, z), scol: 16 (over y_hi, x, core).
Axes of the slice: x: 4, y: 4 (y_hi: 2, y_lo: 2; y = y_hi * 2 + y_lo), z: 4, core: 2. Of those that a mesh axis runs over, the one named last changes fastest.
Arguments:
- frames: bfloat16 [512, 1024, 256], P('srow', 'scol'), may hold values from 0.19921875 to 1.796875
- pixel_gain: float32 [256], replicated, may hold values from 0.5 to 1.5
- eigen_flats: float32 [16, 256], replicated, may hold values from -0.375 to 0.375
- pixels: int32 [256], replicated, may hold values from 0 to 1023, as said below
Outputs:
- object_wave: float32 [512, 2, 1024], P('scol', None, 'srow')
Inputs may be any that keep to these rules, and one draw needn't show every extreme that they name: Distinct indices y * 32 + x of detector pixels whose centre offset (x - 16, y - 16) lies within 13 pixels.
All inputs are finite; a program needn't handle non-finite values.
Results may differ from a plain program's by a relative error of at most 0.011.
Values may be sent and summed in bfloat16 or wider, within the bound.
No kernel may reach another device: no remote copies, remote signals or barrier semaphores. Data moves between devices by JAX's collectives and lax.ppermute only.
A program may use at most 128 MiB of HBM per device.

v0:
```python
import math

import jax
import jax.numpy as jnp
from jax import lax
from jax.sharding import PartitionSpec as P

DET = 32
RAD = 13
HIGHEST = lax.Precision.HIGHEST


def waves(left_ids, right_ids, length):
    product = left_ids[:, None] * right_ids[None, :] % length
    phases = product.astype(jnp.float32) * (2.0 * math.pi / length)
    return (jnp.cos(phases), jnp.sin(phases))


def square_waves(count):
    minor = min(128, count)
    ids = jnp.arange(count, dtype=jnp.int32)
    major_cos, major_sin = waves(ids, jnp.arange(count // minor, dtype=jnp.int32) * minor, count)
    minor_cos, minor_sin = waves(ids, jnp.arange(minor, dtype=jnp.int32), count)
    major_cos = jnp.repeat(major_cos, minor, axis=1)
    major_sin = jnp.repeat(major_sin, minor, axis=1)
    minor_cos = jnp.tile(minor_cos, (1, count // minor))
    minor_sin = jnp.tile(minor_sin, (1, count // minor))
    return (
        major_cos * minor_cos - major_sin * minor_sin,
        major_sin * minor_cos + major_cos * minor_sin,
    )


def shift_index(freq, count):
    signed = jnp.where(freq >= count // 2, freq - count, freq)
    return signed * (4 * RAD) // count + 2 * RAD


def split_dot(left, right):
    hi = lax.reduce_precision(left, exponent_bits=8, mantissa_bits=7)
    lo = left - hi
    return jnp.dot(hi.astype(jnp.bfloat16), right, preferred_element_type=jnp.float32) + jnp.dot(
        lo.astype(jnp.bfloat16), right, preferred_element_type=jnp.float32
    )


def on_device(frames, pixel_gain, eigen_flats, pixels):
    n_srow = lax.axis_size("srow")
    n_scol = lax.axis_size("scol")
    n_dev = n_srow * n_scol
    local_rows, local_cols, n_pix = frames.shape
    row_count = local_rows * n_srow
    col_count = local_cols * n_scol
    n_shift = 4 * RAD
    flat_index = lax.axis_index("scol") * n_srow + lax.axis_index("srow")

    readings = frames.astype(jnp.float32)
    exposure = jnp.mean(readings, axis=2, keepdims=True)
    scaled = readings * pixel_gain / exposure
    fit_weights = jnp.einsum("rcp,ep->rce", scaled, eigen_flats, precision=HIGHEST)
    fitted = jnp.einsum("rce,ep->rcp", fit_weights, eigen_flats, precision=HIGHEST)
    flattened = (scaled - fitted).astype(jnp.bfloat16)

    gathered = lax.all_to_all(flattened, "srow", split_axis=1, concat_axis=0, tiled=True)
    cols_here = gathered.shape[1]

    k_blk = row_count // n_scol
    j_blk = col_count // n_srow
    row_ids = jnp.arange(row_count, dtype=jnp.int32)
    row_cos, row_sin = square_waves(row_count)
    forward_rows = jnp.stack([row_cos, -row_sin], axis=0).reshape(2, n_scol, k_blk, row_count)
    forward_rows = forward_rows.transpose(1, 0, 2, 3).reshape(2 * row_count, row_count)
    spec = jnp.dot(
        forward_rows.astype(jnp.bfloat16),
        gathered.reshape(row_count, cols_here * n_pix),
        preferred_element_type=jnp.float32,
    ).astype(jnp.bfloat16)
    spec = spec.reshape(n_scol, 2 * k_blk * cols_here, n_pix)

    def shift_of(freq, count):
        signed = freq - count if freq >= count // 2 else freq
        return (signed * (4 * RAD)) // count

    dx_first, dy_first = [], []
    for a in range(n_scol):
        shifts = [shift_of(k, row_count) for k in range(a * k_blk, (a + 1) * k_blk)]
        dx_first.append(min(shifts))
    n_dx = max(
        max(shift_of(k, row_count) for k in range(a * k_blk, (a + 1) * k_blk)) - dx_first[a] + 1
        for a in range(n_scol)
    )
    for b in range(n_srow):
        dy_first.append(min(shift_of(j, col_count) for j in range(b * j_blk, (b + 1) * j_blk)))
    n_dyl = max(
        max(shift_of(j, col_count) for j in range(b * j_blk, (b + 1) * j_blk)) - dy_first[b] + 1
        for b in range(n_srow)
    )
    n_dyl = -(-n_dyl // 8) * 8
    move_x = (jnp.array(dx_first, dtype=jnp.int32)[:, None] + jnp.arange(n_dx, dtype=jnp.int32)[None, :])
    move_y = (jnp.array(dy_first, dtype=jnp.int32)[:, None] + jnp.arange(n_dyl, dtype=jnp.int32)[None, :])
    move_x = move_x[:, None, None, :, None]
    move_y = move_y[None, :, :, None, None]
    det_x = (pixels % DET - DET // 2)[None, None, None, None, :]
    det_y = (pixels // DET - DET // 2)[None, None, None, None, :]
    upper = (det_x - move_x) * (det_x - move_x) + (det_y - move_y) * (det_y - move_y) <= RAD * RAD
    lower = (det_x + move_x) * (det_x + move_x) + (det_y + move_y) * (det_y + move_y) <= RAD * RAD
    weight = (upper.astype(jnp.float32) - lower.astype(jnp.float32)).astype(jnp.bfloat16)
    own_dx = (shift_index(row_ids, row_count) - 2 * RAD).reshape(n_scol, k_blk)
    own_dx = own_dx - jnp.array(dx_first, dtype=jnp.int32)[:, None]
    dx_of_n = jnp.broadcast_to(own_dx[:, None, :, None], (n_scol, 2, k_blk, cols_here))
    dx_of_n = dx_of_n.reshape(n_scol, 1, 2 * k_blk * cols_here)
    summed = None
    for d in range(n_dx):
        part = jnp.einsum(
            "axp,anp->axn",
            weight[:, :, :, d].reshape(n_scol, n_srow * n_dyl, n_pix),
            spec,
            preferred_element_type=jnp.float32,
        )
        part = jnp.where(dx_of_n == d, part, 0.0)
        summed = part if summed is None else summed + part
    summed = summed.reshape(n_dev, n_dyl, 2 * k_blk * cols_here)

    summed = lax.all_to_all(summed, ("scol", "srow"), split_axis=0, concat_axis=0, tiled=True)

    a_idx = lax.axis_index("scol")
    b_idx = lax.axis_index("srow")
    col_ids = jnp.arange(col_count, dtype=jnp.int32)
    my_j = b_idx * j_blk + jnp.arange(j_blk, dtype=jnp.int32)
    src_cos, src_sin = waves(jnp.arange(n_dev, dtype=jnp.int32) * cols_here, my_j, col_count)
    by_source = jnp.dot(
        summed.reshape(n_dev, -1).T,
        jnp.concatenate([src_cos, src_sin], axis=1),
        precision=HIGHEST,
        preferred_element_type=jnp.float32,
    ).reshape(n_dyl, 2, k_blk, cols_here, 2, j_blk)
    part_re = by_source[:, 0, :, :, 0] + by_source[:, 1, :, :, 1]
    part_im = by_source[:, 1, :, :, 0] - by_source[:, 0, :, :, 1]
    tw_cos, tw_sin = waves(jnp.arange(cols_here, dtype=jnp.int32), my_j, col_count)
    tw_cos = tw_cos[None, None, :, :]
    tw_sin = tw_sin[None, None, :, :]
    per_shift_re = jnp.sum(part_re * tw_cos + part_im * tw_sin, axis=2)
    per_shift_im = jnp.sum(part_im * tw_cos - part_re * tw_sin, axis=2)
    my_start = jnp.array(dy_first, dtype=jnp.int32)[b_idx]
    pick = (shift_index(my_j, col_count) - 2 * RAD - my_start)[None, :] == jnp.arange(n_dyl, dtype=jnp.int32)[:, None]
    pick = pick[:, None, :]
    psi = jnp.stack(
        [
            jnp.sum(jnp.where(pick, per_shift_re, 0.0), axis=0),
            jnp.sum(jnp.where(pick, per_shift_im, 0.0), axis=0),
        ],
        axis=1,
    )

    my_k = a_idx * k_blk + jnp.arange(k_blk, dtype=jnp.int32)
    inv_cos, inv_sin = waves(row_ids, my_k, row_count)
    inverse_rows = jnp.concatenate(
        [
            jnp.concatenate([inv_cos, -inv_sin], axis=1),
            jnp.concatenate([inv_sin, inv_cos], axis=1),
        ],
        axis=0,
    )
    psi = psi.transpose(1, 0, 2).reshape(2 * k_blk, j_blk)
    half = jnp.dot(inverse_rows, psi, precision=HIGHEST, preferred_element_type=jnp.float32)
    half = half.reshape(2, n_scol, row_count // n_scol, j_blk).transpose(1, 0, 2, 3)
    half = lax.all_to_all(half, "scol", split_axis=0, concat_axis=0, tiled=True)
    half = jnp.sum(half, axis=0)
    out_rows = half.shape[1]

    out_cols = col_count // n_srow
    inv_cos, inv_sin = waves(my_j, col_ids, col_count)
    inverse_cols = jnp.concatenate(
        [
            jnp.concatenate([inv_cos, inv_sin], axis=1),
            jnp.concatenate([-inv_sin, inv_cos], axis=1),
        ],
        axis=0,
    )
    half = half.transpose(1, 0, 2).reshape(out_rows, 2 * j_blk)
    image = jnp.dot(half, inverse_cols, precision=HIGHEST, preferred_element_type=jnp.float32)
    image = image.reshape(out_rows, 2, n_srow, out_cols).transpose(2, 0, 1, 3)
    image = lax.all_to_all(image, "srow", split_axis=0, concat_axis=0, tiled=True)
    image = jnp.sum(image, axis=0) * (1.0 / (row_count * col_count))
    return image


def solution(mesh):
    placed = (P("srow", "scol", None), P(), P(), P())
    return jax.shard_map(
        on_device, mesh=mesh, in_specs=placed, out_specs=P("scol", None, "srow"), check_vma=False
    )
```

profile of v0, /device:TPU:0, one launch (start us, length us, event | category | flops | bytes accessed | tf_op | source)
XLA Modules:
  0.0 145.9 jit_solution(6236803170353322392)
XLA Ops:
  0.0 0.0 copy-start
  0.0 2.4 %convert_reduce_fusion = f32[64,64]{1,0:T(8,128)S(1)} fusion(bf16[64,64,256]{2,1,0:T(8,128)(2,1)} %param.8), kind=kLoop, calls=%fused_computation | loop fusion | flops 2093056 | bytes 2113536 | tf_op jit(solution)/shard_map/reduce_sum | solution.py:58
  2.4 0.0 copy-done
  2.4 0.0 copy-done.3
  2.4 0.0 copy-done.9
  2.4 5.5 %fusion.1 = f32[64,64,16]{1,2,0:T(8,128)S(1)} fusion(bf16[64,64,256]{2,1,0:T(8,128)(2,1)S(1)} %copy-done.3, f32[64,64]{1,0:T(8,128)S(1)} %broadcast_multiply_fusion.1, f32[256]{0:T(256)S(1)} %copy-done.9, f32[16,256]{1,0:T(8,128)S(1)} %copy-done), kind=kOutput, calls=%fused_computation.8 | convolution fusion | flops 204472320 | bytes 2393088 | tf_op jit(solution)/shard_map/rcp,ep->rce/dot_general | solution.py:60
  7.9 4.5 %subtract_convert_fusion = bf16[64,64,256]{2,1,0:T(8,128)(2,1)S(1)} fusion(bf16[64,64,256]{2,1,0:T(8,128)(2,1)S(1)} %copy-done.3, f32[64,64,16]{1,2,0:T(8,128)S(1)} %fusion.1, f32[64,64]{1,0:T(8,128)S(1)} %broadcast_multiply_fusion.1, f32[256]{0:T(256)S(1)} %copy-done.9, f32[16,256]{1,0:T(8,128)S(1)} %copy-done), kind=kOutput, calls=%fused_computation.3 | convolution fusion | flops 206569472 | bytes 4490240 | tf_op jit(solution)/shard_map/rce,ep->rcp/dot_general | solution.py:61
  12.4 2.5 %copy.67 = bf16[64,64,256]{2,0,1:T(8,128)(2,1)} copy(bf16[64,64,256]{2,1,0:T(8,128)(2,1)S(1)} %subtract_convert_fusion) | data formatting | bytes 4194304 | tf_op jit(solution)/shard_map/convert_element_type | solution.py:62
  14.9 6.4 %all-to-all-start = ((bf16[64,64,256]{2,0,1:T(8,128)(2,1)}), bf16[64,64,256]{2,0,1:T(8,128)(2,1)S(1)}, u32[]{:S(2)}, u32[]{:S(2)}) async-start(bf16[64,64,256]{2,0,1:T(8,128)(2,1)} %copy.67), calls=%async_computation | async-start | bytes 4194304 | tf_op jit(solution)/shard_map/all_to_all | solution.py:64
  21.4 1.0 fusion.32
  22.4 0.2 fusion.59
  22.6 0.2 copy.65
  22.7 0.9 copy.66
  23.6 3.7 %subtract_convert_fusion.2 = (bf16[512,4,128]{2,1,0:T(4,128)(2,1)}, bf16[512,4,128]{2,1,0:T(4,128)(2,1)S(1)}) fusion(f32[512,128]{1,0:T(8,128)S(1)} %get-tuple-element.35, f32[512,4]{1,0:T(8,128)} %copy.66, f32[512,128]{1,0:T(8,128)S(1)} %get-tuple-element.36, f32[512,4]{1,0:T(8,128)S(1)} %copy.65), kind=kLoop, calls=%fused_computation.25 | loop fusion | flops 2359296 | bytes 1589248 | tf_op jit(solution)/shard_map/convert.3
  27.3 0.2 neg.22
  27.5 0.0 copy-start.7
  27.5 0.0 copy-start.5
  27.5 0.0 copy-start.6
  27.5 1.3 sub.154
  28.8 0.0 copy-done.8
  28.8 0.1 copy.64
  29.0 0.1 copy.69
  29.1 0.1 copy.70
  29.3 0.1 copy.71
  29.4 1.1 pad_maximum_fusion
  30.5 0.0 copy-done.7
  30.5 0.0 copy-done.5
  30.5 0.0 copy-done.6
  30.5 0.1 iota_add_fusion
  30.6 0.1 subtract_multiply_fusion.1
  30.7 0.1 subtract_multiply_fusion
  30.8 2.7 %subtract_convert_fusion.1 = bf16[16,8,8,4,256]{4,2,1,0,3:T(8,128)(2,1)} fusion(s32[8,8,256]{2,1,0:T(8,128)S(1)} %get-tuple-element.12, s32[16,4,256]{2,0,1:T(8,128)S(1)} %get-tuple-element.14, s32[8,8,256]{2,1,0:T(8,128)S(1)} %get-tuple-element.11, s32[16,4,256]{2,0,1:T(8,128)S(1)} %get-tuple-element.13), kind=kLoop, calls=%fused_computation.4 | loop fusion | flops 8388608 | bytes 2359296 | tf_op jit(solution)/shard_map/convert_element_type | solution.py:107
  33.5 13.9 %all-to-all-done = bf16[64,64,256]{2,0,1:T(8,128)(2,1)S(1)} async-done(((bf16[64,64,256]{2,0,1:T(8,128)(2,1)}), bf16[64,64,256]{2,0,1:T(8,128)(2,1)S(1)}, u32[]{:S(2)}, u32[]{:S(2)}) %all-to-all-start) | async-done | bytes 2097184 | tf_op jit(solution)/shard_map/all_to_all | solution.py:64
  47.4 1.3 copy.68
  48.7 0.0 copy-start.4
  48.7 0.7 copy.90
  49.4 0.5 copy-done.4
  49.9 4.3 %convolution_convert_fusion = bf16[1024,2048]{1,0:T(8,128)(2,1)} fusion(bf16[1024,512]{1,0:T(8,128)(2,1)S(1)} %bitcast.116, bf16[512,2048]{1,0:T(8,128)(2,1)S(1)} %bitcast.114), kind=kOutput, calls=%fused_computation.7 | convolution fusion | flops 2149580800 | bytes 7340032 | tf_op jit(solution)/shard_map/dot_general | solution.py:73
  54.2 7.5 %reshape.452 = bf16[16,512,256]{2,1,0:T(8,128)(2,1)} reshape(bf16[1024,2048]{1,0:T(8,128)(2,1)} %convolution_convert_fusion) | data formatting | bytes 8388608 | tf_op jit(solution)/shard_map/reshape | solution.py:78
  61.8 3.7 %fusion.11 = f32[16,64,512]{2,1,0:T(8,128)S(1)} fusion(bf16[16,512,256]{2,1,0:T(8,128)(2,1)} %reshape.452, bf16[16,8,8,4,256]{4,2,1,0,3:T(8,128)(2,1)S(1)} %copy-done.2), kind=kOutput, calls=%fused_computation.34 | convolution fusion | flops 268435456 | bytes 6815744 | tf_op jit(solution)/shard_map/axp,anp->axn/dot_general | solution.py:114
  65.5 0.0 copy-done.1
  65.5 1.4 fusion.12
  66.9 1.4 fusion.13
  68.2 2.7 %select_add_fusion = f32[16,64,512]{2,1,0:T(8,128)} fusion(f32[16,64,512]{2,1,0:T(8,128)S(1)} %fusion.11, f32[16,64,512]{2,1,0:T(8,128)S(1)} %fusion.12, f32[16,64,512]{2,1,0:T(8,128)S(1)} %fusion.13, bf16[16,512,256]{2,1,0:T(8,128)(2,1)S(1)} %copy-done.1, pred[16,512]{1,0:T(8,128)(4,1)S(1)} %copy.71, pred[16,512]{1,0:T(8,128)(4,1)S(1)} %copy.70, ...), kind=kOutput, calls=%fused_computation.10 | convolution fusion | flops 272105472 | bytes 13139968 | tf_op jit(solution)/shard_map/axp,anp->axn/dot_general | solution.py:114
  71.0 9.3 %all-to-all-start.1 = ((f32[128,8,512]{2,1,0:T(8,128)}), f32[128,8,512]{2,1,0:T(8,128)}, u32[]{:S(2)}, u32[]{:S(2)}) async-start(f32[128,8,512]{2,1,0:T(8,128)} %bitcast.15), calls=%async_computation.1 | async-start | bytes 4194304 | tf_op jit(solution)/shard_map/all_to_all | solution.py:124
  80.3 0.6 dynamic_slice.3
  80.9 0.7 fusion.66
  81.6 0.3 fusion.42
  82.0 1.0 fusion.36
  83.0 0.2 maximum_maximum_fusion.1
  83.2 0.1 fusion.62
  83.3 26.6 %all-to-all-done.1 = f32[128,8,512]{2,1,0:T(8,128)} async-done(((f32[128,8,512]{2,1,0:T(8,128)}), f32[128,8,512]{2,1,0:T(8,128)}, u32[]{:S(2)}, u32[]{:S(2)}) %all-to-all-start.1) | async-done | bytes 2097184 | tf_op jit(solution)/shard_map/all_to_all | solution.py:124
  109.9 2.0 %copy.85 = f32[128,8,512]{0,2,1:T(8,128)S(1)} copy(f32[128,8,512]{2,1,0:T(8,128)} %all-to-all-done.1) | data formatting | bytes 4194304 | tf_op jit(solution)/shard_map/reshape | solution.py:132
  111.9 3.5 %fusion.67 = f32[8,2,32,8,2,128]{5,3,4,2,1,0:T(8,128)S(1)} fusion(f32[8,2,32,8,128,1]{4,3,5,2,1,0:T(8,128)S(1)} %bitcast.111, f32[2,128,128,1,1,1]{2,1,0,5,4,3:T(8,128)S(1)} %bitcast.117), kind=kOutput, calls=%fused_computation.149 | convolution fusion | flops 1610612736 | bytes 6422528 | tf_op jit(solution)/shard_map/dot_general | solution.py:131
  115.4 0.8 add_reduce_fusion
  116.2 0.6 convolution_bitcast_fusion
  116.8 0.8 copy.75
  117.6 3.6 %all-to-all-start.2 = ((f32[16,2,32,128]{3,2,1,0:T(8,128)}), f32[16,2,32,128]{3,2,1,0:T(8,128)S(1)}, u32[]{:S(2)}, u32[]{:S(2)}) async-start(f32[16,2,32,128]{3,2,1,0:T(8,128)} %copy.75), calls=%async_computation.2 | async-start | bytes 1048576 | tf_op jit(solution)/shard_map/all_to_all | solution.py:167
  121.2 2.1 %fusion.23 = (f32[128,1024]{0,1:T(8,128)S(1)}, f32[128,1024]{0,1:T(8,128)S(1)}, f32[128,1024]{0,1:T(8,128)S(1)}) fusion(s32[128]{0:T(128)S(1)} %get-tuple-element.34), kind=kLoop, calls=%fused_computation.55 | loop fusion | flops 1966080 | bytes 1573376 | tf_op jit(solution)/shard_map/sin | solution.py:16
  123.3 0.1 maximum_maximum_fusion
  123.4 10.1 %all-to-all-done.2 = f32[16,2,32,128]{3,2,1,0:T(8,128)S(1)} async-done(((f32[16,2,32,128]{3,2,1,0:T(8,128)}), f32[16,2,32,128]{3,2,1,0:T(8,128)S(1)}, u32[]{:S(2)}, u32[]{:S(2)}) %all-to-all-start.2) | async-done | bytes 524320 | tf_op jit(solution)/shard_map/all_to_all | solution.py:167
  133.6 2.0 %convolution_bitcast_fusion.1 = f32[8,32,2,128]{3,1,0,2:T(8,128)S(1)} fusion(f32[2,8,128,256]{3,2,1,0:T(8,128)S(1)} %bitcast.110, f32[32,256,1,1]{1,0,2,3:T(8,128)S(1)} %reshape.461), kind=kOutput, calls=%fused_computation.14 | convolution fusion | flops 201326592 | bytes 2392064 | tf_op jit(solution)/shard_map/dot_general | solution.py:181
  135.6 9.6 %all_to_all.30 = f32[8,32,2,128]{3,1,2,0:T(8,128)S(1)} all-to-all(f32[8,32,2,128]{3,1,2,0:T(8,128)S(1)} %copy.78), channel_id=1, replica_groups=mesh['srow'=8,'scol'=16] {'srow'}, dimensions={0} | all-to-all | bytes 524288 | tf_op jit(solution)/shard_map/all_to_all | solution.py:183
  145.3 0.6 copy.80
  (27 shorter events, 0.4 us)
Async XLA Ops:
  0.0 2.4 %copy-start = (f32[16,256]{1,0:T(8,128)S(1)}, f32[16,256]{1,0:T(8,128)}, u32[]{:S(2)}) copy-start(f32[16,256]{1,0:T(8,128)} %param.10) | copy-start | bytes 49156
  0.0 2.4 %copy-start.3 = (bf16[64,64,256]{2,1,0:T(8,128)(2,1)S(1)}, bf16[64,64,256]{2,1,0:T(8,128)(2,1)}, u32[]{:S(2)}) copy-start(bf16[64,64,256]{2,1,0:T(8,128)(2,1)} %param.8) | copy-start | bytes 6291460
  0.0 2.4 %copy-start.9 = (f32[256]{0:T(256)S(1)}, f32[256]{0:T(256)}, u32[]{:S(2)}) copy-start(f32[256]{0:T(256)} %param.9) | copy-start | bytes 3076
  14.9 32.5 %all-to-all-start = ((bf16[64,64,256]{2,0,1:T(8,128)(2,1)}), bf16[64,64,256]{2,0,1:T(8,128)(2,1)S(1)}, u32[]{:S(2)}, u32[]{:S(2)}) async-start(bf16[64,64,256]{2,0,1:T(8,128)(2,1)} %copy.67), calls=%async_computation | async-start | bytes 4194304 | tf_op jit(solution)/shard_map/all_to_all | solution.py:64
  23.6 5.2 %copy-start.8 = (s32[16]{0:T(128)S(1)}, s32[16]{0:T(128)}, u32[]{:S(2)}) copy-start(s32[16]{0:T(128)} %constant.186) | copy-start | bytes 196
  27.5 3.0 %copy-start.7 = (s32[16]{0:T(128)S(1)}, s32[16]{0:T(128)}, u32[]{:S(2)}) copy-start(s32[16]{0:T(128)} %constant.184.clone) | copy-start | bytes 196
  27.5 3.0 %copy-start.5 = (s32[256]{0:T(256)S(1)}, s32[256]{0:T(256)}, u32[]{:S(2)}) copy-start(s32[256]{0:T(256)} %param.11) | copy-start | bytes 3076
  27.5 3.0 %copy-start.6 = (s32[8]{0:T(128)S(1)}, s32[8]{0:T(128)}, u32[]{:S(2)}) copy-start(s32[8]{0:T(128)} %constant.185.clone) | copy-start | bytes 100
  48.7 1.2 copy-start.4
  54.2 7.5 %copy-start.2 = (bf16[16,8,8,4,256]{4,2,1,0,3:T(8,128)(2,1)S(1)}, bf16[16,8,8,4,256]{4,2,1,0,3:T(8,128)(2,1)}, u32[]{:S(2)}) copy-start(bf16[16,8,8,4,256]{4,2,1,0,3:T(8,128)(2,1)} %subtract_convert_fusion.1) | copy-start | bytes 6291460
  61.8 3.7 %copy-start.1 = (bf16[16,512,256]{2,1,0:T(8,128)(2,1)S(1)}, bf16[16,512,256]{2,1,0:T(8,128)(2,1)}, u32[]{:S(2)}) copy-start(bf16[16,512,256]{2,1,0:T(8,128)(2,1)} %reshape.452) | copy-start | bytes 12582916
  71.0 38.9 %all-to-all-start.1 = ((f32[128,8,512]{2,1,0:T(8,128)}), f32[128,8,512]{2,1,0:T(8,128)}, u32[]{:S(2)}, u32[]{:S(2)}) async-start(f32[128,8,512]{2,1,0:T(8,128)} %bitcast.15), calls=%async_computation.1 | async-start | bytes 4194304 | tf_op jit(solution)/shard_map/all_to_all | solution.py:124
  117.6 15.9 %all-to-all-start.2 = ((f32[16,2,32,128]{3,2,1,0:T(8,128)}), f32[16,2,32,128]{3,2,1,0:T(8,128)S(1)}, u32[]{:S(2)}, u32[]{:S(2)}) async-start(f32[16,2,32,128]{3,2,1,0:T(8,128)} %copy.75), calls=%async_computation.2 | async-start | bytes 1048576 | tf_op jit(solution)/shard_map/all_to_all | solution.py:167
where the time goes:
time: 147 us; the launch traced here: 146 us
  waiting for transfers between devices  50.6 us (34%)
  matrix products  29.5 us (20%)
  local copies, waits for them, and re-layouts  19.7 us (13%)
  starting transfers between devices  19.4 us (13%)
  other arithmetic  16.7 us (11%)
  blocking collectives  9.64 us (7%)
    all_to_all x1, waiting for transfers between devices, on_device(): lax.all_to_all(summed, ('scol', 'srow'), split_axis=0, concat_axis=0, til...  26.6 us
    all_to_all x1, waiting for transfers between devices, on_device(): lax.all_to_all(flattened, 'srow', split_axis=1, concat_axis=0, tiled=True)  13.9 us
    all_to_all x1, waiting for transfers between devices, on_device(): half = lax.all_to_all(half, 'scol', split_axis=0, concat_axis=0, tiled=True)  10.1 us
    all_to_all x1, blocking collectives, on_device(): lax.all_to_all(image, 'srow', split_axis=0, concat_axis=0, tiled=True)  9.64 us
    all_to_all x1, starting transfers between devices, on_device(): lax.all_to_all(summed, ('scol', 'srow'), split_axis=0, concat_axis=0, til...  9.34 us
    dot_general x4, matrix products, on_device(): jnp.einsum('axp,anp->axn', weight[:, :, :, d].reshape(n_scol, n_srow * n_...  9.21 us
    reshape x1, local copies, waits for them, and re-layouts, on_device(): spec = spec.reshape(n_scol, 2 * k_blk * cols_here, n_pix)  7.54 us
    all_to_all x1, starting transfers between devices, on_device(): lax.all_to_all(flattened, 'srow', split_axis=1, concat_axis=0, tiled=True)  6.44 us
  transfers between devices with their start and end apart: 3, of which 3 were waited for; matrix products, arithmetic and copies ran while one was open for 12% of the time, Pallas kernels for 0%

commit v1 on v0

--- a/solution.py
+++ b/solution.py
@@ -57,8 +57,8 @@
     readings = frames.astype(jnp.float32)
     exposure = jnp.mean(readings, axis=2, keepdims=True)
     scaled = readings * pixel_gain / exposure
-    fit_weights = jnp.einsum("rcp,ep->rce", scaled, eigen_flats, precision=HIGHEST)
-    fitted = jnp.einsum("rce,ep->rcp", fit_weights, eigen_flats, precision=HIGHEST)
+    fit_weights = jnp.einsum("rcp,ep->rce", scaled, eigen_flats, precision=lax.Precision.HIGH)
+    fitted = jnp.einsum("rce,ep->rcp", fit_weights, eigen_flats, precision=lax.Precision.HIGH)
     flattened = (scaled - fitted).astype(jnp.bfloat16)
 
     gathered = lax.all_to_all(flattened, "srow", split_axis=1, concat_axis=0, tiled=True)
@@ -119,7 +119,7 @@
         )
         part = jnp.where(dx_of_n == d, part, 0.0)
         summed = part if summed is None else summed + part
-    summed = summed.reshape(n_dev, n_dyl, 2 * k_blk * cols_here)
+    summed = summed.reshape(n_dev, n_dyl, 2 * k_blk * cols_here).astype(jnp.bfloat16)
 
     summed = lax.all_to_all(summed, ("scol", "srow"), split_axis=0, concat_axis=0, tiled=True)
 
@@ -129,7 +129,7 @@
     my_j = b_idx * j_blk + jnp.arange(j_blk, dtype=jnp.int32)
     src_cos, src_sin = waves(jnp.arange(n_dev, dtype=jnp.int32) * cols_here, my_j, col_count)
     by_source = jnp.dot(
-        summed.reshape(n_dev, -1).T,
+        summed.reshape(n_dev, -1).T.astype(jnp.float32),
         jnp.concatenate([src_cos, src_sin], axis=1),
         precision=HIGHEST,
         preferred_element_type=jnp.float32,

time: 147 us -> 128 us (0.87)
  waiting for transfers between devices: 50.6 us -> 40.2 us
  matrix products: 29.5 us -> 22.9 us
    all_to_all x1, waiting for transfers between devices: 26.6 us -> 17.8 us  [on_device(): lax.all_to_all(summed, ('scol', 'srow'), split_axis=0, concat_axis=0, til...]
    dot_general x3, matrix products: 13.4 us -> 7.21 us  [the longest x1 2.77 us: on_device(): jnp.einsum('rce,ep->rcp', fit_weights, eigen_flats, precision=lax.Precisi...]
    all_to_all x1, waiting for transfers between devices: 13.9 us -> 12.3 us  [on_device(): lax.all_to_all(flattened, 'srow', split_axis=1, concat_axis=0, tiled=True)]
  transfers between devices with their start and end apart: 3 -> 3, of which waited for: 3 -> 3; matrix products, arithmetic and copies ran while one was open for 12% -> 13% of each run, Pallas kernels for 0% -> 0%
where the time goes in v1:
time: 128 us; the launch traced here: 127 us
  waiting for transfers between devices  40.2 us (31%)
  matrix products  22.9 us (18%)
  local copies, waits for them, and re-layouts  18.7 us (15%)
  starting transfers between devices  18.6 us (15%)
  other arithmetic  16.7 us (13%)
  blocking collectives  9.64 us (8%)
    all_to_all x1, waiting for transfers between devices, on_device(): lax.all_to_all(summed, ('scol', 'srow'), split_axis=0, concat_axis=0, til...  17.8 us
    all_to_all x1, waiting for transfers between devices, on_device(): lax.all_to_all(flattened, 'srow', split_axis=1, concat_axis=0, tiled=True)  12.3 us
    all_to_all x1, waiting for transfers between devices, on_device(): half = lax.all_to_all(half, 'scol', split_axis=0, concat_axis=0, tiled=True)  10.1 us
    all_to_all x1, blocking collectives, on_device(): lax.all_to_all(image, 'srow', split_axis=0, concat_axis=0, tiled=True)  9.64 us
    dot_general x4, matrix products, on_device(): jnp.einsum('axp,anp->axn', weight[:, :, :, d].reshape(n_scol, n_srow * n_...  8.87 us
    all_to_all x1, starting transfers between devices, on_device(): lax.all_to_all(summed, ('scol', 'srow'), split_axis=0, concat_axis=0, til...  8.58 us
    reshape x1, local copies, waits for them, and re-layouts, on_device(): spec = spec.reshape(n_scol, 2 * k_blk * cols_here, n_pix)  7.54 us
    all_to_all x1, starting transfers between devices, on_device(): lax.all_to_all(flattened, 'srow', split_axis=1, concat_axis=0, tiled=True)  6.45 us
  transfers between devices with their start and end apart: 3, of which 3 were waited for; matrix products, arithmetic and copies ran while one was open for 13% of the time, Pallas kernels for 0%

profile of v1, /device:TPU:0, one launch (start us, length us, event | category | flops | bytes accessed | tf_op | source)
XLA Modules:
  0.0 127.2 jit_solution(591505309838044561)
XLA Ops:
  0.0 0.0 copy-start
  0.0 2.4 %convert_reduce_fusion = f32[64,64]{1,0:T(8,128)S(1)} fusion(bf16[64,64,256]{2,1,0:T(8,128)(2,1)} %param.8), kind=kLoop, calls=%fused_computation | loop fusion | flops 2093056 | bytes 2113536 | tf_op jit(solution)/shard_map/reduce_sum | solution.py:58
  2.4 0.0 copy-done
  2.4 0.0 copy-done.3
  2.4 0.0 copy-done.9
  2.4 2.6 %fusion.1 = f32[64,64,16]{1,2,0:T(8,128)S(1)} fusion(bf16[64,64,256]{2,1,0:T(8,128)(2,1)S(1)} %copy-done.3, f32[64,64]{1,0:T(8,128)S(1)} %broadcast_multiply_fusion.1, f32[256]{0:T(256)S(1)} %copy-done.9, f32[16,256]{1,0:T(8,128)S(1)} %copy-done), kind=kOutput, calls=%fused_computation.8 | convolution fusion | flops 103809024 | bytes 2393088 | tf_op jit(solution)/shard_map/rcp,ep->rce/dot_general | solution.py:60
  5.0 2.8 %subtract_convert_fusion = bf16[64,64,256]{2,1,0:T(8,128)(2,1)S(1)} fusion(bf16[64,64,256]{2,1,0:T(8,128)(2,1)S(1)} %copy-done.3, f32[64,64,16]{1,2,0:T(8,128)S(1)} %fusion.1, f32[64,64]{1,0:T(8,128)S(1)} %broadcast_multiply_fusion.1, f32[256]{0:T(256)S(1)} %copy-done.9, f32[16,256]{1,0:T(8,128)S(1)} %copy-done), kind=kOutput, calls=%fused_computation.3 | convolution fusion | flops 105906176 | bytes 4490240 | tf_op jit(solution)/shard_map/rce,ep->rcp/dot_general | solution.py:61
  7.8 2.5 %copy.67 = bf16[64,64,256]{2,0,1:T(8,128)(2,1)} copy(bf16[64,64,256]{2,1,0:T(8,128)(2,1)S(1)} %subtract_convert_fusion) | data formatting | bytes 4194304 | tf_op jit(solution)/shard_map/convert_element_type | solution.py:62
  10.3 6.4 %all-to-all-start = ((bf16[64,64,256]{2,0,1:T(8,128)(2,1)}), bf16[64,64,256]{2,0,1:T(8,128)(2,1)S(1)}, u32[]{:S(2)}, u32[]{:S(2)}) async-start(bf16[64,64,256]{2,0,1:T(8,128)(2,1)} %copy.67), calls=%async_computation | async-start | bytes 4194304 | tf_op jit(solution)/shard_map/all_to_all | solution.py:64
  16.8 1.0 fusion.32
  17.8 0.2 fusion.59
  18.0 0.2 copy.65
  18.2 0.9 copy.66
  19.0 3.7 %subtract_convert_fusion.2 = (bf16[512,4,128]{2,1,0:T(4,128)(2,1)}, bf16[512,4,128]{2,1,0:T(4,128)(2,1)S(1)}) fusion(f32[512,128]{1,0:T(8,128)S(1)} %get-tuple-element.35, f32[512,4]{1,0:T(8,128)} %copy.66, f32[512,128]{1,0:T(8,128)S(1)} %get-tuple-element.36, f32[512,4]{1,0:T(8,128)S(1)} %copy.65), kind=kLoop, calls=%fused_computation.25 | loop fusion | flops 2359296 | bytes 1589248 | tf_op jit(solution)/shard_map/convert.3
  22.7 0.2 neg.22
  22.9 0.0 copy-start.7
  22.9 0.0 copy-start.5
  22.9 1.2 sub.154
  24.2 0.0 copy-done.8
  24.3 0.1 copy.64
  24.4 0.1 copy.69
  24.6 0.1 copy.70
  24.7 0.1 copy.71
  24.8 0.0 copy-done.6
  24.8 0.6 dynamic_slice.3
  25.4 0.7 fusion.66
  26.1 1.1 pad_maximum_fusion
  27.2 0.0 copy-done.7
  27.2 0.0 copy-done.5
  27.2 0.1 iota_add_fusion
  27.3 0.3 fusion.42
  27.6 0.1 subtract_multiply_fusion.1
  27.7 0.1 subtract_multiply_fusion
  27.8 2.7 %subtract_convert_fusion.1 = bf16[16,8,8,4,256]{4,2,1,0,3:T(8,128)(2,1)} fusion(s32[8,8,256]{2,1,0:T(8,128)S(1)} %get-tuple-element.12, s32[16,4,256]{2,0,1:T(8,128)S(1)} %get-tuple-element.14, s32[8,8,256]{2,1,0:T(8,128)S(1)} %get-tuple-element.11, s32[16,4,256]{2,0,1:T(8,128)S(1)} %get-tuple-element.13), kind=kLoop, calls=%fused_computation.4 | loop fusion | flops 8388608 | bytes 2359296 | tf_op jit(solution)/shard_map/convert_element_type | solution.py:107
  30.5 12.3 %all-to-all-done = bf16[64,64,256]{2,0,1:T(8,128)(2,1)S(1)} async-done(((bf16[64,64,256]{2,0,1:T(8,128)(2,1)}), bf16[64,64,256]{2,0,1:T(8,128)(2,1)S(1)}, u32[]{:S(2)}, u32[]{:S(2)}) %all-to-all-start) | async-done | bytes 2097184 | tf_op jit(solution)/shard_map/all_to_all | solution.py:64
  42.8 1.3 copy.68
  44.1 0.0 copy-start.4
  44.1 0.7 copy.90
  44.8 0.5 copy-done.4
  45.3 4.3 %convolution_convert_fusion = bf16[1024,2048]{1,0:T(8,128)(2,1)} fusion(bf16[1024,512]{1,0:T(8,128)(2,1)S(1)} %bitcast.116, bf16[512,2048]{1,0:T(8,128)(2,1)S(1)} %bitcast.114), kind=kOutput, calls=%fused_computation.7 | convolution fusion | flops 2149580800 | bytes 7340032 | tf_op jit(solution)/shard_map/dot_general | solution.py:73
  49.6 7.5 %reshape.451 = bf16[16,512,256]{2,1,0:T(8,128)(2,1)} reshape(bf16[1024,2048]{1,0:T(8,128)(2,1)} %convolution_convert_fusion) | data formatting | bytes 8388608 | tf_op jit(solution)/shard_map/reshape | solution.py:78
  57.2 0.0 copy-done.2
  57.2 3.7 %fusion.11 = f32[16,64,512]{2,1,0:T(8,128)S(1)} fusion(bf16[16,512,256]{2,1,0:T(8,128)(2,1)} %reshape.451, bf16[16,8,8,4,256]{4,2,1,0,3:T(8,128)(2,1)S(1)} %copy-done.2), kind=kOutput, calls=%fused_computation.34 | convolution fusion | flops 268435456 | bytes 6815744 | tf_op jit(solution)/shard_map/axp,anp->axn/dot_general | solution.py:114
  60.9 0.0 copy-done.1
  60.9 1.4 %fusion.12 = f32[16,64,512]{2,1,0:T(8,128)S(1)} fusion(bf16[16,512,256]{2,1,0:T(8,128)(2,1)S(1)} %copy-done.1, bf16[16,8,8,4,256]{4,2,1,0,3:T(8,128)(2,1)S(1)} %copy-done.2), kind=kOutput, calls=%fused_computation.36 | convolution fusion | flops 268435456 | bytes 6815744 | tf_op jit(solution)/shard_map/axp,anp->axn/dot_general | solution.py:114
  62.3 1.4 %fusion.13 = f32[16,64,512]{2,1,0:T(8,128)S(1)} fusion(bf16[16,512,256]{2,1,0:T(8,128)(2,1)S(1)} %copy-done.1, bf16[16,8,8,4,256]{4,2,1,0,3:T(8,128)(2,1)S(1)} %copy-done.2), kind=kOutput, calls=%fused_computation.38 | convolution fusion | flops 268435456 | bytes 6815744 | tf_op jit(solution)/shard_map/axp,anp->axn/dot_general | solution.py:114
  63.7 2.4 %add_convert_fusion = bf16[16,64,512]{2,1,0:T(8,128)(2,1)} fusion(f32[16,64,512]{2,1,0:T(8,128)S(1)} %fusion.11, f32[16,64,512]{2,1,0:T(8,128)S(1)} %fusion.12, f32[16,64,512]{2,1,0:T(8,128)S(1)} %fusion.13, bf16[16,512,256]{2,1,0:T(8,128)(2,1)S(1)} %copy-done.1, pred[16,512]{1,0:T(8,128)(4,1)S(1)} %copy.71, pred[16,512]{1,0:T(8,128)(4,1)S(1)} %copy.70, ...), kind=kOutput, calls=%fused_computation.10 | convolution fusion | flops 272629760 | bytes 12091392 | tf_op jit(solution)/shard_map/axp,anp->axn/dot_general | solution.py:114
  66.1 8.6 %all-to-all-start.1 = ((bf16[128,8,512]{2,1,0:T(8,128)(2,1)}), bf16[128,8,512]{2,1,0:T(8,128)(2,1)S(1)}, u32[]{:S(2)}, u32[]{:S(2)}) async-start(bf16[128,8,512]{2,1,0:T(8,128)(2,1)} %bitcast.15), calls=%async_computation.1 | async-start | bytes 2097152 | tf_op jit(solution)/shard_map/all_to_all | solution.py:124
  74.7 1.0 fusion.36
  75.7 0.2 maximum_maximum_fusion.1
  76.0 0.1 fusion.62
  76.0 17.8 %all-to-all-done.1 = bf16[128,8,512]{2,1,0:T(8,128)(2,1)S(1)} async-done(((bf16[128,8,512]{2,1,0:T(8,128)(2,1)}), bf16[128,8,512]{2,1,0:T(8,128)(2,1)S(1)}, u32[]{:S(2)}, u32[]{:S(2)}) %all-to-all-start.1) | async-done | bytes 1048608 | tf_op jit(solution)/shard_map/all_to_all | solution.py:124
  93.8 1.0 copy.85
  94.8 1.8 %fusion.67 = f32[8,2,32,8,2,128]{5,3,4,2,1,0:T(8,128)S(1)} fusion(bf16[8,2,32,8,128,1]{4,3,5,2,1,0:T(8,128)(2,1)S(1)} %bitcast.113, f32[2,128,128,1,1,1]{2,1,0,5,4,3:T(8,128)S(1)} %bitcast.117), kind=kOutput, calls=%fused_computation.149 | convolution fusion | flops 1610612736 | bytes 5373952 | tf_op jit(solution)/shard_map/dot_general | solution.py:131
  96.6 0.8 add_reduce_fusion
  97.5 0.6 convolution_bitcast_fusion
  98.0 0.8 copy.75
  98.9 3.6 %all-to-all-start.2 = ((f32[16,2,32,128]{3,2,1,0:T(8,128)}), f32[16,2,32,128]{3,2,1,0:T(8,128)S(1)}, u32[]{:S(2)}, u32[]{:S(2)}) async-start(f32[16,2,32,128]{3,2,1,0:T(8,128)} %copy.75), calls=%async_computation.2 | async-start | bytes 1048576 | tf_op jit(solution)/shard_map/all_to_all | solution.py:167
  102.4 2.1 %fusion.23 = (f32[128,1024]{0,1:T(8,128)S(1)}, f32[128,1024]{0,1:T(8,128)S(1)}, f32[128,1024]{0,1:T(8,128)S(1)}) fusion(s32[128]{0:T(128)S(1)} %get-tuple-element.34), kind=kLoop, calls=%fused_computation.55 | loop fusion | flops 1966080 | bytes 1573376 | tf_op jit(solution)/shard_map/sin | solution.py:16
  104.5 0.1 maximum_maximum_fusion
  104.7 10.1 %all-to-all-done.2 = f32[16,2,32,128]{3,2,1,0:T(8,128)S(1)} async-done(((f32[16,2,32,128]{3,2,1,0:T(8,128)}), f32[16,2,32,128]{3,2,1,0:T(8,128)S(1)}, u32[]{:S(2)}, u32[]{:S(2)}) %all-to-all-start.2) | async-done | bytes 524320 | tf_op jit(solution)/shard_map/all_to_all | solution.py:167
  114.9 2.0 %convolution_bitcast_fusion.1 = f32[8,32,2,128]{3,1,0,2:T(8,128)S(1)} fusion(f32[2,8,128,256]{3,2,1,0:T(8,128)S(1)} %bitcast.110, f32[32,256,1,1]{1,0,2,3:T(8,128)S(1)} %reshape.459), kind=kOutput, calls=%fused_computation.14 | convolution fusion | flops 201326592 | bytes 2392064 | tf_op jit(solution)/shard_map/dot_general | solution.py:181
  116.9 9.6 %all_to_all.30 = f32[8,32,2,128]{3,1,2,0:T(8,128)S(1)} all-to-all(f32[8,32,2,128]{3,1,2,0:T(8,128)S(1)} %copy.78), channel_id=1, replica_groups=mesh['srow'=8,'scol'=16] {'srow'}, dimensions={0} | all-to-all | bytes 524288 | tf_op jit(solution)/shard_map/all_to_all | solution.py:183
  126.6 0.6 copy.80
  (27 shorter events, 0.4 us)
Async XLA Ops:
  0.0 2.4 %copy-start = (f32[16,256]{1,0:T(8,128)S(1)}, f32[16,256]{1,0:T(8,128)}, u32[]{:S(2)}) copy-start(f32[16,256]{1,0:T(8,128)} %param.10) | copy-start | bytes 49156
  0.0 2.4 %copy-start.3 = (bf16[64,64,256]{2,1,0:T(8,128)(2,1)S(1)}, bf16[64,64,256]{2,1,0:T(8,128)(2,1)}, u32[]{:S(2)}) copy-start(bf16[64,64,256]{2,1,0:T(8,128)(2,1)} %param.8) | copy-start | bytes 6291460
  0.0 2.4 %copy-start.9 = (f32[256]{0:T(256)S(1)}, f32[256]{0:T(256)}, u32[]{:S(2)}) copy-start(f32[256]{0:T(256)} %param.9) | copy-start | bytes 3076
  10.3 32.5 %all-to-all-start = ((bf16[64,64,256]{2,0,1:T(8,128)(2,1)}), bf16[64,64,256]{2,0,1:T(8,128)(2,1)S(1)}, u32[]{:S(2)}, u32[]{:S(2)}) async-start(bf16[64,64,256]{2,0,1:T(8,128)(2,1)} %copy.67), calls=%async_computation | async-start | bytes 4194304 | tf_op jit(solution)/shard_map/all_to_all | solution.py:64
  19.0 5.2 %copy-start.8 = (s32[16]{0:T(128)S(1)}, s32[16]{0:T(128)}, u32[]{:S(2)}) copy-start(s32[16]{0:T(128)} %constant.186) | copy-start | bytes 196
  19.0 5.8 %copy-start.6 = (s32[8]{0:T(128)S(1)}, s32[8]{0:T(128)}, u32[]{:S(2)}) copy-start(s32[8]{0:T(128)} %constant.185.clone) | copy-start | bytes 100
  22.9 4.3 %copy-start.7 = (s32[16]{0:T(128)S(1)}, s32[16]{0:T(128)}, u32[]{:S(2)}) copy-start(s32[16]{0:T(128)} %constant.184.clone) | copy-start | bytes 196
  22.9 4.3 %copy-start.5 = (s32[256]{0:T(256)S(1)}, s32[256]{0:T(256)}, u32[]{:S(2)}) copy-start(s32[256]{0:T(256)} %param.11) | copy-start | bytes 3076
  44.1 1.2 copy-start.4
  49.6 7.5 %copy-start.2 = (bf16[16,8,8,4,256]{4,2,1,0,3:T(8,128)(2,1)S(1)}, bf16[16,8,8,4,256]{4,2,1,0,3:T(8,128)(2,1)}, u32[]{:S(2)}) copy-start(bf16[16,8,8,4,256]{4,2,1,0,3:T(8,128)(2,1)} %subtract_convert_fusion.1) | copy-start | bytes 6291460
  57.2 3.7 %copy-start.1 = (bf16[16,512,256]{2,1,0:T(8,128)(2,1)S(1)}, bf16[16,512,256]{2,1,0:T(8,128)(2,1)}, u32[]{:S(2)}) copy-start(bf16[16,512,256]{2,1,0:T(8,128)(2,1)} %reshape.451) | copy-start | bytes 12582916
  66.1 27.8 %all-to-all-start.1 = ((bf16[128,8,512]{2,1,0:T(8,128)(2,1)}), bf16[128,8,512]{2,1,0:T(8,128)(2,1)S(1)}, u32[]{:S(2)}, u32[]{:S(2)}) async-start(bf16[128,8,512]{2,1,0:T(8,128)(2,1)} %bitcast.15), calls=%async_computation.1 | async-start | bytes 2097152 | tf_op jit(solution)/shard_map/all_to_all | solution.py:124
  98.9 15.9 %all-to-all-start.2 = ((f32[16,2,32,128]{3,2,1,0:T(8,128)}), f32[16,2,32,128]{3,2,1,0:T(8,128)S(1)}, u32[]{:S(2)}, u32[]{:S(2)}) async-start(f32[16,2,32,128]{3,2,1,0:T(8,128)} %copy.75), calls=%async_computation.2 | async-start | bytes 1048576 | tf_op jit(solution)/shard_map/all_to_all | solution.py:167

commit v2 on v1

--- a/solution.py
+++ b/solution.py
@@ -61,8 +61,15 @@
     fitted = jnp.einsum("rce,ep->rcp", fit_weights, eigen_flats, precision=lax.Precision.HIGH)
     flattened = (scaled - fitted).astype(jnp.bfloat16)
 
-    gathered = lax.all_to_all(flattened, "srow", split_axis=1, concat_axis=0, tiled=True)
-    cols_here = gathered.shape[1]
+    n_half = 2
+    p_half = n_pix // n_half
+    gathered = [
+        lax.all_to_all(
+            flattened[:, :, h * p_half : (h + 1) * p_half], "srow", split_axis=1, concat_axis=0, tiled=True
+        )
+        for h in range(n_half)
+    ]
+    cols_here = gathered[0].shape[1]
 
     k_blk = row_count // n_scol
     j_blk = col_count // n_srow
@@ -70,12 +77,7 @@
     row_cos, row_sin = square_waves(row_count)
     forward_rows = jnp.stack([row_cos, -row_sin], axis=0).reshape(2, n_scol, k_blk, row_count)
     forward_rows = forward_rows.transpose(1, 0, 2, 3).reshape(2 * row_count, row_count)
-    spec = jnp.dot(
-        forward_rows.astype(jnp.bfloat16),
-        gathered.reshape(row_count, cols_here * n_pix),
-        preferred_element_type=jnp.float32,
-    ).astype(jnp.bfloat16)
-    spec = spec.reshape(n_scol, 2 * k_blk * cols_here, n_pix)
+    forward_rows = forward_rows.astype(jnp.bfloat16)
 
     def shift_of(freq, count):
         signed = freq - count if freq >= count // 2 else freq
@@ -110,15 +112,22 @@
     dx_of_n = jnp.broadcast_to(own_dx[:, None, :, None], (n_scol, 2, k_blk, cols_here))
     dx_of_n = dx_of_n.reshape(n_scol, 1, 2 * k_blk * cols_here)
     summed = None
-    for d in range(n_dx):
-        part = jnp.einsum(
-            "axp,anp->axn",
-            weight[:, :, :, d].reshape(n_scol, n_srow * n_dyl, n_pix),
-            spec,
+    for h in range(n_half):
+        spec = jnp.dot(
+            forward_rows,
+            gathered[h].reshape(row_count, cols_here * p_half),
             preferred_element_type=jnp.float32,
-        )
-        part = jnp.where(dx_of_n == d, part, 0.0)
-        summed = part if summed is None else summed + part
+        ).astype(jnp.bfloat16)
+        spec = spec.reshape(n_scol, 2 * k_blk * cols_here, p_half)
+        for d in range(n_dx):
+            part = jnp.einsum(
+                "axp,anp->axn",
+                weight[:, :, :, d, h * p_half : (h + 1) * p_half].reshape(n_scol, n_srow * n_dyl, p_half),
+                spec,
+                preferred_element_type=jnp.float32,
+            )
+            part = jnp.where(dx_of_n == d, part, 0.0)
+            summed = part if summed is None else summed + part
     summed = summed.reshape(n_dev, n_dyl, 2 * k_blk * cols_here).astype(jnp.bfloat16)
 
     summed = lax.all_to_all(summed, ("scol", "srow"), split_axis=0, concat_axis=0, tiled=True)

time: 128 us -> 137 us (1.070)
  waiting for transfers between devices: 40.2 us -> 27.7 us
  matrix products: 22.9 us -> 32.1 us
  starting transfers between devices: 18.6 us -> 26.3 us
  local copies, waits for them, and re-layouts: 18.7 us -> 20.9 us
  other arithmetic: 16.7 us -> 18.7 us
    all_to_all x1 -> x2, waiting for transfers between devices: 12.3 us -> 0.01 us  [on_device(): lax.all_to_all(flattened[:, :, h * p_half:(h + 1) * p_half], 'srow', spli...]
    dot_general x5 -> x10, matrix products: 13.2 us -> 22.4 us  [the longest x8 17.2 us: on_device(): jnp.einsum('axp,anp->axn', weight[:, :, :, d, h * p_half:(h + 1) * p_half...]
    all_to_all x1 -> x2, starting transfers between devices: 6.45 us -> 12.3 us  [on_device(): lax.all_to_all(flattened[:, :, h * p_half:(h + 1) * p_half], 'srow', spli...]
    slice x0 -> x3, local copies, waits for them, and re-layouts: none -> 3.8 us  [on_device(): flattened[:, :, h * p_half:(h + 1) * p_half]]
    convert_element_type x1 -> x0, local copies, waits for them, and re-layouts: 2.53 us -> none  [on_device(): flattened = (scaled - fitted).astype(jnp.bfloat16)]
    all_to_all x1, starting transfers between devices: 8.58 us -> 10.5 us  [on_device(): lax.all_to_all(summed, ('scol', 'srow'), split_axis=0, concat_axis=0, til...]
    reshape x1 -> x2, local copies, waits for them, and re-layouts: 7.54 us -> 7 us  [on_device(): spec = spec.reshape(n_scol, 2 * k_blk * cols_here, p_half)]
  transfers between devices with their start and end apart: 3 -> 4, of which waited for: 3 -> 2; matrix products, arithmetic and copies ran while one was open for 13% -> 27% of each run, Pallas kernels for 0% -> 0%
where the time goes in v2:
time: 137 us; the launch traced here: 136 us
  matrix products  32.1 us (23%)
  waiting for transfers between devices  27.7 us (20%)
  starting transfers between devices  26.3 us (19%)
  local copies, waits for them, and re-layouts  20.9 us (15%)
  other arithmetic  18.7 us (14%)
  blocking collectives  9.64 us (7%)
    all_to_all x1, waiting for transfers between devices, on_device(): lax.all_to_all(summed, ('scol', 'srow'), split_axis=0, concat_axis=0, til...  17.6 us
    dot_general x8, matrix products, on_device(): jnp.einsum('axp,anp->axn', weight[:, :, :, d, h * p_half:(h + 1) * p_half...  17.2 us
    all_to_all x2, starting transfers between devices, on_device(): lax.all_to_all(flattened[:, :, h * p_half:(h + 1) * p_half], 'srow', spli...  12.3 us
    all_to_all x1, starting transfers between devices, on_device(): lax.all_to_all(summed, ('scol', 'srow'), split_axis=0, concat_axis=0, til...  10.5 us
    all_to_all x1, waiting for transfers between devices, on_device(): half = lax.all_to_all(half, 'scol', split_axis=0, concat_axis=0, tiled=True)  10.1 us
    all_to_all x1, blocking collectives, on_device(): lax.all_to_all(image, 'srow', split_axis=0, concat_axis=0, tiled=True)  9.64 us
    reshape x2, local copies, waits for them, and re-layouts, on_device(): spec = spec.reshape(n_scol, 2 * k_blk * cols_here, p_half)  7 us
    dot_general x2, matrix products, on_device(): jnp.dot(forward_rows, gathered[h].reshape(row_count, cols_here * p_half),...  5.21 us
  transfers between devices with their start and end apart: 4, of which 2 were waited for; matrix products, arithmetic and copies ran while one was open for 27% of the time, Pallas kernels for 0%

profile of v2, /device:TPU:0, one launch (start us, length us, event | category | flops | bytes accessed | tf_op | source)
XLA Modules:
  0.0 135.9 jit_solution(9334202905865935817)
XLA Ops:
  0.0 2.4 %convert_reduce_fusion = f32[64,64]{1,0:T(8,128)S(1)} fusion(bf16[64,64,256]{2,1,0:T(8,128)(2,1)} %param.8), kind=kLoop, calls=%fused_computation | loop fusion | flops 2093056 | bytes 2113536 | tf_op jit(solution)/shard_map/reduce_sum | solution.py:58
  2.4 2.6 %fusion.1 = f32[64,64,16]{1,2,0:T(8,128)S(1)} fusion(bf16[64,64,256]{2,1,0:T(8,128)(2,1)S(1)} %copy-done.6, f32[64,64]{1,0:T(8,128)S(1)} %broadcast_multiply_fusion.1, f32[256]{0:T(256)S(1)} %copy-done.22, f32[16,256]{1,0:T(8,128)S(1)} %copy-done), kind=kOutput, calls=%fused_computation.7 | convolution fusion | flops 103809024 | bytes 2393088 | tf_op jit(solution)/shard_map/rcp,ep->rce/dot_general | solution.py:60
  5.0 2.8 %subtract_convert_fusion = bf16[64,64,256]{2,1,0:T(8,128)(2,1)S(1)} fusion(bf16[64,64,256]{2,1,0:T(8,128)(2,1)S(1)} %copy-done.6, f32[64,64,16]{1,2,0:T(8,128)S(1)} %fusion.1, f32[64,64]{1,0:T(8,128)S(1)} %broadcast_multiply_fusion.1, f32[256]{0:T(256)S(1)} %copy-done.22, f32[16,256]{1,0:T(8,128)S(1)} %copy-done), kind=kOutput, calls=%fused_computation.3 | convolution fusion | flops 105906176 | bytes 4490240 | tf_op jit(solution)/shard_map/rce,ep->rcp/dot_general | solution.py:61
  7.8 0.4 fusion.75
  8.2 1.7 %copy.79 = bf16[64,64,128]{2,0,1:T(8,128)(2,1)} copy(bf16[64,64,128]{2,1,0:T(8,128)(2,1)S(1)} %get-tuple-element.10) | data formatting | bytes 2097152 | tf_op jit(solution)/shard_map/slice | solution.py:68
  9.9 6.6 %all-to-all-start.1 = ((bf16[64,64,128]{2,0,1:T(8,128)(2,1)}), bf16[64,64,128]{2,0,1:T(8,128)(2,1)S(1)}, u32[]{:S(2)}, u32[]{:S(2)}) async-start(bf16[64,64,128]{2,0,1:T(8,128)(2,1)} %copy.79), calls=%async_computation.1 | async-start | bytes 2097152 | tf_op jit(solution)/shard_map/all_to_all | solution.py:67
  16.4 1.0 fusion.40
  17.5 0.2 fusion.67
  17.7 0.2 copy.72
  17.8 0.9 copy.73
  18.7 0.6 fusion.71
  19.3 0.7 iota_add_fusion
  20.0 0.6 broadcast_compare_fusion.2
  20.6 0.7 dynamic_slice.3
  21.3 1.2 fusion.74
  22.5 0.3 fusion.50
  22.8 0.2 copy-done.14
  23.0 3.7 %subtract_convert_fusion.2 = (bf16[512,4,128]{2,1,0:T(4,128)(2,1)}, bf16[512,4,128]{2,1,0:T(4,128)(2,1)S(1)}) fusion(f32[512,128]{1,0:T(8,128)S(1)} %get-tuple-element.37, f32[512,4]{1,0:T(8,128)} %copy.73, f32[512,128]{1,0:T(8,128)S(1)} %get-tuple-element.38, f32[512,4]{1,0:T(8,128)S(1)} %copy.72), kind=kLoop, calls=%fused_computation.30 | loop fusion | flops 2359296 | bytes 1589248 | tf_op jit(solution)/shard_map/convert.3
  26.7 0.7 iota_add_fusion.1
  27.3 0.2 neg.22
  27.5 1.2 sub.154
  28.8 1.8 %copy.74 = bf16[64,64,128]{2,0,1:T(8,128)(2,1)} copy(bf16[64,64,128]{2,1,0:T(8,128)(2,1)S(1)} %get-tuple-element.9) | data formatting | bytes 2097152 | tf_op jit(solution)/shard_map/slice | solution.py:68
  30.6 0.1 copy.71
  30.7 0.1 copy.76
  30.9 0.1 copy.77
  31.1 0.1 copy.78
  31.2 0.1 pad_maximum_fusion
  31.4 0.1 subtract_multiply_fusion
  31.5 2.7 %subtract_convert_fusion.1 = bf16[16,8,8,4,256]{4,2,1,0,3:T(8,128)(2,1)} fusion(s32[8,8,256]{2,1,0:T(8,128)S(1)} %get-tuple-element.14, s32[16,4,256]{2,0,1:T(8,128)S(1)} %get-tuple-element.16, s32[8,8,256]{2,1,0:T(8,128)S(1)} %get-tuple-element.13, s32[16,4,256]{2,0,1:T(8,128)S(1)} %get-tuple-element.15), kind=kLoop, calls=%fused_computation.4 | loop fusion | flops 8388608 | bytes 2359296 | tf_op jit(solution)/shard_map/convert_element_type | solution.py:109
  34.2 5.7 %all-to-all-start = ((bf16[64,64,128]{2,0,1:T(8,128)(2,1)}), bf16[64,64,128]{2,0,1:T(8,128)(2,1)S(1)}, u32[]{:S(2)}, u32[]{:S(2)}) async-start(bf16[64,64,128]{2,0,1:T(8,128)(2,1)} %copy.74), calls=%async_computation | async-start | bytes 2097152 | tf_op jit(solution)/shard_map/all_to_all | solution.py:67
  39.9 0.7 copy.80
  40.6 2.6 %convolution_convert_fusion = bf16[1024,1024]{1,0:T(8,128)(2,1)} fusion(bf16[1024,512]{1,0:T(8,128)(2,1)S(1)} %bitcast.140, bf16[64,8,8,128]{3,2,1,0:T(8,128)(2,1)S(1)} %bitcast.143), kind=kOutput, calls=%fused_computation.12 | convolution fusion | flops 1074790400 | bytes 4194304 | tf_op jit(solution)/shard_map/dot_general | solution.py:116
  43.1 2.8 %reshape.461 = bf16[16,512,128]{2,1,0:T(8,128)(2,1)S(1)} reshape(bf16[1024,1024]{1,0:T(8,128)(2,1)} %convolution_convert_fusion) | data formatting | bytes 4194304 | tf_op jit(solution)/shard_map/reshape | solution.py:121
  46.0 3.1 %fusion.24 = f32[16,64,512]{2,1,0:T(8,128)} fusion(bf16[16,512,128]{2,1,0:T(8,128)(2,1)S(1)} %reshape.461, bf16[16,8,8,4,256]{4,2,1,0,3:T(8,128)(2,1)} %subtract_convert_fusion.1), kind=kOutput, calls=%fused_computation.55 | convolution fusion | flops 134217728 | bytes 4456448 | tf_op jit(solution)/shard_map/axp,anp->axn/dot_general | solution.py:123
  49.1 3.1 %fusion.25 = f32[16,64,512]{2,1,0:T(8,128)} fusion(bf16[16,512,128]{2,1,0:T(8,128)(2,1)S(1)} %reshape.461, bf16[16,8,8,4,256]{4,2,1,0,3:T(8,128)(2,1)} %subtract_convert_fusion.1), kind=kOutput, calls=%fused_computation.57 | convolution fusion | flops 134217728 | bytes 4456448 | tf_op jit(solution)/shard_map/axp,anp->axn/dot_general | solution.py:123
  52.2 3.2 %fusion.26 = f32[16,64,512]{2,1,0:T(8,128)} fusion(bf16[16,512,128]{2,1,0:T(8,128)(2,1)S(1)} %reshape.461, bf16[16,8,8,4,256]{4,2,1,0,3:T(8,128)(2,1)} %subtract_convert_fusion.1), kind=kOutput, calls=%fused_computation.59 | convolution fusion | flops 134217728 | bytes 4456448 | tf_op jit(solution)/shard_map/axp,anp->axn/dot_general | solution.py:123
  55.4 0.7 copy.75
  56.1 0.5 copy-done.8
  56.6 2.7 %convolution_convert_fusion.1 = bf16[1024,1024]{1,0:T(8,128)(2,1)} fusion(bf16[1024,512]{1,0:T(8,128)(2,1)S(1)} %bitcast.141, bf16[64,8,8,128]{3,2,1,0:T(8,128)(2,1)S(1)} %bitcast.142), kind=kOutput, calls=%fused_computation.13 | convolution fusion | flops 1074790400 | bytes 4194304 | tf_op jit(solution)/shard_map/dot_general | solution.py:116
  59.3 4.2 %reshape.459 = bf16[16,512,128]{2,1,0:T(8,128)(2,1)} reshape(bf16[1024,1024]{1,0:T(8,128)(2,1)} %convolution_convert_fusion.1) | data formatting | bytes 4194304 | tf_op jit(solution)/shard_map/reshape | solution.py:121
  63.5 2.7 %fusion.27 = f32[16,64,512]{2,1,0:T(8,128)S(1)} fusion(bf16[16,512,128]{2,1,0:T(8,128)(2,1)} %reshape.459, bf16[16,8,8,4,256]{4,2,1,0,3:T(8,128)(2,1)} %subtract_convert_fusion.1), kind=kOutput, calls=%fused_computation.61 | convolution fusion | flops 134217728 | bytes 4456448 | tf_op jit(solution)/shard_map/axp,anp->axn/dot_general | solution.py:123
  66.1 0.3 copy-done.2
  66.4 0.8 fusion.28
  67.2 0.8 fusion.29
  68.1 0.9 fusion.30
  69.0 0.9 copy-done.3
  69.8 0.6 copy-done.4
  70.5 2.6 %add_convert_fusion = bf16[16,64,512]{2,1,0:T(8,128)(2,1)} fusion(f32[16,64,512]{2,1,0:T(8,128)S(1)} %copy-done.3, f32[16,64,512]{2,1,0:T(8,128)S(1)} %copy-done.4, f32[16,64,512]{2,1,0:T(8,128)S(1)} %copy-done.5, f32[16,64,512]{2,1,0:T(8,128)S(1)} %fusion.27, f32[16,64,512]{2,1,0:T(8,128)S(1)} %fusion.28, f32[16,64,512]{2,1,0:T(8,128)S(1)} %fusion.29, ...), kind=kOutput, calls=%fused_computation.9 | convolution fusion | flops 142606336 | bytes 18120704 | tf_op jit(solution)/shard_map/axp,anp->axn/dot_general | solution.py:123
  73.0 10.5 %all-to-all-start.2 = ((bf16[128,8,512]{2,1,0:T(8,128)(2,1)}), bf16[128,8,512]{2,1,0:T(8,128)(2,1)S(1)}, u32[]{:S(2)}, u32[]{:S(2)}) async-start(bf16[128,8,512]{2,1,0:T(8,128)(2,1)} %bitcast.22), calls=%async_computation.2 | async-start | bytes 2097152 | tf_op jit(solution)/shard_map/all_to_all | solution.py:133
  83.6 1.0 fusion.44
  84.6 0.2 maximum_maximum_fusion.1
  84.9 17.6 %all-to-all-done.2 = bf16[128,8,512]{2,1,0:T(8,128)(2,1)S(1)} async-done(((bf16[128,8,512]{2,1,0:T(8,128)(2,1)}), bf16[128,8,512]{2,1,0:T(8,128)(2,1)S(1)}, u32[]{:S(2)}, u32[]{:S(2)}) %all-to-all-start.2) | async-done | bytes 1048608 | tf_op jit(solution)/shard_map/all_to_all | solution.py:133
  102.5 1.0 copy.94
  103.5 1.8 %fusion.76 = f32[8,2,32,8,2,128]{5,3,4,2,1,0:T(8,128)S(1)} fusion(bf16[8,2,32,8,128,1]{4,3,5,2,1,0:T(8,128)(2,1)S(1)} %bitcast.138, f32[2,128,128,1,1,1]{2,1,0,5,4,3:T(8,128)S(1)} %bitcast.144), kind=kOutput, calls=%fused_computation.163 | convolution fusion | flops 1610612736 | bytes 5373952 | tf_op jit(solution)/shard_map/dot_general | solution.py:140
  105.3 0.8 add_reduce_fusion
  106.1 0.6 convolution_bitcast_fusion
  106.7 0.8 copy.84
  107.5 3.6 %all-to-all-start.3 = ((f32[16,2,32,128]{3,2,1,0:T(8,128)}), f32[16,2,32,128]{3,2,1,0:T(8,128)S(1)}, u32[]{:S(2)}, u32[]{:S(2)}) async-start(f32[16,2,32,128]{3,2,1,0:T(8,128)} %copy.84), calls=%async_computation.3 | async-start | bytes 1048576 | tf_op jit(solution)/shard_map/all_to_all | solution.py:176
  111.1 2.1 %fusion.31 = (f32[128,1024]{0,1:T(8,128)S(1)}, f32[128,1024]{0,1:T(8,128)S(1)}, f32[128,1024]{0,1:T(8,128)S(1)}) fusion(s32[128]{0:T(128)S(1)} %copy-done.15), kind=kLoop, calls=%fused_computation.68 | loop fusion | flops 1966080 | bytes 1573376 | tf_op jit(solution)/shard_map/sin | solution.py:16
  113.2 0.1 maximum_maximum_fusion
  113.3 10.1 %all-to-all-done.3 = f32[16,2,32,128]{3,2,1,0:T(8,128)S(1)} async-done(((f32[16,2,32,128]{3,2,1,0:T(8,128)}), f32[16,2,32,128]{3,2,1,0:T(8,128)S(1)}, u32[]{:S(2)}, u32[]{:S(2)}) %all-to-all-start.3) | async-done | bytes 524320 | tf_op jit(solution)/shard_map/all_to_all | solution.py:176
  123.5 2.0 %convolution_bitcast_fusion.1 = f32[8,32,2,128]{3,1,0,2:T(8,128)S(1)} fusion(f32[2,8,128,256]{3,2,1,0:T(8,128)S(1)} %bitcast.135, f32[32,256,1,1]{1,0,2,3:T(8,128)S(1)} %reshape.469), kind=kOutput, calls=%fused_computation.15 | convolution fusion | flops 201326592 | bytes 2392064 | tf_op jit(solution)/shard_map/dot_general | solution.py:190
  125.6 9.6 %all_to_all.45 = f32[8,32,2,128]{3,1,2,0:T(8,128)S(1)} all-to-all(f32[8,32,2,128]{3,1,2,0:T(8,128)S(1)} %copy.87), channel_id=1, replica_groups=mesh['srow'=8,'scol'=16] {'srow'}, dimensions={0} | all-to-all | bytes 524288 | tf_op jit(solution)/shard_map/all_to_all | solution.py:192
  135.2 0.6 copy.89
  (63 shorter events, 0.5 us)
Async XLA Ops:
  0.0 2.4 %copy-start = (f32[16,256]{1,0:T(8,128)S(1)}, f32[16,256]{1,0:T(8,128)}, u32[]{:S(2)}) copy-start(f32[16,256]{1,0:T(8,128)} %param.10) | copy-start | bytes 49156
  0.0 2.4 %copy-start.6 = (bf16[64,64,256]{2,1,0:T(8,128)(2,1)S(1)}, bf16[64,64,256]{2,1,0:T(8,128)(2,1)}, u32[]{:S(2)}) copy-start(bf16[64,64,256]{2,1,0:T(8,128)(2,1)} %param.8) | copy-start | bytes 6291460
  0.0 2.4 %copy-start.22 = (f32[256]{0:T(256)S(1)}, f32[256]{0:T(256)}, u32[]{:S(2)}) copy-start(f32[256]{0:T(256)} %param.9) | copy-start | bytes 3076
  9.9 8.8 %copy-start.18 = (s32[256]{0:T(256)S(1)}, s32[256]{0:T(256)}, u32[]{:S(2)}) copy-start(s32[256]{0:T(256)} %param.11) | copy-start | bytes 3076
  9.9 9.4 %copy-start.19 = (s32[8]{0:T(128)S(1)}, s32[8]{0:T(128)}, u32[]{:S(2)}) copy-start(s32[8]{0:T(128)} %constant.185.clone) | copy-start | bytes 100
  9.9 10.1 %copy-start.20 = (s32[16]{0:T(128)S(1)}, s32[16]{0:T(128)}, u32[]{:S(2)}) copy-start(s32[16]{0:T(128)} %constant.186) | copy-start | bytes 196
  9.9 24.3 %all-to-all-start.1 = ((bf16[64,64,128]{2,0,1:T(8,128)(2,1)}), bf16[64,64,128]{2,0,1:T(8,128)(2,1)S(1)}, u32[]{:S(2)}, u32[]{:S(2)}) async-start(bf16[64,64,128]{2,0,1:T(8,128)(2,1)} %copy.79), calls=%async_computation.1 | async-start | bytes 2097152 | tf_op jit(solution)/shard_map/all_to_all | solution.py:67
  22.5 0.5 copy-start.14
  27.3 3.3 %copy-start.13 = (pred[16,32]{0,1:T(8,128)(4,1)S(1)}, pred[16,32]{0,1:T(8,128)(4,1)}, u32[]{:S(2)}) copy-start(pred[16,32]{0,1:T(8,128)(4,1)} %get-tuple-element.21) | copy-start | bytes 1540
  27.3 3.4 %copy-start.12 = (pred[16,32]{0,1:T(8,128)(4,1)S(1)}, pred[16,32]{0,1:T(8,128)(4,1)}, u32[]{:S(2)}) copy-start(pred[16,32]{0,1:T(8,128)(4,1)} %get-tuple-element.22) | copy-start | bytes 1540
  27.3 3.5 %copy-start.11 = (pred[16,32]{0,1:T(8,128)(4,1)S(1)}, pred[16,32]{0,1:T(8,128)(4,1)}, u32[]{:S(2)}) copy-start(pred[16,32]{0,1:T(8,128)(4,1)} %get-tuple-element.23) | copy-start | bytes 1540
  27.3 3.7 %copy-start.10 = (pred[16,32]{0,1:T(8,128)(4,1)S(1)}, pred[16,32]{0,1:T(8,128)(4,1)}, u32[]{:S(2)}) copy-start(pred[16,32]{0,1:T(8,128)(4,1)} %get-tuple-element.24) | copy-start | bytes 1540
  28.8 2.5 %copy-start.17 = (s32[256]{0:T(256)S(1)}, s32[256]{0:T(256)}, u32[]{:S(2)}) copy-start(s32[256]{0:T(256)} %get-tuple-element.19) | copy-start | bytes 3076
  28.8 2.6 %copy-start.9 = (s32[8,8]{1,0:T(8,128)S(1)}, s32[8,8]{1,0:T(8,128)}, u32[]{:S(2)}) copy-start(s32[8,8]{1,0:T(8,128)} %iota_add_fusion) | copy-start | bytes 772
  28.8 2.6 %copy-start.16 = (s32[256]{0:T(256)S(1)}, s32[256]{0:T(256)}, u32[]{:S(2)}) copy-start(s32[256]{0:T(256)} %get-tuple-element.20) | copy-start | bytes 3076
  31.3 9.3 %copy-start.7 = (bf16[2,16,32,512]{3,2,0,1:T(8,128)(2,1)}, bf16[2,16,32,512]{3,2,0,1:T(8,128)(2,1)S(1)}, u32[]{:S(2)}) copy-start(bf16[2,16,32,512]{3,2,0,1:T(8,128)(2,1)S(1)} %pad_maximum_fusion) | copy-start | bytes 3145732
  34.2 21.2 %all-to-all-start = ((bf16[64,64,128]{2,0,1:T(8,128)(2,1)}), bf16[64,64,128]{2,0,1:T(8,128)(2,1)S(1)}, u32[]{:S(2)}, u32[]{:S(2)}) async-start(bf16[64,64,128]{2,0,1:T(8,128)(2,1)} %copy.74), calls=%async_computation | async-start | bytes 2097152 | tf_op jit(solution)/shard_map/all_to_all | solution.py:67
  55.4 1.2 copy-start.8
  63.5 2.7 %copy-start.1 = (bf16[16,512,128]{2,1,0:T(8,128)(2,1)S(1)}, bf16[16,512,128]{2,1,0:T(8,128)(2,1)}, u32[]{:S(2)}) copy-start(bf16[16,512,128]{2,1,0:T(8,128)(2,1)} %reshape.459) | copy-start | bytes 6291460
  63.5 2.9 %copy-start.2 = (bf16[16,8,8,4,256]{4,2,1,0,3:T(8,128)(2,1)S(1)}, bf16[16,8,8,4,256]{4,2,1,0,3:T(8,128)(2,1)}, u32[]{:S(2)}) copy-start(bf16[16,8,8,4,256]{4,2,1,0,3:T(8,128)(2,1)} %subtract_convert_fusion.1) | copy-start | bytes 6291460
  67.2 1.7 %copy-start.5 = (f32[16,64,512]{2,1,0:T(8,128)S(1)}, f32[16,64,512]{2,1,0:T(8,128)}, u32[]{:S(2)}) copy-start(f32[16,64,512]{2,1,0:T(8,128)} %fusion.26) | copy-start | bytes 6291460
  68.1 1.7 %copy-start.3 = (f32[16,64,512]{2,1,0:T(8,128)S(1)}, f32[16,64,512]{2,1,0:T(8,128)}, u32[]{:S(2)}) copy-start(f32[16,64,512]{2,1,0:T(8,128)} %fusion.24) | copy-start | bytes 6291460
  68.1 2.4 %copy-start.4 = (f32[16,64,512]{2,1,0:T(8,128)S(1)}, f32[16,64,512]{2,1,0:T(8,128)}, u32[]{:S(2)}) copy-start(f32[16,64,512]{2,1,0:T(8,128)} %fusion.25) | copy-start | bytes 6291460
  73.0 11.8 %copy-start.21 = (s32[128]{0:T(128)S(1)}, s32[128]{0:T(128)}, u32[]{:S(2)}) copy-start(s32[128]{0:T(128)} %get-tuple-element.35) | copy-start | bytes 1540
  73.0 11.8 %copy-start.15 = (s32[128]{0:T(128)S(1)}, s32[128]{0:T(128)}, u32[]{:S(2)}) copy-start(s32[128]{0:T(128)} %copy-done.14) | copy-start | bytes 1540
  73.0 29.4 %all-to-all-start.2 = ((bf16[128,8,512]{2,1,0:T(8,128)(2,1)}), bf16[128,8,512]{2,1,0:T(8,128)(2,1)S(1)}, u32[]{:S(2)}, u32[]{:S(2)}) async-start(bf16[128,8,512]{2,1,0:T(8,128)(2,1)} %bitcast.22), calls=%async_computation.2 | async-start | bytes 2097152 | tf_op jit(solution)/shard_map/all_to_all | solution.py:133
  107.5 15.9 %all-to-all-start.3 = ((f32[16,2,32,128]{3,2,1,0:T(8,128)}), f32[16,2,32,128]{3,2,1,0:T(8,128)S(1)}, u32[]{:S(2)}, u32[]{:S(2)}) async-start(f32[16,2,32,128]{3,2,1,0:T(8,128)} %copy.84), calls=%async_computation.3 | async-start | bytes 1048576 | tf_op jit(solution)/shard_map/all_to_all | solution.py:176

commit v3 on v1

--- a/solution.py
+++ b/solution.py
@@ -164,8 +164,8 @@
     psi = psi.transpose(1, 0, 2).reshape(2 * k_blk, j_blk)
     half = jnp.dot(inverse_rows, psi, precision=HIGHEST, preferred_element_type=jnp.float32)
     half = half.reshape(2, n_scol, row_count // n_scol, j_blk).transpose(1, 0, 2, 3)
-    half = lax.all_to_all(half, "scol", split_axis=0, concat_axis=0, tiled=True)
-    half = jnp.sum(half, axis=0)
+    half = lax.all_to_all(half.astype(jnp.bfloat16), "scol", split_axis=0, concat_axis=0, tiled=True)
+    half = jnp.sum(half.astype(jnp.float32), axis=0)
     out_rows = half.shape[1]
 
     out_cols = col_count // n_srow
@@ -180,8 +180,8 @@
     half = half.transpose(1, 0, 2).reshape(out_rows, 2 * j_blk)
     image = jnp.dot(half, inverse_cols, precision=HIGHEST, preferred_element_type=jnp.float32)
     image = image.reshape(out_rows, 2, n_srow, out_cols).transpose(2, 0, 1, 3)
-    image = lax.all_to_all(image, "srow", split_axis=0, concat_axis=0, tiled=True)
-    image = jnp.sum(image, axis=0) * (1.0 / (row_count * col_count))
+    image = lax.all_to_all(image.astype(jnp.bfloat16), "srow", split_axis=0, concat_axis=0, tiled=True)
+    image = jnp.sum(image.astype(jnp.float32), axis=0) * (1.0 / (row_count * col_count))
     return image
 
 

time: 128 us -> 125 us (0.977)
  waiting for transfers between devices: 40.2 us -> 33.3 us
  other arithmetic: 16.7 us -> 20.4 us
    all_to_all x1, waiting for transfers between devices: 17.8 us -> 14.1 us  [on_device(): lax.all_to_all(summed, ('scol', 'srow'), split_axis=0, concat_axis=0, til...]
    all_to_all x1, waiting for transfers between devices: 10.1 us -> 8.13 us  [on_device(): lax.all_to_all(half.astype(jnp.bfloat16), 'scol', split_axis=0, concat_ax...]
  transfers between devices with their start and end apart: 3 -> 3, of which waited for: 3 -> 3; matrix products, arithmetic and copies ran while one was open for 13% -> 17% of each run, Pallas kernels for 0% -> 0%
where the time goes in v3:
time: 125 us; the launch traced here: 124 us
  waiting for transfers between devices  33.3 us (27%)
  matrix products  23 us (18%)
  other arithmetic  20.4 us (16%)
  local copies, waits for them, and re-layouts  19 us (15%)
  starting transfers between devices  18.7 us (15%)
  blocking collectives  8.97 us (7%)
    all_to_all x1, waiting for transfers between devices, on_device(): lax.all_to_all(summed, ('scol', 'srow'), split_axis=0, concat_axis=0, til...  14.1 us
    all_to_all x1, waiting for transfers between devices, on_device(): lax.all_to_all(flattened, 'srow', split_axis=1, concat_axis=0, tiled=True)  11.1 us
    all_to_all x1, blocking collectives, on_device(): lax.all_to_all(image.astype(jnp.bfloat16), 'srow', split_axis=0, concat_a...  8.97 us
    dot_general x4, matrix products, on_device(): jnp.einsum('axp,anp->axn', weight[:, :, :, d].reshape(n_scol, n_srow * n_...  8.88 us
    all_to_all x1, starting transfers between devices, on_device(): lax.all_to_all(summed, ('scol', 'srow'), split_axis=0, concat_axis=0, til...  8.58 us
    all_to_all x1, waiting for transfers between devices, on_device(): lax.all_to_all(half.astype(jnp.bfloat16), 'scol', split_axis=0, concat_ax...  8.13 us
    reshape x1, local copies, waits for them, and re-layouts, on_device(): spec = spec.reshape(n_scol, 2 * k_blk * cols_here, n_pix)  7.55 us
    all_to_all x1, starting transfers between devices, on_device(): lax.all_to_all(flattened, 'srow', split_axis=1, concat_axis=0, tiled=True)  6.58 us
  transfers between devices with their start and end apart: 3, of which 3 were waited for; matrix products, arithmetic and copies ran while one was open for 17% of the time, Pallas kernels for 0%

profile of v3, /device:TPU:0, one launch (start us, length us, event | category | flops | bytes accessed | tf_op | source)
XLA Modules:
  0.0 123.7 jit_solution(4727386534011657394)
XLA Ops:
  0.0 0.0 copy-start
  0.0 2.4 %convert_reduce_fusion = f32[64,64]{1,0:T(8,128)S(1)} fusion(bf16[64,64,256]{2,1,0:T(8,128)(2,1)} %param.8), kind=kLoop, calls=%fused_computation | loop fusion | flops 2093056 | bytes 2113536 | tf_op jit(solution)/shard_map/reduce_sum | solution.py:58
  2.4 0.0 copy-done
  2.4 0.0 copy-done.3
  2.4 0.0 copy-done.13
  2.4 2.6 %fusion.1 = f32[64,64,16]{1,2,0:T(8,128)S(1)} fusion(bf16[64,64,256]{2,1,0:T(8,128)(2,1)S(1)} %copy-done.3, f32[64,64]{1,0:T(8,128)S(1)} %broadcast_multiply_fusion.1, f32[256]{0:T(256)S(1)} %copy-done.13, f32[16,256]{1,0:T(8,128)S(1)} %copy-done), kind=kOutput, calls=%fused_computation.8 | convolution fusion | flops 103809024 | bytes 2393088 | tf_op jit(solution)/shard_map/rcp,ep->rce/dot_general | solution.py:60
  5.0 2.8 %subtract_convert_fusion = bf16[64,64,256]{2,1,0:T(8,128)(2,1)S(1)} fusion(bf16[64,64,256]{2,1,0:T(8,128)(2,1)S(1)} %copy-done.3, f32[64,64,16]{1,2,0:T(8,128)S(1)} %fusion.1, f32[64,64]{1,0:T(8,128)S(1)} %broadcast_multiply_fusion.1, f32[256]{0:T(256)S(1)} %copy-done.13, f32[16,256]{1,0:T(8,128)S(1)} %copy-done), kind=kOutput, calls=%fused_computation.3 | convolution fusion | flops 105906176 | bytes 4490240 | tf_op jit(solution)/shard_map/rce,ep->rcp/dot_general | solution.py:61
  7.8 2.5 %copy.67 = bf16[64,64,256]{2,0,1:T(8,128)(2,1)} copy(bf16[64,64,256]{2,1,0:T(8,128)(2,1)S(1)} %subtract_convert_fusion) | data formatting | bytes 4194304 | tf_op jit(solution)/shard_map/convert_element_type | solution.py:62
  10.3 6.6 %all-to-all-start = ((bf16[64,64,256]{2,0,1:T(8,128)(2,1)}), bf16[64,64,256]{2,0,1:T(8,128)(2,1)S(1)}, u32[]{:S(2)}, u32[]{:S(2)}) async-start(bf16[64,64,256]{2,0,1:T(8,128)(2,1)} %copy.67), calls=%async_computation | async-start | bytes 4194304 | tf_op jit(solution)/shard_map/all_to_all | solution.py:64
  16.9 1.0 fusion.34
  18.0 0.2 fusion.61
  18.1 0.2 copy.65
  18.3 0.9 copy.66
  19.2 0.0 copy-done.9
  19.2 0.6 dynamic_slice.3
  19.8 1.2 fusion.68
  20.9 0.3 fusion.44
  21.3 0.2 copy-done.6
  21.4 3.7 %subtract_convert_fusion.2 = (bf16[512,4,128]{2,1,0:T(4,128)(2,1)}, bf16[512,4,128]{2,1,0:T(4,128)(2,1)S(1)}) fusion(f32[512,128]{1,0:T(8,128)S(1)} %get-tuple-element.35, f32[512,4]{1,0:T(8,128)} %copy.66, f32[512,128]{1,0:T(8,128)S(1)} %get-tuple-element.36, f32[512,4]{1,0:T(8,128)S(1)} %copy.65), kind=kLoop, calls=%fused_computation.27 | loop fusion | flops 2359296 | bytes 1589248 | tf_op jit(solution)/shard_map/convert.3
  25.1 0.7 broadcast_compare_fusion.2
  25.8 0.2 neg.22
  26.0 0.0 copy-start.11
  26.0 0.0 copy-start.8
  26.0 0.0 copy-start.10
  26.0 1.3 %sub.154 = bf16[1,16,32,512]{3,2,0,1:T(8,128)(2,1)S(1)} reshape(bf16[512,4,128]{2,1,0:T(4,128)(2,1)} %get-tuple-element.9) | data formatting | bytes 1048576 | tf_op jit(solution)/shard_map/sub | solution.py:29
  27.3 0.1 copy.64
  27.4 0.1 copy.69
  27.6 0.1 copy.70
  27.7 0.1 copy.71
  27.9 1.1 pad_maximum_fusion
  29.0 0.0 copy-done.8
  29.0 0.1 iota_add_fusion
  29.1 0.1 subtract_multiply_fusion.1
  29.1 0.1 subtract_multiply_fusion
  29.2 2.6 %subtract_convert_fusion.1 = bf16[16,8,8,4,256]{4,2,1,0,3:T(8,128)(2,1)} fusion(s32[8,8,256]{2,1,0:T(8,128)S(1)} %get-tuple-element.12, s32[16,4,256]{2,0,1:T(8,128)S(1)} %get-tuple-element.14, s32[8,8,256]{2,1,0:T(8,128)S(1)} %get-tuple-element.11, s32[16,4,256]{2,0,1:T(8,128)S(1)} %get-tuple-element.13), kind=kLoop, calls=%fused_computation.4 | loop fusion | flops 8388608 | bytes 2359296 | tf_op jit(solution)/shard_map/convert_element_type | solution.py:107
  31.9 11.1 %all-to-all-done = bf16[64,64,256]{2,0,1:T(8,128)(2,1)S(1)} async-done(((bf16[64,64,256]{2,0,1:T(8,128)(2,1)}), bf16[64,64,256]{2,0,1:T(8,128)(2,1)S(1)}, u32[]{:S(2)}, u32[]{:S(2)}) %all-to-all-start) | async-done | bytes 2097184 | tf_op jit(solution)/shard_map/all_to_all | solution.py:64
  43.0 1.3 %copy.68 = bf16[64,8,8,256]{3,2,0,1:T(8,128)(2,1)S(1)} copy(bf16[64,8,8,256]{3,0,2,1:T(8,128)(2,1)S(1)} %bitcast.111) | data formatting | bytes 4194304 | tf_op jit(solution)/shard_map/all_to_all | solution.py:64
  44.2 0.7 copy.90
  44.9 0.5 copy-done.5
  45.4 4.3 %convolution_convert_fusion = bf16[1024,2048]{1,0:T(8,128)(2,1)} fusion(bf16[1024,512]{1,0:T(8,128)(2,1)S(1)} %bitcast.116, bf16[512,2048]{1,0:T(8,128)(2,1)S(1)} %bitcast.114), kind=kOutput, calls=%fused_computation.7 | convolution fusion | flops 2149580800 | bytes 7340032 | tf_op jit(solution)/shard_map/dot_general | solution.py:73
  49.8 7.5 %reshape.451 = bf16[16,512,256]{2,1,0:T(8,128)(2,1)} reshape(bf16[1024,2048]{1,0:T(8,128)(2,1)} %convolution_convert_fusion) | data formatting | bytes 8388608 | tf_op jit(solution)/shard_map/reshape | solution.py:78
  57.3 3.7 %fusion.13 = f32[16,64,512]{2,1,0:T(8,128)S(1)} fusion(bf16[16,512,256]{2,1,0:T(8,128)(2,1)} %reshape.451, bf16[16,8,8,4,256]{4,2,1,0,3:T(8,128)(2,1)S(1)} %copy-done.2), kind=kOutput, calls=%fused_computation.36 | convolution fusion | flops 268435456 | bytes 6815744 | tf_op jit(solution)/shard_map/axp,anp->axn/dot_general | solution.py:114
  61.0 0.0 copy-done.1
  61.0 1.4 %fusion.14 = f32[16,64,512]{2,1,0:T(8,128)S(1)} fusion(bf16[16,512,256]{2,1,0:T(8,128)(2,1)S(1)} %copy-done.1, bf16[16,8,8,4,256]{4,2,1,0,3:T(8,128)(2,1)S(1)} %copy-done.2), kind=kOutput, calls=%fused_computation.38 | convolution fusion | flops 268435456 | bytes 6815744 | tf_op jit(solution)/shard_map/axp,anp->axn/dot_general | solution.py:114
  62.4 1.4 %fusion.15 = f32[16,64,512]{2,1,0:T(8,128)S(1)} fusion(bf16[16,512,256]{2,1,0:T(8,128)(2,1)S(1)} %copy-done.1, bf16[16,8,8,4,256]{4,2,1,0,3:T(8,128)(2,1)S(1)} %copy-done.2), kind=kOutput, calls=%fused_computation.40 | convolution fusion | flops 268435456 | bytes 6815744 | tf_op jit(solution)/shard_map/axp,anp->axn/dot_general | solution.py:114
  63.8 2.4 %add_convert_fusion = bf16[16,64,512]{2,1,0:T(8,128)(2,1)} fusion(f32[16,64,512]{2,1,0:T(8,128)S(1)} %fusion.13, f32[16,64,512]{2,1,0:T(8,128)S(1)} %fusion.14, f32[16,64,512]{2,1,0:T(8,128)S(1)} %fusion.15, bf16[16,512,256]{2,1,0:T(8,128)(2,1)S(1)} %copy-done.1, pred[16,512]{1,0:T(8,128)(4,1)S(1)} %copy.71, pred[16,512]{1,0:T(8,128)(4,1)S(1)} %copy.70, ...), kind=kOutput, calls=%fused_computation.10 | convolution fusion | flops 272629760 | bytes 12091392 | tf_op jit(solution)/shard_map/axp,anp->axn/dot_general | solution.py:114
  66.2 8.6 %all-to-all-start.1 = ((bf16[128,8,512]{2,1,0:T(8,128)(2,1)}), bf16[128,8,512]{2,1,0:T(8,128)(2,1)S(1)}, u32[]{:S(2)}, u32[]{:S(2)}) async-start(bf16[128,8,512]{2,1,0:T(8,128)(2,1)} %bitcast.15), calls=%async_computation.1 | async-start | bytes 2097152 | tf_op jit(solution)/shard_map/all_to_all | solution.py:124
  74.8 1.0 fusion.38
  75.8 1.0 maximum_maximum_fusion.1
  76.9 0.1 fusion.64
  76.9 2.9 %fusion.25 = (f32[128,1024]{0,1:T(8,128)S(1)}, f32[128,1024]{0,1:T(8,128)S(1)}, f32[128,1024]{0,1:T(8,128)}) fusion(s32[128]{0:T(128)S(1)} %copy-done.7), kind=kLoop, calls=%fused_computation.59 | loop fusion | flops 1966080 | bytes 1573376 | tf_op jit(solution)/shard_map/sin | solution.py:16
  79.9 14.1 %all-to-all-done.1 = bf16[128,8,512]{2,1,0:T(8,128)(2,1)S(1)} async-done(((bf16[128,8,512]{2,1,0:T(8,128)(2,1)}), bf16[128,8,512]{2,1,0:T(8,128)(2,1)S(1)}, u32[]{:S(2)}, u32[]{:S(2)}) %all-to-all-start.1) | async-done | bytes 1048608 | tf_op jit(solution)/shard_map/all_to_all | solution.py:124
  94.0 1.0 copy.85
  95.0 1.8 %fusion.69 = f32[8,2,32,8,2,128]{5,3,4,2,1,0:T(8,128)S(1)} fusion(bf16[8,2,32,8,128,1]{4,3,5,2,1,0:T(8,128)(2,1)S(1)} %bitcast.113, f32[2,128,128,1,1,1]{2,1,0,5,4,3:T(8,128)S(1)} %bitcast.117), kind=kOutput, calls=%fused_computation.153 | convolution fusion | flops 1610612736 | bytes 5373952 | tf_op jit(solution)/shard_map/dot_general | solution.py:131
  96.8 0.8 add_reduce_fusion
  97.6 0.2 copy-done.4
  97.8 0.6 fusion.5
  98.4 0.7 copy.75
  99.1 3.5 %all-to-all-start.2 = ((bf16[16,2,32,128]{3,2,1,0:T(8,128)(2,1)}), bf16[16,2,32,128]{3,2,1,0:T(8,128)(2,1)S(1)}, u32[]{:S(2)}, u32[]{:S(2)}) async-start(bf16[16,2,32,128]{3,2,1,0:T(8,128)(2,1)} %copy.75), calls=%async_computation.2 | async-start | bytes 524288 | tf_op jit(solution)/shard_map/all_to_all | solution.py:167
  102.6 1.2 maximum_maximum_fusion
  103.8 8.1 %all-to-all-done.2 = bf16[16,2,32,128]{3,2,1,0:T(8,128)(2,1)S(1)} async-done(((bf16[16,2,32,128]{3,2,1,0:T(8,128)(2,1)}), bf16[16,2,32,128]{3,2,1,0:T(8,128)(2,1)S(1)}, u32[]{:S(2)}, u32[]{:S(2)}) %all-to-all-start.2) | async-done | bytes 262176 | tf_op jit(solution)/shard_map/all_to_all | solution.py:167
  112.1 2.0 %fusion.6 = bf16[8,32,2,128]{3,1,0,2:T(8,128)(2,1)S(1)} fusion(f32[2,8,128,256]{3,2,1,0:T(8,128)S(1)} %bitcast.110, f32[32,256,1,1]{1,0,2,3:T(8,128)S(1)} %reshape.459), kind=kOutput, calls=%fused_computation.16 | convolution fusion | flops 201392128 | bytes 2260992 | tf_op jit(solution)/shard_map/dot_general | solution.py:181
  114.1 9.0 %all_to_all.30 = bf16[8,32,2,128]{3,1,2,0:T(8,128)(2,1)S(1)} all-to-all(bf16[8,32,2,128]{3,1,2,0:T(8,128)(2,1)S(1)} %copy.78), channel_id=1, replica_groups=mesh['srow'=8,'scol'=16] {'srow'}, dimensions={0} | all-to-all | bytes 262144 | tf_op jit(solution)/shard_map/all_to_all | solution.py:183
  123.1 0.6 copy.80
  (35 shorter events, 0.3 us)
Async XLA Ops:
  0.0 2.4 %copy-start = (f32[16,256]{1,0:T(8,128)S(1)}, f32[16,256]{1,0:T(8,128)}, u32[]{:S(2)}) copy-start(f32[16,256]{1,0:T(8,128)} %param.10) | copy-start | bytes 49156
  0.0 2.4 %copy-start.3 = (bf16[64,64,256]{2,1,0:T(8,128)(2,1)S(1)}, bf16[64,64,256]{2,1,0:T(8,128)(2,1)}, u32[]{:S(2)}) copy-start(bf16[64,64,256]{2,1,0:T(8,128)(2,1)} %param.8) | copy-start | bytes 6291460
  0.0 2.4 %copy-start.13 = (f32[256]{0:T(256)S(1)}, f32[256]{0:T(256)}, u32[]{:S(2)}) copy-start(f32[256]{0:T(256)} %param.9) | copy-start | bytes 3076
  10.3 8.8 %copy-start.9 = (s32[8]{0:T(128)S(1)}, s32[8]{0:T(128)}, u32[]{:S(2)}) copy-start(s32[8]{0:T(128)} %constant.185.clone) | copy-start | bytes 100
  10.3 32.6 %all-to-all-start = ((bf16[64,64,256]{2,0,1:T(8,128)(2,1)}), bf16[64,64,256]{2,0,1:T(8,128)(2,1)S(1)}, u32[]{:S(2)}, u32[]{:S(2)}) async-start(bf16[64,64,256]{2,0,1:T(8,128)(2,1)} %copy.67), calls=%async_computation | async-start | bytes 4194304 | tf_op jit(solution)/shard_map/all_to_all | solution.py:64
  20.9 0.5 copy-start.6
  26.0 3.0 %copy-start.11 = (s32[16]{0:T(128)S(1)}, s32[16]{0:T(128)}, u32[]{:S(2)}) copy-start(s32[16]{0:T(128)} %constant.184.clone) | copy-start | bytes 196
  26.0 3.0 %copy-start.8 = (s32[256]{0:T(256)S(1)}, s32[256]{0:T(256)}, u32[]{:S(2)}) copy-start(s32[256]{0:T(256)} %param.11) | copy-start | bytes 3076
  26.0 3.0 %copy-start.10 = (s32[8]{0:T(128)S(1)}, s32[8]{0:T(128)}, u32[]{:S(2)}) copy-start(s32[8]{0:T(128)} %constant.185.clone) | copy-start | bytes 100
  44.2 1.2 copy-start.5
  49.8 7.6 %copy-start.2 = (bf16[16,8,8,4,256]{4,2,1,0,3:T(8,128)(2,1)S(1)}, bf16[16,8,8,4,256]{4,2,1,0,3:T(8,128)(2,1)}, u32[]{:S(2)}) copy-start(bf16[16,8,8,4,256]{4,2,1,0,3:T(8,128)(2,1)} %subtract_convert_fusion.1) | copy-start | bytes 6291460
  57.3 3.7 %copy-start.1 = (bf16[16,512,256]{2,1,0:T(8,128)(2,1)S(1)}, bf16[16,512,256]{2,1,0:T(8,128)(2,1)}, u32[]{:S(2)}) copy-start(bf16[16,512,256]{2,1,0:T(8,128)(2,1)} %reshape.451) | copy-start | bytes 12582916
  66.2 10.7 %copy-start.12 = (s32[128]{0:T(128)S(1)}, s32[128]{0:T(128)}, u32[]{:S(2)}) copy-start(s32[128]{0:T(128)} %get-tuple-element.33) | copy-start | bytes 1540
  66.2 10.7 %copy-start.7 = (s32[128]{0:T(128)S(1)}, s32[128]{0:T(128)}, u32[]{:S(2)}) copy-start(s32[128]{0:T(128)} %copy-done.6) | copy-start | bytes 1540
  66.2 27.8 %all-to-all-start.1 = ((bf16[128,8,512]{2,1,0:T(8,128)(2,1)}), bf16[128,8,512]{2,1,0:T(8,128)(2,1)S(1)}, u32[]{:S(2)}, u32[]{:S(2)}) async-start(bf16[128,8,512]{2,1,0:T(8,128)(2,1)} %bitcast.15), calls=%async_computation.1 | async-start | bytes 2097152 | tf_op jit(solution)/shard_map/all_to_all | solution.py:124
  96.8 1.0 copy-start.4
  99.1 12.9 %all-to-all-start.2 = ((bf16[16,2,32,128]{3,2,1,0:T(8,128)(2,1)}), bf16[16,2,32,128]{3,2,1,0:T(8,128)(2,1)S(1)}, u32[]{:S(2)}, u32[]{:S(2)}) async-start(bf16[16,2,32,128]{3,2,1,0:T(8,128)(2,1)} %copy.75), calls=%async_computation.2 | async-start | bytes 524288 | tf_op jit(solution)/shard_map/all_to_all | solution.py:167

commit v4 on v3

--- a/solution.py
+++ b/solution.py
@@ -61,14 +61,24 @@
     fitted = jnp.einsum("rce,ep->rcp", fit_weights, eigen_flats, precision=lax.Precision.HIGH)
     flattened = (scaled - fitted).astype(jnp.bfloat16)
 
-    gathered = lax.all_to_all(flattened, "srow", split_axis=1, concat_axis=0, tiled=True)
-    cols_here = gathered.shape[1]
+    cols_here = local_cols // n_srow
+    me = lax.axis_index("srow")
+    blocks = [lax.dynamic_slice_in_dim(flattened, me * cols_here, cols_here, axis=1)]
+    for shift in range(1, n_srow):
+        dest = (me + shift) % n_srow
+        chunk = lax.dynamic_slice_in_dim(flattened, dest * cols_here, cols_here, axis=1)
+        perm = [(i, (i + shift) % n_srow) for i in range(n_srow)]
+        blocks.append(lax.ppermute(chunk, "srow", perm))
+    gathered = jnp.concatenate(blocks, axis=0)
 
     k_blk = row_count // n_scol
     j_blk = col_count // n_srow
     row_ids = jnp.arange(row_count, dtype=jnp.int32)
     row_cos, row_sin = square_waves(row_count)
-    forward_rows = jnp.stack([row_cos, -row_sin], axis=0).reshape(2, n_scol, k_blk, row_count)
+    src_rows = ((me - jnp.arange(n_srow, dtype=jnp.int32)) % n_srow)[:, None] * local_rows
+    src_rows = (src_rows + jnp.arange(local_rows, dtype=jnp.int32)[None, :]).reshape(row_count)
+    shifted_cos, shifted_sin = waves(row_ids, src_rows, row_count)
+    forward_rows = jnp.stack([shifted_cos, -shifted_sin], axis=0).reshape(2, n_scol, k_blk, row_count)
     forward_rows = forward_rows.transpose(1, 0, 2, 3).reshape(2 * row_count, row_count)
     spec = jnp.dot(
         forward_rows.astype(jnp.bfloat16),

time: 125 us -> 143 us (1.14)
  local copies, waits for them, and re-layouts: 19 us -> 40.9 us
  waiting for transfers between devices: 33.3 us -> 23.7 us
  starting transfers between devices: 18.7 us -> 26.4 us
  other arithmetic: 20.4 us -> 18.4 us
    ppermute x0 -> x7, starting transfers between devices: none -> 12.9 us  [on_device(): blocks.append(lax.ppermute(chunk, 'srow', perm))]
    eq x4 -> x8, local copies, waits for them, and re-layouts: 0.45 us -> 11.5 us  [on_device(): part = jnp.where(dx_of_n == d, part, 0.0)]
    all_to_all x1 -> x0, waiting for transfers between devices: 11.1 us -> none  [on_device(): lax.all_to_all(flattened, 'srow', split_axis=1, concat_axis=0, tiled=True)]
    unnamed x29 -> x43, local copies, waits for them, and re-layouts: 1.64 us -> 11.6 us
    all_to_all x1 -> x0, starting transfers between devices: 6.58 us -> none  [on_device(): lax.all_to_all(flattened, 'srow', split_axis=1, concat_axis=0, tiled=True)]
    broadcast_in_dim x4, local copies, waits for them, and re-layouts: 0.1 us -> 5.29 us  [on_device(): jnp.broadcast_to(own_dx[:, None, :, None], (n_scol, 2, k_blk, cols_here))]
    convert_element_type x1 -> x0, local copies, waits for them, and re-layouts: 2.52 us -> none  [on_device(): flattened = (scaled - fitted).astype(jnp.bfloat16)]
    ppermute x0 -> x7, waiting for transfers between devices: none -> 1.7 us  [on_device(): blocks.append(lax.ppermute(chunk, 'srow', perm))]
  transfers between devices with their start and end apart: 3 -> 9, of which waited for: 3 -> 3; matrix products, arithmetic and copies ran while one was open for 17% -> 29% of each run, Pallas kernels for 0% -> 0%
where the time goes in v4:
time: 143 us; the launch traced here: 142 us
  local copies, waits for them, and re-layouts  40.9 us (29%)
  starting transfers between devices  26.4 us (18%)
  waiting for transfers between devices  23.7 us (17%)
  matrix products  22.9 us (16%)
  other arithmetic  18.4 us (13%)
  blocking collectives  8.97 us (6%)
    all_to_all x1, waiting for transfers between devices, on_device(): lax.all_to_all(summed, ('scol', 'srow'), split_axis=0, concat_axis=0, til...  13.9 us
    ppermute x7, starting transfers between devices, on_device(): blocks.append(lax.ppermute(chunk, 'srow', perm))  12.9 us
    unnamed x43, local copies, waits for them, and re-layouts  11.6 us
    eq x8, local copies, waits for them, and re-layouts, on_device(): part = jnp.where(dx_of_n == d, part, 0.0)  11.5 us
    all_to_all x1, starting transfers between devices, on_device(): lax.all_to_all(summed, ('scol', 'srow'), split_axis=0, concat_axis=0, til...  10 us
    all_to_all x1, blocking collectives, on_device(): lax.all_to_all(image.astype(jnp.bfloat16), 'srow', split_axis=0, concat_a...  8.97 us
    dot_general x4, matrix products, on_device(): jnp.einsum('axp,anp->axn', weight[:, :, :, d].reshape(n_scol, n_srow * n_...  8.88 us
    all_to_all x1, waiting for transfers between devices, on_device(): lax.all_to_all(half.astype(jnp.bfloat16), 'scol', split_axis=0, concat_ax...  8.13 us
  transfers between devices with their start and end apart: 9, of which 3 were waited for; matrix products, arithmetic and copies ran while one was open for 29% of the time, Pallas kernels for 0%

profile of v4, /device:TPU:0, one launch (start us, length us, event | category | flops | bytes accessed | tf_op | source)
XLA Modules:
  0.0 141.8 jit_solution(1407804734350759559)
XLA Ops:
  0.0 2.4 %convert_reduce_fusion = f32[64,64]{1,0:T(8,128)S(1)} fusion(bf16[64,64,256]{2,1,0:T(8,128)(2,1)} %param.8), kind=kLoop, calls=%fused_computation | loop fusion | flops 2093056 | bytes 2113536 | tf_op jit(solution)/shard_map/reduce_sum | solution.py:58
  2.4 2.6 %fusion.1 = f32[64,64,16]{1,2,0:T(8,128)S(1)} fusion(bf16[64,64,256]{2,1,0:T(8,128)(2,1)S(1)} %copy-done.2, f32[64,64]{1,0:T(8,128)S(1)} %broadcast_multiply_fusion.1, f32[256]{0:T(256)S(1)} %copy-done.17, f32[16,256]{1,0:T(8,128)S(1)} %copy-done), kind=kOutput, calls=%fused_computation.8 | convolution fusion | flops 103809024 | bytes 2393088 | tf_op jit(solution)/shard_map/rcp,ep->rce/dot_general | solution.py:60
  5.1 2.8 %subtract_convert_fusion = bf16[64,64,256]{2,1,0:T(8,128)(2,1)S(1)} fusion(bf16[64,64,256]{2,1,0:T(8,128)(2,1)S(1)} %copy-done.3, f32[64,64,16]{1,2,0:T(8,128)S(1)} %fusion.1, f32[64,64]{1,0:T(8,128)S(1)} %broadcast_multiply_fusion.1, f32[256]{0:T(256)S(1)} %copy-done.17, f32[16,256]{1,0:T(8,128)S(1)} %copy-done), kind=kOutput, calls=%fused_computation.3 | convolution fusion | flops 105906176 | bytes 4490240 | tf_op jit(solution)/shard_map/rce,ep->rcp/dot_general | solution.py:61
  7.9 1.3 constant_dynamic-slice_fusion
  9.2 2.1 %collective-permute-start = (bf16[64,8,256]{2,1,0:T(8,128)(2,1)}, bf16[64,8,256]{2,1,0:T(8,128)(2,1)}, u32[]{:S(2)}, u32[]{:S(2)}) collective-permute-start(bf16[64,8,256]{2,1,0:T(8,128)(2,1)} %get-tuple-element.15), channel_id=1, source_target_pairs={{0,16},{16,32},{32,48},{48,64},{64,80},{80,96},{96,112},{112,0},{1... | collective-permute-start | bytes 786440 | tf_op jit(solution)/shard_map/ppermute | solution.py:71
  11.3 3.6 %collective-permute-start.1 = (bf16[64,8,256]{2,1,0:T(8,128)(2,1)}, bf16[64,8,256]{2,1,0:T(8,128)(2,1)}, u32[]{:S(2)}, u32[]{:S(2)}) collective-permute-start(bf16[64,8,256]{2,1,0:T(8,128)(2,1)} %get-tuple-element.14), channel_id=1, source_target_pairs={{0,32},{16,48},{32,64},{48,80},{64,96},{80,112},{96,0},{112,16},{1... | collective-permute-start | bytes 786440 | tf_op jit(solution)/shard_map/ppermute | solution.py:71
  14.9 2.0 %collective-permute-start.2 = (bf16[64,8,256]{2,1,0:T(8,128)(2,1)}, bf16[64,8,256]{2,1,0:T(8,128)(2,1)}, u32[]{:S(2)}, u32[]{:S(2)}) collective-permute-start(bf16[64,8,256]{2,1,0:T(8,128)(2,1)} %get-tuple-element.13), channel_id=1, source_target_pairs={{0,48},{16,64},{32,80},{48,96},{64,112},{80,0},{96,16},{112,32},{1... | collective-permute-start | bytes 786440 | tf_op jit(solution)/shard_map/ppermute | solution.py:71
  16.9 0.4 collective-permute-start.3
  17.4 2.0 %collective-permute-start.4 = (bf16[64,8,256]{2,1,0:T(8,128)(2,1)}, bf16[64,8,256]{2,1,0:T(8,128)(2,1)}, u32[]{:S(2)}, u32[]{:S(2)}) collective-permute-start(bf16[64,8,256]{2,1,0:T(8,128)(2,1)} %get-tuple-element.11), channel_id=1, source_target_pairs={{0,80},{16,96},{32,112},{48,0},{64,16},{80,32},{96,48},{112,64},{1... | collective-permute-start | bytes 786440 | tf_op jit(solution)/shard_map/ppermute | solution.py:71
  19.5 0.1 add.387
  19.7 0.7 broadcast_compare_fusion.2
  20.4 0.6 dynamic_slice.27
  21.0 4.6 %cosine_convert_fusion = (bf16[1,16,32,512]{3,2,0,1:T(8,128)(2,1)S(1)}, bf16[1,16,32,512]{3,2,0,1:T(8,128)(2,1)S(1)}) fusion(s32[512]{0:T(512)S(1)} %add.387, s32[16,32]{1,0:T(8,128)S(1)} %multiply_add_fusion), kind=kLoop, calls=%fused_computation.35 | loop fusion | flops 4456448 | bytes 1052672 | tf_op jit(solution)/shard_map/convert
  25.7 1.2 fusion.59
  26.9 0.3 fusion.39
  27.2 1.2 subtract_convert_fusion.1
  28.4 0.1 pad_maximum_fusion
  28.5 0.6 iota_add_fusion.4
  29.1 1.3 copy.56
  30.5 1.3 broadcast_in_dim.86
  31.8 1.5 %copy.57 = pred[16,512]{1,0:T(8,128)(4,1)} copy(pred[16,512]{0,1:T(8,128)(4,1)} %bitcast.114) | data formatting | bytes 16384 | tf_op jit(solution)/shard_map/eq | solution.py:130
  33.3 1.3 copy.58
  34.7 1.3 broadcast_in_dim.89
  36.0 1.5 %copy.59 = pred[16,512]{1,0:T(8,128)(4,1)} copy(pred[16,512]{0,1:T(8,128)(4,1)} %bitcast.115) | data formatting | bytes 16384 | tf_op jit(solution)/shard_map/eq | solution.py:130
  37.5 1.3 copy.60
  38.9 1.3 broadcast_in_dim.91
  40.2 1.5 %copy.61 = pred[16,512]{1,0:T(8,128)(4,1)} copy(pred[16,512]{0,1:T(8,128)(4,1)} %bitcast.116) | data formatting | bytes 16384 | tf_op jit(solution)/shard_map/eq | solution.py:130
  41.8 1.4 copy.62
  43.1 1.3 broadcast_in_dim.93
  44.4 1.5 %copy.63 = pred[16,512]{1,0:T(8,128)(4,1)} copy(pred[16,512]{0,1:T(8,128)(4,1)} %bitcast.117) | data formatting | bytes 16384 | tf_op jit(solution)/shard_map/eq | solution.py:130
  46.0 0.8 collective-permute-start.5
  46.8 1.7 %constant_dynamic-update-slice_fusion.6 = bf16[512,8,256]{2,1,0:T(8,128)(2,1)} fusion(bf16[512,8,256]{2,1,0:T(8,128)(2,1)} %get-tuple-element.16, bf16[64,8,256]{2,1,0:T(8,128)(2,1)} %collective-permute-done), kind=kLoop, calls=%fused_computation.97 | loop fusion | bytes 524288
  48.5 1.8 %collective-permute-start.6 = (bf16[64,8,256]{2,1,0:T(8,128)(2,1)S(1)}, bf16[64,8,256]{2,1,0:T(8,128)(2,1)S(1)}, u32[]{:S(2)}, u32[]{:S(2)}) collective-permute-start(bf16[64,8,256]{2,1,0:T(8,128)(2,1)S(1)} %get-tuple-element.9), channel_id=1, source_target_pairs={{0,112},{16,0},{32,16},{48,32},{64,48},{80,64},{96,80},{112,96},{1... | collective-permute-start | bytes 786440 | tf_op jit(solution)/shard_map/ppermute | solution.py:71
  50.3 1.7 %constant_dynamic-update-slice_fusion.5 = bf16[512,8,256]{2,1,0:T(8,128)(2,1)} fusion(bf16[512,8,256]{2,1,0:T(8,128)(2,1)} %constant_dynamic-update-slice_fusion.6, bf16[64,8,256]{2,1,0:T(8,128)(2,1)} %collective-permute-done.1), kind=kLoop, calls=%fused_computation.96 | loop fusion | bytes 524288
  52.0 1.7 %constant_dynamic-update-slice_fusion.4 = bf16[512,8,256]{2,1,0:T(8,128)(2,1)} fusion(bf16[512,8,256]{2,1,0:T(8,128)(2,1)} %constant_dynamic-update-slice_fusion.5, bf16[64,8,256]{2,1,0:T(8,128)(2,1)} %collective-permute-done.2), kind=kLoop, calls=%fused_computation.95 | loop fusion | bytes 524288
  53.7 1.7 %constant_dynamic-update-slice_fusion.3 = bf16[512,8,256]{2,1,0:T(8,128)(2,1)} fusion(bf16[512,8,256]{2,1,0:T(8,128)(2,1)} %constant_dynamic-update-slice_fusion.4, bf16[64,8,256]{2,1,0:T(8,128)(2,1)} %collective-permute-done.3), kind=kLoop, calls=%fused_computation.94 | loop fusion | bytes 524288
  55.3 1.7 %constant_dynamic-update-slice_fusion.2 = bf16[512,8,256]{2,1,0:T(8,128)(2,1)} fusion(bf16[512,8,256]{2,1,0:T(8,128)(2,1)} %constant_dynamic-update-slice_fusion.3, bf16[64,8,256]{2,1,0:T(8,128)(2,1)} %collective-permute-done.4), kind=kLoop, calls=%fused_computation.93 | loop fusion | bytes 524288
  57.0 0.7 constant_dynamic-update-slice_fusion.1
  57.7 1.7 %collective-permute-done.6 = bf16[64,8,256]{2,1,0:T(8,128)(2,1)S(1)} collective-permute-done((bf16[64,8,256]{2,1,0:T(8,128)(2,1)S(1)}, bf16[64,8,256]{2,1,0:T(8,128)(2,1)S(1)}, u32[]{:S(2)}, u32[]{:S(2)}) %collective-permute-start.6) | collective-permute-done | bytes 262176 | tf_op jit(solution)/shard_map/ppermute | solution.py:71
  59.4 0.7 constant_dynamic-update-slice_fusion
  60.1 2.3 %copy.82 = bf16[64,8,8,256]{3,1,2,0:T(8,128)(2,1)S(1)} copy(bf16[64,8,8,256]{3,2,1,0:T(8,128)(2,1)} %bitcast.109) | data formatting | bytes 4194304
  62.4 4.3 %convolution_convert_fusion = bf16[1024,2048]{1,0:T(8,128)(2,1)} fusion(bf16[1024,512]{1,0:T(8,128)(2,1)S(1)} %bitcast.112, bf16[512,2048]{1,0:T(8,128)(2,1)S(1)} %bitcast.110), kind=kOutput, calls=%fused_computation.7 | convolution fusion | flops 2149580800 | bytes 7340032 | tf_op jit(solution)/shard_map/dot_general | solution.py:83
  66.7 7.4 %reshape.416 = bf16[16,512,256]{2,1,0:T(8,128)(2,1)} reshape(bf16[1024,2048]{1,0:T(8,128)(2,1)} %convolution_convert_fusion) | data formatting | bytes 8388608 | tf_op jit(solution)/shard_map/reshape | solution.py:88
  74.1 3.7 %fusion.17 = f32[16,64,512]{2,1,0:T(8,128)S(1)} fusion(bf16[16,512,256]{2,1,0:T(8,128)(2,1)} %reshape.416, bf16[16,8,8,4,256]{4,2,1,0,3:T(8,128)(2,1)S(1)} %subtract_convert_fusion.1), kind=kOutput, calls=%fused_computation.46 | convolution fusion | flops 268435456 | bytes 6815744 | tf_op jit(solution)/shard_map/axp,anp->axn/dot_general | solution.py:124
  77.8 1.4 fusion.18
  79.2 1.4 fusion.16
  80.7 2.4 %add_convert_fusion = bf16[16,64,512]{2,1,0:T(8,128)(2,1)} fusion(f32[16,64,512]{2,1,0:T(8,128)S(1)} %fusion.16, f32[16,64,512]{2,1,0:T(8,128)S(1)} %fusion.17, f32[16,64,512]{2,1,0:T(8,128)S(1)} %fusion.18, bf16[16,512,256]{2,1,0:T(8,128)(2,1)S(1)} %copy-done.1, pred[16,512]{1,0:T(8,128)(4,1)S(1)} %copy-done.8, pred[16,512]{1,0:T(8,128)(4,1)S(1)} %copy-done.7, ...), kind=kOutput, calls=%fused_computation.10 | convolution fusion | flops 272629760 | bytes 12091392 | tf_op jit(solution)/shard_map/axp,anp->axn/dot_general | solution.py:124
  83.1 10.0 %all-to-all-start = ((bf16[128,8,512]{2,1,0:T(8,128)(2,1)}), bf16[128,8,512]{2,1,0:T(8,128)(2,1)S(1)}, u32[]{:S(2)}, u32[]{:S(2)}) async-start(bf16[128,8,512]{2,1,0:T(8,128)(2,1)} %bitcast.13), calls=%async_computation | async-start | bytes 2097152 | tf_op jit(solution)/shard_map/all_to_all | solution.py:134
  93.1 1.0 fusion.33
  94.2 1.0 maximum_maximum_fusion.1
  95.2 2.9 %fusion.25 = (f32[128,1024]{0,1:T(8,128)S(1)}, f32[128,1024]{0,1:T(8,128)S(1)}, f32[128,1024]{0,1:T(8,128)}) fusion(s32[128]{0:T(128)S(1)} %copy-done.10), kind=kLoop, calls=%fused_computation.61 | loop fusion | flops 1966080 | bytes 1573376 | tf_op jit(solution)/shard_map/sin | solution.py:16
  98.2 13.9 %all-to-all-done = bf16[128,8,512]{2,1,0:T(8,128)(2,1)S(1)} async-done(((bf16[128,8,512]{2,1,0:T(8,128)(2,1)}), bf16[128,8,512]{2,1,0:T(8,128)(2,1)S(1)}, u32[]{:S(2)}, u32[]{:S(2)}) %all-to-all-start) | async-done | bytes 1048608 | tf_op jit(solution)/shard_map/all_to_all | solution.py:134
  112.1 1.0 copy.77
  113.0 1.8 %fusion.60 = f32[8,2,32,8,2,128]{5,3,4,2,1,0:T(8,128)S(1)} fusion(bf16[8,2,32,8,128,1]{4,3,5,2,1,0:T(8,128)(2,1)S(1)} %bitcast.108, f32[2,128,128,1,1,1]{2,1,0,5,4,3:T(8,128)S(1)} %bitcast.113), kind=kOutput, calls=%fused_computation.162 | convolution fusion | flops 1610612736 | bytes 5373952 | tf_op jit(solution)/shard_map/dot_general | solution.py:141
  114.9 0.8 add_reduce_fusion
  115.7 0.2 copy-done.4
  115.9 0.6 fusion.5
  116.5 0.7 copy.67
  117.2 3.5 %all-to-all-start.1 = ((bf16[16,2,32,128]{3,2,1,0:T(8,128)(2,1)}), bf16[16,2,32,128]{3,2,1,0:T(8,128)(2,1)S(1)}, u32[]{:S(2)}, u32[]{:S(2)}) async-start(bf16[16,2,32,128]{3,2,1,0:T(8,128)(2,1)} %copy.67), calls=%async_computation.1 | async-start | bytes 524288 | tf_op jit(solution)/shard_map/all_to_all | solution.py:177
  120.7 1.2 maximum_maximum_fusion
  121.9 8.1 %all-to-all-done.1 = bf16[16,2,32,128]{3,2,1,0:T(8,128)(2,1)S(1)} async-done(((bf16[16,2,32,128]{3,2,1,0:T(8,128)(2,1)}), bf16[16,2,32,128]{3,2,1,0:T(8,128)(2,1)S(1)}, u32[]{:S(2)}, u32[]{:S(2)}) %all-to-all-start.1) | async-done | bytes 262176 | tf_op jit(solution)/shard_map/all_to_all | solution.py:177
  130.2 2.0 %fusion.6 = bf16[8,32,2,128]{3,1,0,2:T(8,128)(2,1)S(1)} fusion(f32[2,8,128,256]{3,2,1,0:T(8,128)S(1)} %bitcast.107, f32[32,256,1,1]{1,0,2,3:T(8,128)S(1)} %reshape.424), kind=kOutput, calls=%fused_computation.21 | convolution fusion | flops 201392128 | bytes 2260992 | tf_op jit(solution)/shard_map/dot_general | solution.py:191
  132.2 9.0 %all_to_all.15 = bf16[8,32,2,128]{3,1,2,0:T(8,128)(2,1)S(1)} all-to-all(bf16[8,32,2,128]{3,1,2,0:T(8,128)(2,1)S(1)} %copy.70), channel_id=1, replica_groups=mesh['srow'=8,'scol'=16] {'srow'}, dimensions={0} | all-to-all | bytes 262144 | tf_op jit(solution)/shard_map/all_to_all | solution.py:193
  141.2 0.6 copy.72
  (62 shorter events, 0.7 us)
Async XLA Ops:
  0.0 2.4 %copy-start = (f32[16,256]{1,0:T(8,128)S(1)}, f32[16,256]{1,0:T(8,128)}, u32[]{:S(2)}) copy-start(f32[16,256]{1,0:T(8,128)} %param.10) | copy-start | bytes 49156
  0.0 2.4 %copy-start.2 = (bf16[64,64,256]{2,1,0:T(8,128)(2,1)S(1)}, bf16[64,64,256]{2,1,0:T(8,128)(2,1)}, u32[]{:S(2)}) copy-start(bf16[64,64,256]{2,1,0:T(8,128)(2,1)} %param.8) | copy-start | bytes 6291460
  0.0 2.4 %copy-start.17 = (f32[256]{0:T(256)S(1)}, f32[256]{0:T(256)}, u32[]{:S(2)}) copy-start(f32[256]{0:T(256)} %param.9) | copy-start | bytes 3076
  2.4 2.6 %copy-start.3 = (bf16[64,64,256]{2,1,0:T(8,128)(2,1)S(1)}, bf16[64,64,256]{2,1,0:T(8,128)(2,1)}, u32[]{:S(2)}) copy-start(bf16[64,64,256]{2,1,0:T(8,128)(2,1)} %param.8) | copy-start | bytes 6291460
  7.9 11.7 %copy-start.11 = (s32[256]{0:T(256)S(1)}, s32[256]{0:T(256)}, u32[]{:S(2)}) copy-start(s32[256]{0:T(256)} %param.11) | copy-start | bytes 3076
  7.9 11.7 %copy-start.12 = (s32[8]{0:T(128)S(1)}, s32[8]{0:T(128)}, u32[]{:S(2)}) copy-start(s32[8]{0:T(128)} %constant.231.clone) | copy-start | bytes 100
  7.9 11.8 %copy-start.14 = (s32[16]{0:T(128)S(1)}, s32[16]{0:T(128)}, u32[]{:S(2)}) copy-start(s32[16]{0:T(128)} %constant.230.clone) | copy-start | bytes 196
  7.9 11.8 %copy-start.13 = (s32[16]{0:T(128)S(1)}, s32[16]{0:T(128)}, u32[]{:S(2)}) copy-start(s32[16]{0:T(128)} %constant.232) | copy-start | bytes 196
  9.2 36.8 %collective-permute-start = (bf16[64,8,256]{2,1,0:T(8,128)(2,1)}, bf16[64,8,256]{2,1,0:T(8,128)(2,1)}, u32[]{:S(2)}, u32[]{:S(2)}) collective-permute-start(bf16[64,8,256]{2,1,0:T(8,128)(2,1)} %get-tuple-element.15), channel_id=1, source_target_pairs={{0,16},{16,32},{32,48},{48,64},{64,80},{80,96},{96,112},{112,0},{1... | collective-permute-start | bytes 786440 | tf_op jit(solution)/shard_map/ppermute | solution.py:71
  11.3 37.2 %collective-permute-start.1 = (bf16[64,8,256]{2,1,0:T(8,128)(2,1)}, bf16[64,8,256]{2,1,0:T(8,128)(2,1)}, u32[]{:S(2)}, u32[]{:S(2)}) collective-permute-start(bf16[64,8,256]{2,1,0:T(8,128)(2,1)} %get-tuple-element.14), channel_id=1, source_target_pairs={{0,32},{16,48},{32,64},{48,80},{64,96},{80,112},{96,0},{112,16},{1... | collective-permute-start | bytes 786440 | tf_op jit(solution)/shard_map/ppermute | solution.py:71
  14.9 37.1 %collective-permute-start.2 = (bf16[64,8,256]{2,1,0:T(8,128)(2,1)}, bf16[64,8,256]{2,1,0:T(8,128)(2,1)}, u32[]{:S(2)}, u32[]{:S(2)}) collective-permute-start(bf16[64,8,256]{2,1,0:T(8,128)(2,1)} %get-tuple-element.13), channel_id=1, source_target_pairs={{0,48},{16,64},{32,80},{48,96},{64,112},{80,0},{96,16},{112,32},{1... | collective-permute-start | bytes 786440 | tf_op jit(solution)/shard_map/ppermute | solution.py:71
  16.9 36.7 %collective-permute-start.3 = (bf16[64,8,256]{2,1,0:T(8,128)(2,1)}, bf16[64,8,256]{2,1,0:T(8,128)(2,1)}, u32[]{:S(2)}, u32[]{:S(2)}) collective-permute-start(bf16[64,8,256]{2,1,0:T(8,128)(2,1)} %get-tuple-element.12), channel_id=1, source_target_pairs={{0,64},{16,80},{32,96},{48,112},{64,0},{80,16},{96,32},{112,48},{1... | collective-permute-start | bytes 786440 | tf_op jit(solution)/shard_map/ppermute | solution.py:71
  17.4 38.0 %collective-permute-start.4 = (bf16[64,8,256]{2,1,0:T(8,128)(2,1)}, bf16[64,8,256]{2,1,0:T(8,128)(2,1)}, u32[]{:S(2)}, u32[]{:S(2)}) collective-permute-start(bf16[64,8,256]{2,1,0:T(8,128)(2,1)} %get-tuple-element.11), channel_id=1, source_target_pairs={{0,80},{16,96},{32,112},{48,0},{64,16},{80,32},{96,48},{112,64},{1... | collective-permute-start | bytes 786440 | tf_op jit(solution)/shard_map/ppermute | solution.py:71
  26.9 1.5 %copy-start.9 = (s32[128]{0:T(128)}, s32[128]{0:T(128)S(1)}, u32[]{:S(2)}) copy-start(s32[128]{0:T(128)S(1)} %get-tuple-element.40) | copy-start | bytes 1540
  46.0 11.0 %collective-permute-start.5 = (bf16[64,8,256]{2,1,0:T(8,128)(2,1)}, bf16[64,8,256]{2,1,0:T(8,128)(2,1)S(1)}, u32[]{:S(2)}, u32[]{:S(2)}) collective-permute-start(bf16[64,8,256]{2,1,0:T(8,128)(2,1)} %get-tuple-element.10), channel_id=1, source_target_pairs={{0,96},{16,112},{32,0},{48,16},{64,32},{80,48},{96,64},{112,80},{1... | collective-permute-start | bytes 786440 | tf_op jit(solution)/shard_map/ppermute | solution.py:71
  48.5 10.9 %collective-permute-start.6 = (bf16[64,8,256]{2,1,0:T(8,128)(2,1)S(1)}, bf16[64,8,256]{2,1,0:T(8,128)(2,1)S(1)}, u32[]{:S(2)}, u32[]{:S(2)}) collective-permute-start(bf16[64,8,256]{2,1,0:T(8,128)(2,1)S(1)} %get-tuple-element.9), channel_id=1, source_target_pairs={{0,112},{16,0},{32,16},{48,32},{64,48},{80,64},{96,80},{112,96},{1... | collective-permute-start | bytes 786440 | tf_op jit(solution)/shard_map/ppermute | solution.py:71
  74.1 3.7 %copy-start.1 = (bf16[16,512,256]{2,1,0:T(8,128)(2,1)S(1)}, bf16[16,512,256]{2,1,0:T(8,128)(2,1)}, u32[]{:S(2)}) copy-start(bf16[16,512,256]{2,1,0:T(8,128)(2,1)} %reshape.416) | copy-start | bytes 12582916
  79.2 1.4 copy-start.5
  79.2 1.4 copy-start.6
  79.2 1.4 copy-start.7
  79.2 1.4 copy-start.8
  83.1 10.0 %copy-start.16 = (s32[32]{0:T(128)S(1)}, s32[32]{0:T(128)}, u32[]{:S(2)}) copy-start(s32[32]{0:T(128)} %iota_add_fusion.4) | copy-start | bytes 388
  83.1 12.1 %copy-start.15 = (s32[128]{0:T(128)S(1)}, s32[128]{0:T(128)}, u32[]{:S(2)}) copy-start(s32[128]{0:T(128)} %get-tuple-element.39) | copy-start | bytes 1540
  83.1 12.1 %copy-start.10 = (s32[128]{0:T(128)S(1)}, s32[128]{0:T(128)}, u32[]{:S(2)}) copy-start(s32[128]{0:T(128)} %copy-done.9) | copy-start | bytes 1540
  83.1 29.0 %all-to-all-start = ((bf16[128,8,512]{2,1,0:T(8,128)(2,1)}), bf16[128,8,512]{2,1,0:T(8,128)(2,1)S(1)}, u32[]{:S(2)}, u32[]{:S(2)}) async-start(bf16[128,8,512]{2,1,0:T(8,128)(2,1)} %bitcast.13), calls=%async_computation | async-start | bytes 2097152 | tf_op jit(solution)/shard_map/all_to_all | solution.py:134
  114.9 1.0 copy-start.4
  117.2 12.9 %all-to-all-start.1 = ((bf16[16,2,32,128]{3,2,1,0:T(8,128)(2,1)}), bf16[16,2,32,128]{3,2,1,0:T(8,128)(2,1)S(1)}, u32[]{:S(2)}, u32[]{:S(2)}) async-start(bf16[16,2,32,128]{3,2,1,0:T(8,128)(2,1)} %copy.67), calls=%async_computation.1 | async-start | bytes 524288 | tf_op jit(solution)/shard_map/all_to_all | solution.py:177

commit v5 on v3

--- a/solution.py
+++ b/solution.py
@@ -131,7 +131,7 @@
     by_source = jnp.dot(
         summed.reshape(n_dev, -1).T.astype(jnp.float32),
         jnp.concatenate([src_cos, src_sin], axis=1),
-        precision=HIGHEST,
+        precision=lax.Precision.HIGH,
         preferred_element_type=jnp.float32,
     ).reshape(n_dyl, 2, k_blk, cols_here, 2, j_blk)
     part_re = by_source[:, 0, :, :, 0] + by_source[:, 1, :, :, 1]
@@ -162,7 +162,7 @@
         axis=0,
     )
     psi = psi.transpose(1, 0, 2).reshape(2 * k_blk, j_blk)
-    half = jnp.dot(inverse_rows, psi, precision=HIGHEST, preferred_element_type=jnp.float32)
+    half = jnp.dot(inverse_rows, psi, precision=lax.Precision.HIGH, preferred_element_type=jnp.float32)
     half = half.reshape(2, n_scol, row_count // n_scol, j_blk).transpose(1, 0, 2, 3)
     half = lax.all_to_all(half.astype(jnp.bfloat16), "scol", split_axis=0, concat_axis=0, tiled=True)
     half = jnp.sum(half.astype(jnp.float32), axis=0)
@@ -178,7 +178,7 @@
         axis=0,
     )
     half = half.transpose(1, 0, 2).reshape(out_rows, 2 * j_blk)
-    image = jnp.dot(half, inverse_cols, precision=HIGHEST, preferred_element_type=jnp.float32)
+    image = jnp.dot(half, inverse_cols, precision=lax.Precision.HIGH, preferred_element_type=jnp.float32)
     image = image.reshape(out_rows, 2, n_srow, out_cols).transpose(2, 0, 1, 3)
     image = lax.all_to_all(image.astype(jnp.bfloat16), "srow", split_axis=0, concat_axis=0, tiled=True)
     image = jnp.sum(image.astype(jnp.float32), axis=0) * (1.0 / (row_count * col_count))

time: 125 us -> 123 us (0.984)
  matrix products: 23 us -> 21.2 us
where the time goes in v5:
time: 123 us; the launch traced here: 122 us
  waiting for transfers between devices  33.3 us (27%)
  matrix products  21.2 us (17%)
  other arithmetic  20.4 us (17%)
  local copies, waits for them, and re-layouts  19 us (15%)
  starting transfers between devices  18.7 us (15%)
  blocking collectives  8.97 us (7%)
    all_to_all x1, waiting for transfers between devices, on_device(): lax.all_to_all(summed, ('scol', 'srow'), split_axis=0, concat_axis=0, til...  14.1 us
    all_to_all x1, waiting for transfers between devices, on_device(): lax.all_to_all(flattened, 'srow', split_axis=1, concat_axis=0, tiled=True)  11.1 us
    all_to_all x1, blocking collectives, on_device(): lax.all_to_all(image.astype(jnp.bfloat16), 'srow', split_axis=0, concat_a...  8.97 us
    dot_general x4, matrix products, on_device(): jnp.einsum('axp,anp->axn', weight[:, :, :, d].reshape(n_scol, n_srow * n_...  8.88 us
    all_to_all x1, starting transfers between devices, on_device(): lax.all_to_all(summed, ('scol', 'srow'), split_axis=0, concat_axis=0, til...  8.58 us
    all_to_all x1, waiting for transfers between devices, on_device(): lax.all_to_all(half.astype(jnp.bfloat16), 'scol', split_axis=0, concat_ax...  8.13 us
    reshape x1, local copies, waits for them, and re-layouts, on_device(): spec = spec.reshape(n_scol, 2 * k_blk * cols_here, n_pix)  7.55 us
    all_to_all x1, starting transfers between devices, on_device(): lax.all_to_all(flattened, 'srow', split_axis=1, concat_axis=0, tiled=True)  6.58 us
  transfers between devices with their start and end apart: 3, of which 3 were waited for; matrix products, arithmetic and copies ran while one was open for 17% of the time, Pallas kernels for 0%

profile of v5, /device:TPU:0, one launch (start us, length us, event | category | flops | bytes accessed | tf_op | source)
XLA Modules:
  0.0 122.0 jit_solution(1738748284950692261)
XLA Ops:
  0.0 0.0 copy-start
  0.0 2.4 %convert_reduce_fusion = f32[64,64]{1,0:T(8,128)S(1)} fusion(bf16[64,64,256]{2,1,0:T(8,128)(2,1)} %param.8), kind=kLoop, calls=%fused_computation | loop fusion | flops 2093056 | bytes 2113536 | tf_op jit(solution)/shard_map/reduce_sum | solution.py:58
  2.4 0.0 copy-done
  2.4 0.0 copy-done.3
  2.4 0.0 copy-done.13
  2.4 2.6 %fusion.1 = f32[64,64,16]{1,2,0:T(8,128)S(1)} fusion(bf16[64,64,256]{2,1,0:T(8,128)(2,1)S(1)} %copy-done.3, f32[64,64]{1,0:T(8,128)S(1)} %broadcast_multiply_fusion.1, f32[256]{0:T(256)S(1)} %copy-done.13, f32[16,256]{1,0:T(8,128)S(1)} %copy-done), kind=kOutput, calls=%fused_computation.8 | convolution fusion | flops 103809024 | bytes 2393088 | tf_op jit(solution)/shard_map/rcp,ep->rce/dot_general | solution.py:60
  5.0 2.8 %subtract_convert_fusion = bf16[64,64,256]{2,1,0:T(8,128)(2,1)S(1)} fusion(bf16[64,64,256]{2,1,0:T(8,128)(2,1)S(1)} %copy-done.3, f32[64,64,16]{1,2,0:T(8,128)S(1)} %fusion.1, f32[64,64]{1,0:T(8,128)S(1)} %broadcast_multiply_fusion.1, f32[256]{0:T(256)S(1)} %copy-done.13, f32[16,256]{1,0:T(8,128)S(1)} %copy-done), kind=kOutput, calls=%fused_computation.3 | convolution fusion | flops 105906176 | bytes 4490240 | tf_op jit(solution)/shard_map/rce,ep->rcp/dot_general | solution.py:61
  7.8 2.5 %copy.67 = bf16[64,64,256]{2,0,1:T(8,128)(2,1)} copy(bf16[64,64,256]{2,1,0:T(8,128)(2,1)S(1)} %subtract_convert_fusion) | data formatting | bytes 4194304 | tf_op jit(solution)/shard_map/convert_element_type | solution.py:62
  10.3 6.6 %all-to-all-start = ((bf16[64,64,256]{2,0,1:T(8,128)(2,1)}), bf16[64,64,256]{2,0,1:T(8,128)(2,1)S(1)}, u32[]{:S(2)}, u32[]{:S(2)}) async-start(bf16[64,64,256]{2,0,1:T(8,128)(2,1)} %copy.67), calls=%async_computation | async-start | bytes 4194304 | tf_op jit(solution)/shard_map/all_to_all | solution.py:64
  16.9 1.0 fusion.34
  18.0 0.2 fusion.61
  18.1 0.2 copy.65
  18.3 0.9 copy.66
  19.2 0.0 copy-done.9
  19.2 0.6 dynamic_slice.3
  19.8 1.2 fusion.68
  20.9 0.3 fusion.44
  21.3 0.2 copy-done.6
  21.4 3.7 %subtract_convert_fusion.2 = (bf16[512,4,128]{2,1,0:T(4,128)(2,1)}, bf16[512,4,128]{2,1,0:T(4,128)(2,1)S(1)}) fusion(f32[512,128]{1,0:T(8,128)S(1)} %get-tuple-element.35, f32[512,4]{1,0:T(8,128)} %copy.66, f32[512,128]{1,0:T(8,128)S(1)} %get-tuple-element.36, f32[512,4]{1,0:T(8,128)S(1)} %copy.65), kind=kLoop, calls=%fused_computation.27 | loop fusion | flops 2359296 | bytes 1589248 | tf_op jit(solution)/shard_map/convert.3
  25.1 0.7 broadcast_compare_fusion.2
  25.8 0.2 neg.22
  26.0 0.0 copy-start.11
  26.0 0.0 copy-start.8
  26.0 0.0 copy-start.10
  26.0 1.3 %sub.154 = bf16[1,16,32,512]{3,2,0,1:T(8,128)(2,1)S(1)} reshape(bf16[512,4,128]{2,1,0:T(4,128)(2,1)} %get-tuple-element.9) | data formatting | bytes 1048576 | tf_op jit(solution)/shard_map/sub | solution.py:29
  27.3 0.1 copy.64
  27.4 0.1 copy.69
  27.6 0.1 copy.70
  27.7 0.1 copy.71
  27.9 1.1 pad_maximum_fusion
  29.0 0.0 copy-done.8
  29.0 0.1 iota_add_fusion
  29.1 0.1 subtract_multiply_fusion.1
  29.1 0.1 subtract_multiply_fusion
  29.2 2.6 %subtract_convert_fusion.1 = bf16[16,8,8,4,256]{4,2,1,0,3:T(8,128)(2,1)} fusion(s32[8,8,256]{2,1,0:T(8,128)S(1)} %get-tuple-element.12, s32[16,4,256]{2,0,1:T(8,128)S(1)} %get-tuple-element.14, s32[8,8,256]{2,1,0:T(8,128)S(1)} %get-tuple-element.11, s32[16,4,256]{2,0,1:T(8,128)S(1)} %get-tuple-element.13), kind=kLoop, calls=%fused_computation.4 | loop fusion | flops 8388608 | bytes 2359296 | tf_op jit(solution)/shard_map/convert_element_type | solution.py:107
  31.9 11.1 %all-to-all-done = bf16[64,64,256]{2,0,1:T(8,128)(2,1)S(1)} async-done(((bf16[64,64,256]{2,0,1:T(8,128)(2,1)}), bf16[64,64,256]{2,0,1:T(8,128)(2,1)S(1)}, u32[]{:S(2)}, u32[]{:S(2)}) %all-to-all-start) | async-done | bytes 2097184 | tf_op jit(solution)/shard_map/all_to_all | solution.py:64
  43.0 1.3 %copy.68 = bf16[64,8,8,256]{3,2,0,1:T(8,128)(2,1)S(1)} copy(bf16[64,8,8,256]{3,0,2,1:T(8,128)(2,1)S(1)} %bitcast.111) | data formatting | bytes 4194304 | tf_op jit(solution)/shard_map/all_to_all | solution.py:64
  44.2 0.7 copy.90
  44.9 0.5 copy-done.5
  45.4 4.3 %convolution_convert_fusion = bf16[1024,2048]{1,0:T(8,128)(2,1)} fusion(bf16[1024,512]{1,0:T(8,128)(2,1)S(1)} %bitcast.116, bf16[512,2048]{1,0:T(8,128)(2,1)S(1)} %bitcast.114), kind=kOutput, calls=%fused_computation.7 | convolution fusion | flops 2149580800 | bytes 7340032 | tf_op jit(solution)/shard_map/dot_general | solution.py:73
  49.8 7.5 %reshape.451 = bf16[16,512,256]{2,1,0:T(8,128)(2,1)} reshape(bf16[1024,2048]{1,0:T(8,128)(2,1)} %convolution_convert_fusion) | data formatting | bytes 8388608 | tf_op jit(solution)/shard_map/reshape | solution.py:78
  57.3 3.7 %fusion.13 = f32[16,64,512]{2,1,0:T(8,128)S(1)} fusion(bf16[16,512,256]{2,1,0:T(8,128)(2,1)} %reshape.451, bf16[16,8,8,4,256]{4,2,1,0,3:T(8,128)(2,1)S(1)} %copy-done.2), kind=kOutput, calls=%fused_computation.36 | convolution fusion | flops 268435456 | bytes 6815744 | tf_op jit(solution)/shard_map/axp,anp->axn/dot_general | solution.py:114
  61.0 0.0 copy-done.1
  61.0 1.4 %fusion.14 = f32[16,64,512]{2,1,0:T(8,128)S(1)} fusion(bf16[16,512,256]{2,1,0:T(8,128)(2,1)S(1)} %copy-done.1, bf16[16,8,8,4,256]{4,2,1,0,3:T(8,128)(2,1)S(1)} %copy-done.2), kind=kOutput, calls=%fused_computation.38 | convolution fusion | flops 268435456 | bytes 6815744 | tf_op jit(solution)/shard_map/axp,anp->axn/dot_general | solution.py:114
  62.4 1.4 %fusion.15 = f32[16,64,512]{2,1,0:T(8,128)S(1)} fusion(bf16[16,512,256]{2,1,0:T(8,128)(2,1)S(1)} %copy-done.1, bf16[16,8,8,4,256]{4,2,1,0,3:T(8,128)(2,1)S(1)} %copy-done.2), kind=kOutput, calls=%fused_computation.40 | convolution fusion | flops 268435456 | bytes 6815744 | tf_op jit(solution)/shard_map/axp,anp->axn/dot_general | solution.py:114
  63.8 2.4 %add_convert_fusion = bf16[16,64,512]{2,1,0:T(8,128)(2,1)} fusion(f32[16,64,512]{2,1,0:T(8,128)S(1)} %fusion.13, f32[16,64,512]{2,1,0:T(8,128)S(1)} %fusion.14, f32[16,64,512]{2,1,0:T(8,128)S(1)} %fusion.15, bf16[16,512,256]{2,1,0:T(8,128)(2,1)S(1)} %copy-done.1, pred[16,512]{1,0:T(8,128)(4,1)S(1)} %copy.71, pred[16,512]{1,0:T(8,128)(4,1)S(1)} %copy.70, ...), kind=kOutput, calls=%fused_computation.10 | convolution fusion | flops 272629760 | bytes 12091392 | tf_op jit(solution)/shard_map/axp,anp->axn/dot_general | solution.py:114
  66.2 8.6 %all-to-all-start.1 = ((bf16[128,8,512]{2,1,0:T(8,128)(2,1)}), bf16[128,8,512]{2,1,0:T(8,128)(2,1)S(1)}, u32[]{:S(2)}, u32[]{:S(2)}) async-start(bf16[128,8,512]{2,1,0:T(8,128)(2,1)} %bitcast.15), calls=%async_computation.1 | async-start | bytes 2097152 | tf_op jit(solution)/shard_map/all_to_all | solution.py:124
  74.8 1.0 fusion.38
  75.8 1.0 maximum_maximum_fusion.1
  76.9 0.1 fusion.64
  76.9 2.9 %fusion.25 = (f32[128,1024]{0,1:T(8,128)S(1)}, f32[128,1024]{0,1:T(8,128)S(1)}, f32[128,1024]{0,1:T(8,128)}) fusion(s32[128]{0:T(128)S(1)} %copy-done.7), kind=kLoop, calls=%fused_computation.59 | loop fusion | flops 1966080 | bytes 1573376 | tf_op jit(solution)/shard_map/sin | solution.py:16
  79.9 14.1 %all-to-all-done.1 = bf16[128,8,512]{2,1,0:T(8,128)(2,1)S(1)} async-done(((bf16[128,8,512]{2,1,0:T(8,128)(2,1)}), bf16[128,8,512]{2,1,0:T(8,128)(2,1)S(1)}, u32[]{:S(2)}, u32[]{:S(2)}) %all-to-all-start.1) | async-done | bytes 1048608 | tf_op jit(solution)/shard_map/all_to_all | solution.py:124
  94.0 1.0 copy.85
  95.0 1.2 %fusion.69 = f32[8,2,32,8,2,128]{5,3,4,2,1,0:T(8,128)S(1)} fusion(bf16[8,2,32,8,128,1]{4,3,5,2,1,0:T(8,128)(2,1)S(1)} %bitcast.113, f32[2,128,128,1,1,1]{2,1,0,5,4,3:T(8,128)S(1)} %bitcast.117), kind=kOutput, calls=%fused_computation.153 | convolution fusion | flops 805306368 | bytes 5373952 | tf_op jit(solution)/shard_map/dot_general | solution.py:131
  96.2 0.8 add_reduce_fusion
  97.0 0.2 copy-done.4
  97.3 0.4 fusion.5
  97.6 0.7 copy.75
  98.3 3.5 %all-to-all-start.2 = ((bf16[16,2,32,128]{3,2,1,0:T(8,128)(2,1)}), bf16[16,2,32,128]{3,2,1,0:T(8,128)(2,1)S(1)}, u32[]{:S(2)}, u32[]{:S(2)}) async-start(bf16[16,2,32,128]{3,2,1,0:T(8,128)(2,1)} %copy.75), calls=%async_computation.2 | async-start | bytes 524288 | tf_op jit(solution)/shard_map/all_to_all | solution.py:167
  101.9 1.2 maximum_maximum_fusion
  103.1 8.1 %all-to-all-done.2 = bf16[16,2,32,128]{3,2,1,0:T(8,128)(2,1)S(1)} async-done(((bf16[16,2,32,128]{3,2,1,0:T(8,128)(2,1)}), bf16[16,2,32,128]{3,2,1,0:T(8,128)(2,1)S(1)}, u32[]{:S(2)}, u32[]{:S(2)}) %all-to-all-start.2) | async-done | bytes 262176 | tf_op jit(solution)/shard_map/all_to_all | solution.py:167
  111.3 1.0 fusion.6
  112.4 9.0 %all_to_all.30 = bf16[8,32,2,128]{3,1,2,0:T(8,128)(2,1)S(1)} all-to-all(bf16[8,32,2,128]{3,1,2,0:T(8,128)(2,1)S(1)} %copy.78), channel_id=1, replica_groups=mesh['srow'=8,'scol'=16] {'srow'}, dimensions={0} | all-to-all | bytes 262144 | tf_op jit(solution)/shard_map/all_to_all | solution.py:183
  121.4 0.6 copy.80
  (35 shorter events, 0.3 us)
Async XLA Ops:
  0.0 2.4 %copy-start = (f32[16,256]{1,0:T(8,128)S(1)}, f32[16,256]{1,0:T(8,128)}, u32[]{:S(2)}) copy-start(f32[16,256]{1,0:T(8,128)} %param.10) | copy-start | bytes 49156
  0.0 2.4 %copy-start.3 = (bf16[64,64,256]{2,1,0:T(8,128)(2,1)S(1)}, bf16[64,64,256]{2,1,0:T(8,128)(2,1)}, u32[]{:S(2)}) copy-start(bf16[64,64,256]{2,1,0:T(8,128)(2,1)} %param.8) | copy-start | bytes 6291460
  0.0 2.4 %copy-start.13 = (f32[256]{0:T(256)S(1)}, f32[256]{0:T(256)}, u32[]{:S(2)}) copy-start(f32[256]{0:T(256)} %param.9) | copy-start | bytes 3076
  10.3 8.8 %copy-start.9 = (s32[8]{0:T(128)S(1)}, s32[8]{0:T(128)}, u32[]{:S(2)}) copy-start(s32[8]{0:T(128)} %constant.185.clone) | copy-start | bytes 100
  10.3 32.6 %all-to-all-start = ((bf16[64,64,256]{2,0,1:T(8,128)(2,1)}), bf16[64,64,256]{2,0,1:T(8,128)(2,1)S(1)}, u32[]{:S(2)}, u32[]{:S(2)}) async-start(bf16[64,64,256]{2,0,1:T(8,128)(2,1)} %copy.67), calls=%async_computation | async-start | bytes 4194304 | tf_op jit(solution)/shard_map/all_to_all | solution.py:64
  20.9 0.5 copy-start.6
  26.0 3.0 %copy-start.11 = (s32[16]{0:T(128)S(1)}, s32[16]{0:T(128)}, u32[]{:S(2)}) copy-start(s32[16]{0:T(128)} %constant.184.clone) | copy-start | bytes 196
  26.0 3.0 %copy-start.8 = (s32[256]{0:T(256)S(1)}, s32[256]{0:T(256)}, u32[]{:S(2)}) copy-start(s32[256]{0:T(256)} %param.11) | copy-start | bytes 3076
  26.0 3.0 %copy-start.10 = (s32[8]{0:T(128)S(1)}, s32[8]{0:T(128)}, u32[]{:S(2)}) copy-start(s32[8]{0:T(128)} %constant.185.clone) | copy-start | bytes 100
  44.2 1.2 %copy-start.5 = (bf16[2,16,32,512]{3,2,0,1:T(8,128)(2,1)S(1)}, bf16[2,16,32,512]{3,2,0,1:T(8,128)(2,1)}, u32[]{:S(2)}) copy-start(bf16[2,16,32,512]{3,2,0,1:T(8,128)(2,1)} %pad_maximum_fusion) | copy-start | bytes 3145732
  49.8 7.6 %copy-start.2 = (bf16[16,8,8,4,256]{4,2,1,0,3:T(8,128)(2,1)S(1)}, bf16[16,8,8,4,256]{4,2,1,0,3:T(8,128)(2,1)}, u32[]{:S(2)}) copy-start(bf16[16,8,8,4,256]{4,2,1,0,3:T(8,128)(2,1)} %subtract_convert_fusion.1) | copy-start | bytes 6291460
  57.3 3.7 %copy-start.1 = (bf16[16,512,256]{2,1,0:T(8,128)(2,1)S(1)}, bf16[16,512,256]{2,1,0:T(8,128)(2,1)}, u32[]{:S(2)}) copy-start(bf16[16,512,256]{2,1,0:T(8,128)(2,1)} %reshape.451) | copy-start | bytes 12582916
  66.2 10.7 %copy-start.12 = (s32[128]{0:T(128)S(1)}, s32[128]{0:T(128)}, u32[]{:S(2)}) copy-start(s32[128]{0:T(128)} %get-tuple-element.33) | copy-start | bytes 1540
  66.2 10.7 %copy-start.7 = (s32[128]{0:T(128)S(1)}, s32[128]{0:T(128)}, u32[]{:S(2)}) copy-start(s32[128]{0:T(128)} %copy-done.6) | copy-start | bytes 1540
  66.2 27.8 %all-to-all-start.1 = ((bf16[128,8,512]{2,1,0:T(8,128)(2,1)}), bf16[128,8,512]{2,1,0:T(8,128)(2,1)S(1)}, u32[]{:S(2)}, u32[]{:S(2)}) async-start(bf16[128,8,512]{2,1,0:T(8,128)(2,1)} %bitcast.15), calls=%async_computation.1 | async-start | bytes 2097152 | tf_op jit(solution)/shard_map/all_to_all | solution.py:124
  96.2 1.0 copy-start.4
  98.3 12.9 %all-to-all-start.2 = ((bf16[16,2,32,128]{3,2,1,0:T(8,128)(2,1)}), bf16[16,2,32,128]{3,2,1,0:T(8,128)(2,1)S(1)}, u32[]{:S(2)}, u32[]{:S(2)}) async-start(bf16[16,2,32,128]{3,2,1,0:T(8,128)(2,1)} %copy.75), calls=%async_computation.2 | async-start | bytes 524288 | tf_op jit(solution)/shard_map/all_to_all | solution.py:167

commit v6 on v5

--- a/solution.py
+++ b/solution.py
@@ -109,16 +109,11 @@
     own_dx = own_dx - jnp.array(dx_first, dtype=jnp.int32)[:, None]
     dx_of_n = jnp.broadcast_to(own_dx[:, None, :, None], (n_scol, 2, k_blk, cols_here))
     dx_of_n = dx_of_n.reshape(n_scol, 1, 2 * k_blk * cols_here)
-    summed = None
-    for d in range(n_dx):
-        part = jnp.einsum(
-            "axp,anp->axn",
-            weight[:, :, :, d].reshape(n_scol, n_srow * n_dyl, n_pix),
-            spec,
-            preferred_element_type=jnp.float32,
-        )
-        part = jnp.where(dx_of_n == d, part, 0.0)
-        summed = part if summed is None else summed + part
+    weight = weight.transpose(0, 3, 1, 2, 4).reshape(n_scol, n_dx * n_srow * n_dyl, n_pix)
+    every_dx = jnp.einsum("axp,anp->axn", weight, spec, preferred_element_type=jnp.float32)
+    every_dx = every_dx.reshape(n_scol, n_dx, n_srow * n_dyl, 2 * k_blk * cols_here)
+    dx_pick = dx_of_n[:, None, :, :] == jnp.arange(n_dx, dtype=jnp.int32)[None, :, None, None]
+    summed = jnp.sum(jnp.where(dx_pick, every_dx, 0.0), axis=1)
     summed = summed.reshape(n_dev, n_dyl, 2 * k_blk * cols_here).astype(jnp.bfloat16)
 
     summed = lax.all_to_all(summed, ("scol", "srow"), split_axis=0, concat_axis=0, tiled=True)

time: 123 us -> 122 us (level)
  waiting for transfers between devices: 33.3 us -> 40.3 us
  matrix products: 21.2 us -> 17.4 us
  other arithmetic: 20.4 us -> 18.1 us
  local copies, waits for them, and re-layouts: 19 us -> 17.4 us
    all_to_all x1, waiting for transfers between devices: 11.1 us -> 18.3 us  [on_device(): lax.all_to_all(flattened, 'srow', split_axis=1, concat_axis=0, tiled=True)]
    dot_general x4 -> x1, matrix products: 8.88 us -> 3.47 us  [on_device(): jnp.einsum('axp,anp->axn', weight, spec, preferred_element_type=jnp.float32)]
    reduce_sum x0 -> x1, other arithmetic: none -> 2.47 us  [on_device(): summed = jnp.sum(jnp.where(dx_pick, every_dx, 0.0), axis=1)]
    another operation x1, other arithmetic: 3.66 us -> 1.39 us
    all_to_all x1, local copies, waits for them, and re-layouts: 1.27 us -> 2.95 us  [on_device(): lax.all_to_all(flattened, 'srow', split_axis=1, concat_axis=0, tiled=True)]
    dot_general x1, matrix products: 2.63 us -> 4.21 us  [on_device(): jnp.einsum('rcp,ep->rce', scaled, eigen_flats, precision=lax.Precision.HIGH)]
    convert_element_type x1, other arithmetic: 2.63 us -> 1.22 us  [on_device(): (upper.astype(jnp.float32) - lower.astype(jnp.float32)).astype(jnp.bfloat16)]
  transfers between devices with their start and end apart: 3 -> 3, of which waited for: 3 -> 3; matrix products, arithmetic and copies ran while one was open for 17% -> 11% of each run, Pallas kernels for 0% -> 0%
where the time goes in v6:
time: 122 us; the launch traced here: 121 us
  waiting for transfers between devices  40.3 us (33%)
  starting transfers between devices  18.9 us (15%)
  other arithmetic  18.1 us (15%)
  local copies, waits for them, and re-layouts  17.4 us (14%)
  matrix products  17.4 us (14%)
  blocking collectives  8.97 us (7%)
    all_to_all x1, waiting for transfers between devices, on_device(): lax.all_to_all(flattened, 'srow', split_axis=1, concat_axis=0, tiled=True)  18.3 us
    all_to_all x1, waiting for transfers between devices, on_device(): lax.all_to_all(summed, ('scol', 'srow'), split_axis=0, concat_axis=0, til...  13.9 us
    all_to_all x1, blocking collectives, on_device(): lax.all_to_all(image.astype(jnp.bfloat16), 'srow', split_axis=0, concat_a...  8.97 us
    all_to_all x1, starting transfers between devices, on_device(): lax.all_to_all(summed, ('scol', 'srow'), split_axis=0, concat_axis=0, til...  8.8 us
    all_to_all x1, waiting for transfers between devices, on_device(): lax.all_to_all(half.astype(jnp.bfloat16), 'scol', split_axis=0, concat_ax...  8.13 us
    reshape x1, local copies, waits for them, and re-layouts, on_device(): spec = spec.reshape(n_scol, 2 * k_blk * cols_here, n_pix)  7.42 us
    all_to_all x1, starting transfers between devices, on_device(): lax.all_to_all(flattened, 'srow', split_axis=1, concat_axis=0, tiled=True)  6.57 us
    dot_general x1, matrix products, on_device(): jnp.dot(forward_rows.astype(jnp.bfloat16), gathered.reshape(row_count, co...  4.28 us
  transfers between devices with their start and end apart: 3, of which 3 were waited for; matrix products, arithmetic and copies ran while one was open for 11% of the time, Pallas kernels for 0%

profile of v6, /device:TPU:0, one launch (start us, length us, event | category | flops | bytes accessed | tf_op | source)
XLA Modules:
  0.0 121.4 jit_solution(5523411698362843073)
XLA Ops:
  0.0 0.0 copy-start
  0.0 2.2 %convert_reduce_fusion = f32[64,64]{1,0:T(8,128)S(1)} fusion(bf16[64,64,256]{2,1,0:T(8,128)(2,1)} %param.8), kind=kLoop, calls=%fused_computation.1 | loop fusion | flops 2093056 | bytes 2113536 | tf_op jit(solution)/shard_map/reduce_sum | solution.py:58
  2.2 0.0 copy-done
  2.2 0.0 copy-start.1
  2.3 0.0 copy-start.8
  2.3 4.2 %fusion.3 = f32[64,64,16]{1,2,0:T(8,128)S(1)} fusion(bf16[64,64,256]{2,1,0:T(8,128)(2,1)} %param.8, f32[64,64]{1,0:T(8,128)S(1)} %broadcast_multiply_fusion.1, f32[256]{0:T(256)} %param.9, f32[16,256]{1,0:T(8,128)S(1)} %copy-done), kind=kOutput, calls=%fused_computation.11 | convolution fusion | flops 103809024 | bytes 2393088 | tf_op jit(solution)/shard_map/rcp,ep->rce/dot_general | solution.py:60
  6.5 0.0 copy-done.1
  6.5 0.0 copy-done.8
  6.5 2.8 %subtract_convert_fusion = bf16[64,64,256]{2,1,0:T(8,128)(2,1)S(1)} fusion(bf16[64,64,256]{2,1,0:T(8,128)(2,1)S(1)} %copy-done.1, f32[64,64,16]{1,2,0:T(8,128)S(1)} %fusion.3, f32[64,64]{1,0:T(8,128)S(1)} %broadcast_multiply_fusion.1, f32[256]{0:T(256)S(1)} %copy-done.8, f32[16,256]{1,0:T(8,128)S(1)} %copy-done), kind=kOutput, calls=%fused_computation.8 | convolution fusion | flops 105906176 | bytes 4490240 | tf_op jit(solution)/shard_map/rce,ep->rcp/dot_general | solution.py:61
  9.3 0.0 copy-start.6
  9.3 0.0 copy-start.7
  9.3 2.5 %copy.54 = bf16[64,64,256]{2,0,1:T(8,128)(2,1)} copy(bf16[64,64,256]{2,1,0:T(8,128)(2,1)S(1)} %subtract_convert_fusion) | data formatting | bytes 4194304 | tf_op jit(solution)/shard_map/convert_element_type | solution.py:62
  11.8 0.0 copy-start.4
  11.8 0.0 copy-start.5
  11.8 6.6 %all-to-all-start = ((bf16[64,64,256]{2,0,1:T(8,128)(2,1)}), bf16[64,64,256]{2,0,1:T(8,128)(2,1)}, u32[]{:S(2)}, u32[]{:S(2)}) async-start(bf16[64,64,256]{2,0,1:T(8,128)(2,1)} %copy.54), calls=%async_computation | async-start | bytes 4194304 | tf_op jit(solution)/shard_map/all_to_all | solution.py:64
  18.4 1.0 fusion.33
  19.4 0.2 fusion.60
  19.6 0.2 copy.52
  19.8 0.1 copy.53
  19.9 0.0 copy-done.6
  19.9 0.1 iota_add_fusion.1
  20.0 0.0 copy-done.7
  20.0 1.4 %subtract_convert_fusion.2 = (bf16[512,4,128]{2,1,0:T(4,128)(2,1)S(1)}, bf16[512,4,128]{2,1,0:T(4,128)(2,1)S(1)}) fusion(f32[512,128]{1,0:T(8,128)S(1)} %get-tuple-element.31, f32[512,4]{1,0:T(8,128)S(1)} %copy.53, f32[512,128]{1,0:T(8,128)S(1)} %get-tuple-element.32, f32[512,4]{1,0:T(8,128)S(1)} %copy.52), kind=kLoop, calls=%fused_computation.29 | loop fusion | flops 2359296 | bytes 1589248 | tf_op jit(solution)/shard_map/convert.3
  21.4 0.0 copy-done.4
  21.5 0.6 dynamic_slice.3
  22.0 0.2 neg.22
  22.2 0.2 sub.156
  22.5 0.1 copy.51
  22.6 0.0 copy-done.5
  22.6 0.1 iota_add_fusion
  22.6 0.1 subtract_multiply_fusion
  22.7 0.1 subtract_multiply_fusion.1
  22.9 1.2 %subtract_convert_fusion.1 = bf16[16,256,256]{2,1,0:T(8,128)(2,1)S(1)} fusion(s32[256,256]{1,0:T(8,128)S(1)} %bitcast.117, s32[16,4,256]{2,1,0:T(4,128)S(1)} %get-tuple-element.12, s32[256,256]{1,0:T(8,128)S(1)} %bitcast.116, s32[16,4,256]{2,1,0:T(4,128)S(1)} %get-tuple-element.11), kind=kLoop, calls=%fused_computation.9 | loop fusion | flops 8388608 | bytes 2752512 | tf_op jit(solution)/shard_map/convert_element_type | solution.py:107
  24.1 0.7 fusion.67
  24.8 0.3 fusion.43
  25.2 1.1 pad_maximum_fusion
  26.3 18.3 %all-to-all-done = bf16[64,64,256]{2,0,1:T(8,128)(2,1)} async-done(((bf16[64,64,256]{2,0,1:T(8,128)(2,1)}), bf16[64,64,256]{2,0,1:T(8,128)(2,1)}, u32[]{:S(2)}, u32[]{:S(2)}) %all-to-all-start) | async-done | bytes 2097184 | tf_op jit(solution)/shard_map/all_to_all | solution.py:64
  44.5 0.0 copy-start.3
  44.5 2.9 %copy.55 = bf16[64,8,8,256]{3,2,0,1:T(8,128)(2,1)S(1)} copy(bf16[64,8,8,256]{3,0,2,1:T(8,128)(2,1)} %bitcast.10) | data formatting | bytes 4194304 | tf_op jit(solution)/shard_map/all_to_all | solution.py:64
  47.5 0.7 copy.74
  48.2 0.0 copy-done.3
  48.2 4.3 %convolution_convert_fusion = bf16[1024,2048]{1,0:T(8,128)(2,1)} fusion(bf16[1024,512]{1,0:T(8,128)(2,1)S(1)} %bitcast.114, bf16[512,2048]{1,0:T(8,128)(2,1)S(1)} %bitcast.112), kind=kOutput, calls=%fused_computation.10 | convolution fusion | flops 2149580800 | bytes 7340032 | tf_op jit(solution)/shard_map/dot_general | solution.py:73
  52.5 7.4 %reshape.430 = bf16[16,512,256]{2,1,0:T(8,128)(2,1)} reshape(bf16[1024,2048]{1,0:T(8,128)(2,1)} %convolution_convert_fusion) | data formatting | bytes 8388608 | tf_op jit(solution)/shard_map/reshape | solution.py:78
  59.9 3.5 %fusion.68 = f32[16,256,512]{2,1,0:T(8,128)S(1)} fusion(bf16[16,256,256]{2,1,0:T(8,128)(2,1)S(1)} %subtract_convert_fusion.1, bf16[16,512,256]{2,1,0:T(8,128)(2,1)} %reshape.430), kind=kOutput, calls=%fused_computation.145 | convolution fusion | flops 1073741824 | bytes 14680064 | tf_op jit(solution)/shard_map/axp,anp->axn/dot_general | solution.py:113
  63.4 2.5 %select_reduce_fusion = bf16[16,64,512]{2,1,0:T(8,128)(2,1)} fusion(f32[16,4,64,512]{3,2,1,0:T(8,128)S(1)} %bitcast.108, pred[16,4,512]{2,1,0:T(4,128)(4,1)S(1)} %iota_compare_fusion), kind=kLoop, calls=%fused_computation | loop fusion | flops 3670016 | bytes 9469952 | tf_op jit(solution)/shard_map/reduce_sum | solution.py:116
  65.8 8.8 %all-to-all-start.1 = ((bf16[128,8,512]{2,1,0:T(8,128)(2,1)}), bf16[128,8,512]{2,1,0:T(8,128)(2,1)S(1)}, u32[]{:S(2)}, u32[]{:S(2)}) async-start(bf16[128,8,512]{2,1,0:T(8,128)(2,1)} %bitcast.13), calls=%async_computation.1 | async-start | bytes 2097152 | tf_op jit(solution)/shard_map/all_to_all | solution.py:119
  74.6 1.0 fusion.37
  75.7 1.0 maximum_maximum_fusion.1
  76.7 0.1 fusion.63
  76.7 2.9 %fusion.24 = (f32[128,1024]{0,1:T(8,128)S(1)}, f32[128,1024]{0,1:T(8,128)S(1)}, f32[128,1024]{0,1:T(8,128)}) fusion(s32[128]{0:T(128)S(1)} %get-tuple-element.30), kind=kLoop, calls=%fused_computation.54 | loop fusion | flops 1966080 | bytes 1573376 | tf_op jit(solution)/shard_map/sin | solution.py:16
  79.7 13.9 %all-to-all-done.1 = bf16[128,8,512]{2,1,0:T(8,128)(2,1)S(1)} async-done(((bf16[128,8,512]{2,1,0:T(8,128)(2,1)}), bf16[128,8,512]{2,1,0:T(8,128)(2,1)S(1)}, u32[]{:S(2)}, u32[]{:S(2)}) %all-to-all-start.1) | async-done | bytes 1048608 | tf_op jit(solution)/shard_map/all_to_all | solution.py:119
  93.6 1.0 copy.69
  94.6 0.0 copy-start.2
  94.6 1.2 %fusion.69 = f32[8,2,32,8,2,128]{5,3,4,2,1,0:T(8,128)S(1)} fusion(bf16[8,2,32,8,128,1]{4,3,5,2,1,0:T(8,128)(2,1)S(1)} %bitcast.111, f32[2,128,128,1,1,1]{2,1,0,5,4,3:T(8,128)S(1)} %bitcast.118), kind=kOutput, calls=%fused_computation.146 | convolution fusion | flops 805306368 | bytes 5373952 | tf_op jit(solution)/shard_map/dot_general | solution.py:126
  95.9 0.8 add_reduce_fusion
  96.7 0.0 copy-done.2
  96.7 0.4 fusion.7
  97.1 0.7 copy.59
  97.8 3.5 %all-to-all-start.2 = ((bf16[16,2,32,128]{3,2,1,0:T(8,128)(2,1)}), bf16[16,2,32,128]{3,2,1,0:T(8,128)(2,1)S(1)}, u32[]{:S(2)}, u32[]{:S(2)}) async-start(bf16[16,2,32,128]{3,2,1,0:T(8,128)(2,1)} %copy.59), calls=%async_computation.2 | async-start | bytes 524288 | tf_op jit(solution)/shard_map/all_to_all | solution.py:162
  101.3 1.2 maximum_maximum_fusion
  102.5 8.1 %all-to-all-done.2 = bf16[16,2,32,128]{3,2,1,0:T(8,128)(2,1)S(1)} async-done(((bf16[16,2,32,128]{3,2,1,0:T(8,128)(2,1)}), bf16[16,2,32,128]{3,2,1,0:T(8,128)(2,1)S(1)}, u32[]{:S(2)}, u32[]{:S(2)}) %all-to-all-start.2) | async-done | bytes 262176 | tf_op jit(solution)/shard_map/all_to_all | solution.py:162
  110.7 1.0 fusion.8
  111.8 9.0 %all_to_all.30 = bf16[8,32,2,128]{3,1,2,0:T(8,128)(2,1)S(1)} all-to-all(bf16[8,32,2,128]{3,1,2,0:T(8,128)(2,1)S(1)} %copy.62), channel_id=1, replica_groups=mesh['srow'=8,'scol'=16] {'srow'}, dimensions={0} | all-to-all | bytes 262144 | tf_op jit(solution)/shard_map/all_to_all | solution.py:178
  120.8 0.6 copy.64
  (20 shorter events, 0.3 us)
Async XLA Ops:
  0.0 2.2 %copy-start = (f32[16,256]{1,0:T(8,128)S(1)}, f32[16,256]{1,0:T(8,128)}, u32[]{:S(2)}) copy-start(f32[16,256]{1,0:T(8,128)} %param.10) | copy-start | bytes 49156
  2.2 4.2 %copy-start.1 = (bf16[64,64,256]{2,1,0:T(8,128)(2,1)S(1)}, bf16[64,64,256]{2,1,0:T(8,128)(2,1)}, u32[]{:S(2)}) copy-start(bf16[64,64,256]{2,1,0:T(8,128)(2,1)} %param.8) | copy-start | bytes 6291460
  2.3 4.2 %copy-start.8 = (f32[256]{0:T(256)S(1)}, f32[256]{0:T(256)}, u32[]{:S(2)}) copy-start(f32[256]{0:T(256)} %param.9) | copy-start | bytes 3076
  9.3 10.6 %copy-start.6 = (s32[8]{0:T(128)S(1)}, s32[8]{0:T(128)}, u32[]{:S(2)}) copy-start(s32[8]{0:T(128)} %constant.179.clone) | copy-start | bytes 100
  9.3 10.7 %copy-start.7 = (s32[16]{0:T(128)S(1)}, s32[16]{0:T(128)}, u32[]{:S(2)}) copy-start(s32[16]{0:T(128)} %constant.180) | copy-start | bytes 196
  11.8 9.6 %copy-start.4 = (s32[256]{0:T(256)S(1)}, s32[256]{0:T(256)}, u32[]{:S(2)}) copy-start(s32[256]{0:T(256)} %param.11) | copy-start | bytes 3076
  11.8 10.8 %copy-start.5 = (s32[16]{0:T(128)S(1)}, s32[16]{0:T(128)}, u32[]{:S(2)}) copy-start(s32[16]{0:T(128)} %constant.178.clone) | copy-start | bytes 196
  11.8 32.7 %all-to-all-start = ((bf16[64,64,256]{2,0,1:T(8,128)(2,1)}), bf16[64,64,256]{2,0,1:T(8,128)(2,1)}, u32[]{:S(2)}, u32[]{:S(2)}) async-start(bf16[64,64,256]{2,0,1:T(8,128)(2,1)} %copy.54), calls=%async_computation | async-start | bytes 4194304 | tf_op jit(solution)/shard_map/all_to_all | solution.py:64
  44.5 3.6 %copy-start.3 = (bf16[2,16,32,512]{3,2,0,1:T(8,128)(2,1)S(1)}, bf16[2,16,32,512]{3,2,0,1:T(8,128)(2,1)}, u32[]{:S(2)}) copy-start(bf16[2,16,32,512]{3,2,0,1:T(8,128)(2,1)} %pad_maximum_fusion) | copy-start | bytes 3145732
  65.8 27.8 %all-to-all-start.1 = ((bf16[128,8,512]{2,1,0:T(8,128)(2,1)}), bf16[128,8,512]{2,1,0:T(8,128)(2,1)S(1)}, u32[]{:S(2)}, u32[]{:S(2)}) async-start(bf16[128,8,512]{2,1,0:T(8,128)(2,1)} %bitcast.13), calls=%async_computation.1 | async-start | bytes 2097152 | tf_op jit(solution)/shard_map/all_to_all | solution.py:119
  94.6 2.1 %copy-start.2 = (f32[1024,64]{1,0:T(8,128)S(1)}, f32[1024,64]{1,0:T(8,128)}, u32[]{:S(2)}) copy-start(f32[1024,64]{1,0:T(8,128)} %maximum_maximum_fusion.1) | copy-start | bytes 786436
  97.8 12.9 %all-to-all-start.2 = ((bf16[16,2,32,128]{3,2,1,0:T(8,128)(2,1)}), bf16[16,2,32,128]{3,2,1,0:T(8,128)(2,1)S(1)}, u32[]{:S(2)}, u32[]{:S(2)}) async-start(bf16[16,2,32,128]{3,2,1,0:T(8,128)(2,1)} %copy.59), calls=%async_computation.2 | async-start | bytes 524288 | tf_op jit(solution)/shard_map/all_to_all | solution.py:162

commit v7 on v6

--- a/solution.py
+++ b/solution.py
@@ -61,8 +61,9 @@
     fitted = jnp.einsum("rce,ep->rcp", fit_weights, eigen_flats, precision=lax.Precision.HIGH)
     flattened = (scaled - fitted).astype(jnp.bfloat16)
 
-    gathered = lax.all_to_all(flattened, "srow", split_axis=1, concat_axis=0, tiled=True)
-    cols_here = gathered.shape[1]
+    cols_here = local_cols // n_srow
+    flattened = flattened.reshape(local_rows, n_srow, cols_here * n_pix).transpose(1, 0, 2)
+    gathered = lax.all_to_all(flattened, "srow", split_axis=0, concat_axis=0, tiled=True)
 
     k_blk = row_count // n_scol
     j_blk = col_count // n_srow

time: 122 us -> 124 us (1.016)
  matrix products: 17.4 us -> 20.3 us
    reshape x0 -> x2, local copies, waits for them, and re-layouts: none -> 5.36 us  [on_device(): flattened.reshape(local_rows, n_srow, cols_here * n_pix).transpose(1, 0, 2)]
    all_to_all x1 -> x0, local copies, waits for them, and re-layouts: 2.95 us -> none  [on_device(): lax.all_to_all(flattened, 'srow', split_axis=1, concat_axis=0, tiled=True)]
    convert_element_type x1 -> x0, local copies, waits for them, and re-layouts: 2.5 us -> none  [on_device(): flattened = (scaled - fitted).astype(jnp.bfloat16)]
    dot_general x1, matrix products: 4.28 us -> 6.2 us  [on_device(): jnp.dot(forward_rows.astype(jnp.bfloat16), gathered.reshape(row_count, co...]
where the time goes in v7:
time: 124 us
  waiting for transfers between devices  40.3 us (32%)
  matrix products  20.3 us (16%)
  starting transfers between devices  18.9 us (15%)
  other arithmetic  18.1 us (15%)
  local copies, waits for them, and re-layouts  16.7 us (13%)
  blocking collectives  8.97 us (7%)
    all_to_all x1, waiting for transfers between devices, on_device(): lax.all_to_all(flattened, 'srow', split_axis=0, concat_axis=0, tiled=True)  18.2 us
    all_to_all x1, waiting for transfers between devices, on_device(): lax.all_to_all(summed, ('scol', 'srow'), split_axis=0, concat_axis=0, til...  13.9 us
    all_to_all x1, blocking collectives, on_device(): lax.all_to_all(image.astype(jnp.bfloat16), 'srow', split_axis=0, concat_a...  8.97 us
    all_to_all x1, starting transfers between devices, on_device(): lax.all_to_all(summed, ('scol', 'srow'), split_axis=0, concat_axis=0, til...  8.8 us
    all_to_all x1, waiting for transfers between devices, on_device(): lax.all_to_all(half.astype(jnp.bfloat16), 'scol', split_axis=0, concat_ax...  8.13 us
    reshape x1, local copies, waits for them, and re-layouts, on_device(): spec = spec.reshape(n_scol, 2 * k_blk * cols_here, n_pix)  7.44 us
    all_to_all x1, starting transfers between devices, on_device(): lax.all_to_all(flattened, 'srow', split_axis=0, concat_axis=0, tiled=True)  6.57 us
    dot_general x1, matrix products, on_device(): jnp.dot(forward_rows.astype(jnp.bfloat16), gathered.reshape(row_count, co...  6.2 us
  transfers between devices with their start and end apart: 3, of which 3 were waited for; matrix products, arithmetic and copies ran while one was open for 11% of the time, Pallas kernels for 0%

profile of v7, /device:TPU:0, one launch (start us, length us, event | category | flops | bytes accessed | tf_op | source)
XLA Modules:
  0.0 123.6 jit_solution(17596411751458873173)
XLA Ops:
  0.0 0.0 copy-start
  0.0 2.2 %convert_reduce_fusion = f32[64,64]{1,0:T(8,128)S(1)} fusion(bf16[64,64,256]{2,1,0:T(8,128)(2,1)} %param.8), kind=kLoop, calls=%fused_computation.1 | loop fusion | flops 2093056 | bytes 2113536 | tf_op jit(solution)/shard_map/reduce_sum | solution.py:58
  2.2 0.0 copy-done
  2.2 0.0 copy-start.1
  2.3 0.0 copy-start.7
  2.3 4.2 %fusion.3 = f32[64,64,16]{1,2,0:T(8,128)S(1)} fusion(bf16[64,64,256]{2,1,0:T(8,128)(2,1)} %param.8, f32[64,64]{1,0:T(8,128)S(1)} %broadcast_multiply_fusion.1, f32[256]{0:T(256)} %param.9, f32[16,256]{1,0:T(8,128)S(1)} %copy-done), kind=kOutput, calls=%fused_computation.11 | convolution fusion | flops 103809024 | bytes 2393088 | tf_op jit(solution)/shard_map/rcp,ep->rce/dot_general | solution.py:60
  6.5 0.0 copy-done.1
  6.5 0.0 copy-done.7
  6.5 3.8 %subtract_convert_fusion = bf16[64,64,256]{2,1,0:T(8,128)(2,1)} fusion(bf16[64,64,256]{2,1,0:T(8,128)(2,1)S(1)} %copy-done.1, f32[64,64,16]{1,2,0:T(8,128)S(1)} %fusion.3, f32[64,64]{1,0:T(8,128)S(1)} %broadcast_multiply_fusion.1, f32[256]{0:T(256)S(1)} %copy-done.7, f32[16,256]{1,0:T(8,128)S(1)} %copy-done), kind=kOutput, calls=%fused_computation.8 | convolution fusion | flops 105906176 | bytes 4490240 | tf_op jit(solution)/shard_map/rce,ep->rcp/dot_general | solution.py:61
  10.3 2.9 %reshape.431 = bf16[64,8,2048]{2,1,0:T(8,128)(2,1)S(1)} reshape(bf16[64,64,256]{2,1,0:T(8,128)(2,1)} %subtract_convert_fusion) | data formatting | bytes 4194304 | tf_op jit(solution)/shard_map/reshape | solution.py:65
  13.2 0.0 copy-start.5
  13.2 0.0 copy-start.6
  13.2 2.5 %copy.71 = bf16[64,8,2048]{2,0,1:T(8,128)(2,1)} copy(bf16[64,8,2048]{2,1,0:T(8,128)(2,1)S(1)} %reshape.431) | data formatting | bytes 4194304 | tf_op jit(solution)/shard_map/reshape | solution.py:65
  15.7 0.0 copy-start.3
  15.7 0.0 copy-start.4
  15.7 6.6 %all-to-all-start = ((bf16[8,64,2048]{2,1,0:T(8,128)(2,1)}), bf16[8,64,2048]{2,1,0:T(8,128)(2,1)}, u32[]{:S(2)}, u32[]{:S(2)}) async-start(bf16[8,64,2048]{2,1,0:T(8,128)(2,1)} %bitcast.106), calls=%async_computation | async-start | bytes 4194304 | tf_op jit(solution)/shard_map/all_to_all | solution.py:66
  22.3 1.0 fusion.33
  23.3 0.2 fusion.60
  23.5 0.2 copy.49
  23.6 0.1 copy.50
  23.8 0.0 copy-done.5
  23.8 0.1 iota_add_fusion.1
  23.9 0.0 copy-done.6
  23.9 1.4 %subtract_convert_fusion.2 = (bf16[512,4,128]{2,1,0:T(4,128)(2,1)S(1)}, bf16[512,4,128]{2,1,0:T(4,128)(2,1)S(1)}) fusion(f32[512,128]{1,0:T(8,128)S(1)} %get-tuple-element.31, f32[512,4]{1,0:T(8,128)S(1)} %copy.50, f32[512,128]{1,0:T(8,128)S(1)} %get-tuple-element.32, f32[512,4]{1,0:T(8,128)S(1)} %copy.49), kind=kLoop, calls=%fused_computation.30 | loop fusion | flops 2359296 | bytes 1589248 | tf_op jit(solution)/shard_map/convert.3
  25.3 0.0 copy-done.3
  25.3 0.6 dynamic_slice.3
  25.9 0.2 neg.22
  26.1 0.2 sub.156
  26.3 0.1 copy.48
  26.4 0.0 copy-done.4
  26.4 0.1 iota_add_fusion
  26.5 0.1 subtract_multiply_fusion
  26.6 0.1 subtract_multiply_fusion.1
  26.8 1.2 subtract_convert_fusion.1
  28.0 0.7 fusion.67
  28.7 0.3 fusion.43
  29.0 1.1 pad_maximum_fusion
  30.2 18.2 %all-to-all-done = bf16[8,64,2048]{2,1,0:T(8,128)(2,1)} async-done(((bf16[8,64,2048]{2,1,0:T(8,128)(2,1)}), bf16[8,64,2048]{2,1,0:T(8,128)(2,1)}, u32[]{:S(2)}, u32[]{:S(2)}) %all-to-all-start) | async-done | bytes 2097184 | tf_op jit(solution)/shard_map/all_to_all | solution.py:66
  48.4 6.2 %convolution_convert_fusion = bf16[1024,2048]{1,0:T(8,128)(2,1)} fusion(bf16[1024,512]{1,0:T(8,128)(2,1)} %bitcast.111, bf16[512,2048]{1,0:T(8,128)(2,1)} %bitcast.11), kind=kOutput, calls=%fused_computation.10 | convolution fusion | flops 2149580800 | bytes 7340032 | tf_op jit(solution)/shard_map/dot_general | solution.py:74
  54.6 7.4 %reshape.433 = bf16[16,512,256]{2,1,0:T(8,128)(2,1)} reshape(bf16[1024,2048]{1,0:T(8,128)(2,1)} %convolution_convert_fusion) | data formatting | bytes 8388608 | tf_op jit(solution)/shard_map/reshape | solution.py:79
  62.0 3.5 %fusion.68 = f32[16,256,512]{2,1,0:T(8,128)S(1)} fusion(bf16[16,256,256]{2,1,0:T(8,128)(2,1)S(1)} %subtract_convert_fusion.1, bf16[16,512,256]{2,1,0:T(8,128)(2,1)} %reshape.433), kind=kOutput, calls=%fused_computation.146 | convolution fusion | flops 1073741824 | bytes 14680064 | tf_op jit(solution)/shard_map/axp,anp->axn/dot_general | solution.py:114
  65.5 2.5 %select_reduce_fusion = bf16[16,64,512]{2,1,0:T(8,128)(2,1)} fusion(f32[16,4,64,512]{3,2,1,0:T(8,128)S(1)} %bitcast.107, pred[16,4,512]{2,1,0:T(4,128)(4,1)S(1)} %iota_compare_fusion), kind=kLoop, calls=%fused_computation | loop fusion | flops 3670016 | bytes 9469952 | tf_op jit(solution)/shard_map/reduce_sum | solution.py:117
  68.0 8.8 %all-to-all-start.1 = ((bf16[128,8,512]{2,1,0:T(8,128)(2,1)}), bf16[128,8,512]{2,1,0:T(8,128)(2,1)S(1)}, u32[]{:S(2)}, u32[]{:S(2)}) async-start(bf16[128,8,512]{2,1,0:T(8,128)(2,1)} %bitcast.13), calls=%async_computation.1 | async-start | bytes 2097152 | tf_op jit(solution)/shard_map/all_to_all | solution.py:120
  76.8 1.0 fusion.37
  77.8 1.0 maximum_maximum_fusion.1
  78.8 0.1 fusion.63
  78.9 2.9 %fusion.24 = (f32[128,1024]{0,1:T(8,128)S(1)}, f32[128,1024]{0,1:T(8,128)S(1)}, f32[128,1024]{0,1:T(8,128)}) fusion(s32[128]{0:T(128)S(1)} %get-tuple-element.30), kind=kLoop, calls=%fused_computation.55 | loop fusion | flops 1966080 | bytes 1573376 | tf_op jit(solution)/shard_map/sin | solution.py:16
  81.8 13.9 %all-to-all-done.1 = bf16[128,8,512]{2,1,0:T(8,128)(2,1)S(1)} async-done(((bf16[128,8,512]{2,1,0:T(8,128)(2,1)}), bf16[128,8,512]{2,1,0:T(8,128)(2,1)S(1)}, u32[]{:S(2)}, u32[]{:S(2)}) %all-to-all-start.1) | async-done | bytes 1048608 | tf_op jit(solution)/shard_map/all_to_all | solution.py:120
  95.8 1.0 copy.65
  96.7 0.0 copy-start.2
  96.7 1.2 %fusion.69 = f32[8,2,32,8,2,128]{5,3,4,2,1,0:T(8,128)S(1)} fusion(bf16[8,2,32,8,128,1]{4,3,5,2,1,0:T(8,128)(2,1)S(1)} %bitcast.109, f32[2,128,128,1,1,1]{2,1,0,5,4,3:T(8,128)S(1)} %bitcast.115), kind=kOutput, calls=%fused_computation.147 | convolution fusion | flops 805306368 | bytes 5373952 | tf_op jit(solution)/shard_map/dot_general | solution.py:127
  98.0 0.8 add_reduce_fusion
  98.8 0.0 copy-done.2
  98.8 0.4 fusion.7
  99.2 0.7 copy.55
  99.9 3.5 %all-to-all-start.2 = ((bf16[16,2,32,128]{3,2,1,0:T(8,128)(2,1)}), bf16[16,2,32,128]{3,2,1,0:T(8,128)(2,1)S(1)}, u32[]{:S(2)}, u32[]{:S(2)}) async-start(bf16[16,2,32,128]{3,2,1,0:T(8,128)(2,1)} %copy.55), calls=%async_computation.2 | async-start | bytes 524288 | tf_op jit(solution)/shard_map/all_to_all | solution.py:163
  103.5 1.2 maximum_maximum_fusion
  104.6 8.1 %all-to-all-done.2 = bf16[16,2,32,128]{3,2,1,0:T(8,128)(2,1)S(1)} async-done(((bf16[16,2,32,128]{3,2,1,0:T(8,128)(2,1)}), bf16[16,2,32,128]{3,2,1,0:T(8,128)(2,1)S(1)}, u32[]{:S(2)}, u32[]{:S(2)}) %all-to-all-start.2) | async-done | bytes 262176 | tf_op jit(solution)/shard_map/all_to_all | solution.py:163
  112.9 1.0 fusion.8
  113.9 9.0 %all_to_all.20 = bf16[8,32,2,128]{3,1,2,0:T(8,128)(2,1)S(1)} all-to-all(bf16[8,32,2,128]{3,1,2,0:T(8,128)(2,1)S(1)} %copy.58), channel_id=1, replica_groups=mesh['srow'=8,'scol'=16] {'srow'}, dimensions={0} | all-to-all | bytes 262144 | tf_op jit(solution)/shard_map/all_to_all | solution.py:179
  123.0 0.6 copy.60
  (20 shorter events, 0.3 us)
Async XLA Ops:
  0.0 2.2 %copy-start = (f32[16,256]{1,0:T(8,128)S(1)}, f32[16,256]{1,0:T(8,128)}, u32[]{:S(2)}) copy-start(f32[16,256]{1,0:T(8,128)} %param.10) | copy-start | bytes 49156
  2.2 4.2 %copy-start.1 = (bf16[64,64,256]{2,1,0:T(8,128)(2,1)S(1)}, bf16[64,64,256]{2,1,0:T(8,128)(2,1)}, u32[]{:S(2)}) copy-start(bf16[64,64,256]{2,1,0:T(8,128)(2,1)} %param.8) | copy-start | bytes 6291460
  2.3 4.2 %copy-start.7 = (f32[256]{0:T(256)S(1)}, f32[256]{0:T(256)}, u32[]{:S(2)}) copy-start(f32[256]{0:T(256)} %param.9) | copy-start | bytes 3076
  13.2 10.6 %copy-start.5 = (s32[8]{0:T(128)S(1)}, s32[8]{0:T(128)}, u32[]{:S(2)}) copy-start(s32[8]{0:T(128)} %constant.179.clone) | copy-start | bytes 100
  13.2 10.7 %copy-start.6 = (s32[16]{0:T(128)S(1)}, s32[16]{0:T(128)}, u32[]{:S(2)}) copy-start(s32[16]{0:T(128)} %constant.180) | copy-start | bytes 196
  15.7 9.6 %copy-start.3 = (s32[256]{0:T(256)S(1)}, s32[256]{0:T(256)}, u32[]{:S(2)}) copy-start(s32[256]{0:T(256)} %param.11) | copy-start | bytes 3076
  15.7 10.8 %copy-start.4 = (s32[16]{0:T(128)S(1)}, s32[16]{0:T(128)}, u32[]{:S(2)}) copy-start(s32[16]{0:T(128)} %constant.178.clone) | copy-start | bytes 196
  15.7 32.7 %all-to-all-start = ((bf16[8,64,2048]{2,1,0:T(8,128)(2,1)}), bf16[8,64,2048]{2,1,0:T(8,128)(2,1)}, u32[]{:S(2)}, u32[]{:S(2)}) async-start(bf16[8,64,2048]{2,1,0:T(8,128)(2,1)} %bitcast.106), calls=%async_computation | async-start | bytes 4194304 | tf_op jit(solution)/shard_map/all_to_all | solution.py:66
  68.0 27.8 %all-to-all-start.1 = ((bf16[128,8,512]{2,1,0:T(8,128)(2,1)}), bf16[128,8,512]{2,1,0:T(8,128)(2,1)S(1)}, u32[]{:S(2)}, u32[]{:S(2)}) async-start(bf16[128,8,512]{2,1,0:T(8,128)(2,1)} %bitcast.13), calls=%async_computation.1 | async-start | bytes 2097152 | tf_op jit(solution)/shard_map/all_to_all | solution.py:120
  96.7 2.1 %copy-start.2 = (f32[1024,64]{1,0:T(8,128)S(1)}, f32[1024,64]{1,0:T(8,128)}, u32[]{:S(2)}) copy-start(f32[1024,64]{1,0:T(8,128)} %maximum_maximum_fusion.1) | copy-start | bytes 786436
  99.9 12.9 %all-to-all-start.2 = ((bf16[16,2,32,128]{3,2,1,0:T(8,128)(2,1)}), bf16[16,2,32,128]{3,2,1,0:T(8,128)(2,1)S(1)}, u32[]{:S(2)}, u32[]{:S(2)}) async-start(bf16[16,2,32,128]{3,2,1,0:T(8,128)(2,1)} %copy.55), calls=%async_computation.2 | async-start | bytes 524288 | tf_op jit(solution)/shard_map/all_to_all | solution.py:163

commit v8 on v6

--- a/solution.py
+++ b/solution.py
@@ -114,7 +114,7 @@
     every_dx = every_dx.reshape(n_scol, n_dx, n_srow * n_dyl, 2 * k_blk * cols_here)
     dx_pick = dx_of_n[:, None, :, :] == jnp.arange(n_dx, dtype=jnp.int32)[None, :, None, None]
     summed = jnp.sum(jnp.where(dx_pick, every_dx, 0.0), axis=1)
-    summed = summed.reshape(n_dev, n_dyl, 2 * k_blk * cols_here).astype(jnp.bfloat16)
+    summed = summed.reshape(n_dev, 2 * n_dyl, k_blk * cols_here).astype(jnp.bfloat16)
 
     summed = lax.all_to_all(summed, ("scol", "srow"), split_axis=0, concat_axis=0, tiled=True)
 

time: 122 us -> 122 us (level)
  no operation moved by 1% of the time
where the time goes in v8:
time: 122 us
  waiting for transfers between devices  40.3 us (33%)
  starting transfers between devices  18.9 us (15%)
  local copies, waits for them, and re-layouts  18.6 us (15%)
  matrix products  17.4 us (14%)
  other arithmetic  17 us (14%)
  blocking collectives  8.97 us (7%)
    all_to_all x1, waiting for transfers between devices, on_device(): lax.all_to_all(flattened, 'srow', split_axis=1, concat_axis=0, tiled=True)  18.3 us
    all_to_all x1, waiting for transfers between devices, on_device(): lax.all_to_all(summed, ('scol', 'srow'), split_axis=0, concat_axis=0, til...  13.9 us
    all_to_all x1, blocking collectives, on_device(): lax.all_to_all(image.astype(jnp.bfloat16), 'srow', split_axis=0, concat_a...  8.97 us
    all_to_all x1, starting transfers between devices, on_device(): lax.all_to_all(summed, ('scol', 'srow'), split_axis=0, concat_axis=0, til...  8.8 us
    all_to_all x1, waiting for transfers between devices, on_device(): lax.all_to_all(half.astype(jnp.bfloat16), 'scol', split_axis=0, concat_ax...  8.13 us
    reshape x1, local copies, waits for them, and re-layouts, on_device(): spec = spec.reshape(n_scol, 2 * k_blk * cols_here, n_pix)  7.42 us
    all_to_all x1, starting transfers between devices, on_device(): lax.all_to_all(flattened, 'srow', split_axis=1, concat_axis=0, tiled=True)  6.57 us
    dot_general x1, matrix products, on_device(): jnp.dot(forward_rows.astype(jnp.bfloat16), gathered.reshape(row_count, co...  4.28 us
  transfers between devices with their start and end apart: 3, of which 3 were waited for; matrix products, arithmetic and copies ran while one was open for 11% of the time, Pallas kernels for 0%

profile of v8, /device:TPU:0, one launch (start us, length us, event | category | flops | bytes accessed | tf_op | source)
XLA Modules:
  0.0 121.5 jit_solution(13874198190565075990)
XLA Ops:
  0.0 0.0 copy-start
  0.0 2.2 %convert_reduce_fusion = f32[64,64]{1,0:T(8,128)S(1)} fusion(bf16[64,64,256]{2,1,0:T(8,128)(2,1)} %param.8), kind=kLoop, calls=%fused_computation.1 | loop fusion | flops 2093056 | bytes 2113536 | tf_op jit(solution)/shard_map/reduce_sum | solution.py:58
  2.2 0.0 copy-done
  2.2 0.0 copy-start.1
  2.3 0.0 copy-start.8
  2.3 4.2 %fusion.3 = f32[64,64,16]{1,2,0:T(8,128)S(1)} fusion(bf16[64,64,256]{2,1,0:T(8,128)(2,1)} %param.8, f32[64,64]{1,0:T(8,128)S(1)} %broadcast_multiply_fusion.1, f32[256]{0:T(256)} %param.9, f32[16,256]{1,0:T(8,128)S(1)} %copy-done), kind=kOutput, calls=%fused_computation.11 | convolution fusion | flops 103809024 | bytes 2393088 | tf_op jit(solution)/shard_map/rcp,ep->rce/dot_general | solution.py:60
  6.5 0.0 copy-done.1
  6.5 0.0 copy-done.8
  6.5 2.8 %subtract_convert_fusion = bf16[64,64,256]{2,1,0:T(8,128)(2,1)S(1)} fusion(bf16[64,64,256]{2,1,0:T(8,128)(2,1)S(1)} %copy-done.1, f32[64,64,16]{1,2,0:T(8,128)S(1)} %fusion.3, f32[64,64]{1,0:T(8,128)S(1)} %broadcast_multiply_fusion.1, f32[256]{0:T(256)S(1)} %copy-done.8, f32[16,256]{1,0:T(8,128)S(1)} %copy-done), kind=kOutput, calls=%fused_computation.8 | convolution fusion | flops 105906176 | bytes 4490240 | tf_op jit(solution)/shard_map/rce,ep->rcp/dot_general | solution.py:61
  9.3 0.0 copy-start.6
  9.3 0.0 copy-start.7
  9.3 2.5 %copy.54 = bf16[64,64,256]{2,0,1:T(8,128)(2,1)} copy(bf16[64,64,256]{2,1,0:T(8,128)(2,1)S(1)} %subtract_convert_fusion) | data formatting | bytes 4194304 | tf_op jit(solution)/shard_map/convert_element_type | solution.py:62
  11.8 0.0 copy-start.4
  11.8 0.0 copy-start.5
  11.8 6.6 %all-to-all-start = ((bf16[64,64,256]{2,0,1:T(8,128)(2,1)}), bf16[64,64,256]{2,0,1:T(8,128)(2,1)}, u32[]{:S(2)}, u32[]{:S(2)}) async-start(bf16[64,64,256]{2,0,1:T(8,128)(2,1)} %copy.54), calls=%async_computation | async-start | bytes 4194304 | tf_op jit(solution)/shard_map/all_to_all | solution.py:64
  18.4 1.0 fusion.33
  19.4 0.2 fusion.60
  19.6 0.2 copy.52
  19.8 0.1 copy.53
  19.9 0.0 copy-done.6
  19.9 0.1 iota_add_fusion.1
  20.0 0.0 copy-done.7
  20.0 1.4 %subtract_convert_fusion.2 = (bf16[512,4,128]{2,1,0:T(4,128)(2,1)S(1)}, bf16[512,4,128]{2,1,0:T(4,128)(2,1)S(1)}) fusion(f32[512,128]{1,0:T(8,128)S(1)} %get-tuple-element.31, f32[512,4]{1,0:T(8,128)S(1)} %copy.53, f32[512,128]{1,0:T(8,128)S(1)} %get-tuple-element.32, f32[512,4]{1,0:T(8,128)S(1)} %copy.52), kind=kLoop, calls=%fused_computation.29 | loop fusion | flops 2359296 | bytes 1589248 | tf_op jit(solution)/shard_map/convert.3
  21.4 0.0 copy-done.4
  21.5 0.6 dynamic_slice.3
  22.0 0.2 neg.22
  22.2 0.2 sub.156
  22.5 0.1 copy.51
  22.6 0.0 copy-done.5
  22.6 0.1 iota_add_fusion
  22.6 0.1 subtract_multiply_fusion
  22.7 0.1 subtract_multiply_fusion.1
  22.9 1.2 %subtract_convert_fusion.1 = bf16[16,256,256]{2,1,0:T(8,128)(2,1)S(1)} fusion(s32[256,256]{1,0:T(8,128)S(1)} %bitcast.116, s32[16,4,256]{2,1,0:T(4,128)S(1)} %get-tuple-element.12, s32[256,256]{1,0:T(8,128)S(1)} %bitcast.115, s32[16,4,256]{2,1,0:T(4,128)S(1)} %get-tuple-element.11), kind=kLoop, calls=%fused_computation.9 | loop fusion | flops 8388608 | bytes 2752512 | tf_op jit(solution)/shard_map/convert_element_type | solution.py:107
  24.1 0.7 fusion.67
  24.8 0.3 fusion.43
  25.2 1.1 pad_maximum_fusion
  26.3 18.3 %all-to-all-done = bf16[64,64,256]{2,0,1:T(8,128)(2,1)} async-done(((bf16[64,64,256]{2,0,1:T(8,128)(2,1)}), bf16[64,64,256]{2,0,1:T(8,128)(2,1)}, u32[]{:S(2)}, u32[]{:S(2)}) %all-to-all-start) | async-done | bytes 2097184 | tf_op jit(solution)/shard_map/all_to_all | solution.py:64
  44.5 2.9 %copy.55 = bf16[64,8,8,256]{3,2,0,1:T(8,128)(2,1)S(1)} copy(bf16[64,8,8,256]{3,0,2,1:T(8,128)(2,1)} %bitcast.10) | data formatting | bytes 4194304 | tf_op jit(solution)/shard_map/all_to_all | solution.py:64
  47.5 0.7 copy.74
  48.2 0.0 copy-done.3
  48.2 4.3 %convolution_convert_fusion = bf16[1024,2048]{1,0:T(8,128)(2,1)} fusion(bf16[1024,512]{1,0:T(8,128)(2,1)S(1)} %bitcast.113, bf16[512,2048]{1,0:T(8,128)(2,1)S(1)} %bitcast.111), kind=kOutput, calls=%fused_computation.10 | convolution fusion | flops 2149580800 | bytes 7340032 | tf_op jit(solution)/shard_map/dot_general | solution.py:73
  52.5 7.4 %reshape.430 = bf16[16,512,256]{2,1,0:T(8,128)(2,1)} reshape(bf16[1024,2048]{1,0:T(8,128)(2,1)} %convolution_convert_fusion) | data formatting | bytes 8388608 | tf_op jit(solution)/shard_map/reshape | solution.py:78
  59.9 3.5 %fusion.68 = f32[16,256,512]{2,1,0:T(8,128)S(1)} fusion(bf16[16,256,256]{2,1,0:T(8,128)(2,1)S(1)} %subtract_convert_fusion.1, bf16[16,512,256]{2,1,0:T(8,128)(2,1)} %reshape.430), kind=kOutput, calls=%fused_computation.145 | convolution fusion | flops 1073741824 | bytes 14680064 | tf_op jit(solution)/shard_map/axp,anp->axn/dot_general | solution.py:113
  63.4 1.4 %select_reduce_fusion = bf16[16,64,512]{2,1,0:T(8,128)(2,1)S(1)} fusion(f32[16,4,64,512]{3,2,1,0:T(8,128)S(1)} %bitcast.107, pred[16,4,512]{2,1,0:T(4,128)(4,1)S(1)} %iota_compare_fusion), kind=kLoop, calls=%fused_computation | loop fusion | flops 3670016 | bytes 9469952 | tf_op jit(solution)/shard_map/reduce_sum | solution.py:116
  64.8 1.2 convert_element_type.104
  65.9 8.8 %all-to-all-start.1 = ((bf16[128,16,256]{2,1,0:T(8,128)(2,1)}), bf16[128,16,256]{2,1,0:T(8,128)(2,1)S(1)}, u32[]{:S(2)}, u32[]{:S(2)}) async-start(bf16[128,16,256]{2,1,0:T(8,128)(2,1)} %convert_element_type.104), calls=%async_computation.1 | async-start | bytes 2097152 | tf_op jit(solution)/shard_map/all_to_all | solution.py:119
  74.7 1.0 fusion.37
  75.8 1.0 maximum_maximum_fusion.1
  76.8 0.1 fusion.63
  76.8 2.9 %fusion.24 = (f32[128,1024]{0,1:T(8,128)S(1)}, f32[128,1024]{0,1:T(8,128)S(1)}, f32[128,1024]{0,1:T(8,128)}) fusion(s32[128]{0:T(128)S(1)} %get-tuple-element.30), kind=kLoop, calls=%fused_computation.54 | loop fusion | flops 1966080 | bytes 1573376 | tf_op jit(solution)/shard_map/sin | solution.py:16
  79.8 13.9 %all-to-all-done.1 = bf16[128,16,256]{2,1,0:T(8,128)(2,1)S(1)} async-done(((bf16[128,16,256]{2,1,0:T(8,128)(2,1)}), bf16[128,16,256]{2,1,0:T(8,128)(2,1)S(1)}, u32[]{:S(2)}, u32[]{:S(2)}) %all-to-all-start.1) | async-done | bytes 1048608 | tf_op jit(solution)/shard_map/all_to_all | solution.py:119
  93.7 1.0 copy.69
  94.7 0.0 copy-start.2
  94.7 1.2 %fusion.69 = f32[8,2,32,8,2,128]{5,3,4,2,1,0:T(8,128)S(1)} fusion(bf16[8,2,32,8,128,1]{4,3,5,2,1,0:T(8,128)(2,1)S(1)} %bitcast.110, f32[2,128,128,1,1,1]{2,1,0,5,4,3:T(8,128)S(1)} %bitcast.117), kind=kOutput, calls=%fused_computation.146 | convolution fusion | flops 805306368 | bytes 5373952 | tf_op jit(solution)/shard_map/dot_general | solution.py:126
  95.9 0.8 add_reduce_fusion
  96.8 0.0 copy-done.2
  96.8 0.4 fusion.7
  97.1 0.7 copy.59
  97.9 3.5 %all-to-all-start.2 = ((bf16[16,2,32,128]{3,2,1,0:T(8,128)(2,1)}), bf16[16,2,32,128]{3,2,1,0:T(8,128)(2,1)S(1)}, u32[]{:S(2)}, u32[]{:S(2)}) async-start(bf16[16,2,32,128]{3,2,1,0:T(8,128)(2,1)} %copy.59), calls=%async_computation.2 | async-start | bytes 524288 | tf_op jit(solution)/shard_map/all_to_all | solution.py:162
  101.4 1.2 maximum_maximum_fusion
  102.6 8.1 %all-to-all-done.2 = bf16[16,2,32,128]{3,2,1,0:T(8,128)(2,1)S(1)} async-done(((bf16[16,2,32,128]{3,2,1,0:T(8,128)(2,1)}), bf16[16,2,32,128]{3,2,1,0:T(8,128)(2,1)S(1)}, u32[]{:S(2)}, u32[]{:S(2)}) %all-to-all-start.2) | async-done | bytes 262176 | tf_op jit(solution)/shard_map/all_to_all | solution.py:162
  110.8 1.0 fusion.8
  111.9 9.0 %all_to_all.30 = bf16[8,32,2,128]{3,1,2,0:T(8,128)(2,1)S(1)} all-to-all(bf16[8,32,2,128]{3,1,2,0:T(8,128)(2,1)S(1)} %copy.62), channel_id=1, replica_groups=mesh['srow'=8,'scol'=16] {'srow'}, dimensions={0} | all-to-all | bytes 262144 | tf_op jit(solution)/shard_map/all_to_all | solution.py:178
  120.9 0.6 copy.64
  (21 shorter events, 0.3 us)
Async XLA Ops:
  0.0 2.2 %copy-start = (f32[16,256]{1,0:T(8,128)S(1)}, f32[16,256]{1,0:T(8,128)}, u32[]{:S(2)}) copy-start(f32[16,256]{1,0:T(8,128)} %param.10) | copy-start | bytes 49156
  2.2 4.2 %copy-start.1 = (bf16[64,64,256]{2,1,0:T(8,128)(2,1)S(1)}, bf16[64,64,256]{2,1,0:T(8,128)(2,1)}, u32[]{:S(2)}) copy-start(bf16[64,64,256]{2,1,0:T(8,128)(2,1)} %param.8) | copy-start | bytes 6291460
  2.3 4.2 %copy-start.8 = (f32[256]{0:T(256)S(1)}, f32[256]{0:T(256)}, u32[]{:S(2)}) copy-start(f32[256]{0:T(256)} %param.9) | copy-start | bytes 3076
  9.3 10.6 %copy-start.6 = (s32[8]{0:T(128)S(1)}, s32[8]{0:T(128)}, u32[]{:S(2)}) copy-start(s32[8]{0:T(128)} %constant.179.clone) | copy-start | bytes 100
  9.3 10.7 %copy-start.7 = (s32[16]{0:T(128)S(1)}, s32[16]{0:T(128)}, u32[]{:S(2)}) copy-start(s32[16]{0:T(128)} %constant.180) | copy-start | bytes 196
  11.8 9.6 %copy-start.4 = (s32[256]{0:T(256)S(1)}, s32[256]{0:T(256)}, u32[]{:S(2)}) copy-start(s32[256]{0:T(256)} %param.11) | copy-start | bytes 3076
  11.8 10.8 %copy-start.5 = (s32[16]{0:T(128)S(1)}, s32[16]{0:T(128)}, u32[]{:S(2)}) copy-start(s32[16]{0:T(128)} %constant.178.clone) | copy-start | bytes 196
  11.8 32.7 %all-to-all-start = ((bf16[64,64,256]{2,0,1:T(8,128)(2,1)}), bf16[64,64,256]{2,0,1:T(8,128)(2,1)}, u32[]{:S(2)}, u32[]{:S(2)}) async-start(bf16[64,64,256]{2,0,1:T(8,128)(2,1)} %copy.54), calls=%async_computation | async-start | bytes 4194304 | tf_op jit(solution)/shard_map/all_to_all | solution.py:64
  44.5 3.6 %copy-start.3 = (bf16[2,16,32,512]{3,2,0,1:T(8,128)(2,1)S(1)}, bf16[2,16,32,512]{3,2,0,1:T(8,128)(2,1)}, u32[]{:S(2)}) copy-start(bf16[2,16,32,512]{3,2,0,1:T(8,128)(2,1)} %pad_maximum_fusion) | copy-start | bytes 3145732
  65.9 27.8 %all-to-all-start.1 = ((bf16[128,16,256]{2,1,0:T(8,128)(2,1)}), bf16[128,16,256]{2,1,0:T(8,128)(2,1)S(1)}, u32[]{:S(2)}, u32[]{:S(2)}) async-start(bf16[128,16,256]{2,1,0:T(8,128)(2,1)} %convert_element_type.104), calls=%async_computation.1 | async-start | bytes 2097152 | tf_op jit(solution)/shard_map/all_to_all | solution.py:119
  94.7 2.1 %copy-start.2 = (f32[1024,64]{1,0:T(8,128)S(1)}, f32[1024,64]{1,0:T(8,128)}, u32[]{:S(2)}) copy-start(f32[1024,64]{1,0:T(8,128)} %maximum_maximum_fusion.1) | copy-start | bytes 786436
  97.9 12.9 %all-to-all-start.2 = ((bf16[16,2,32,128]{3,2,1,0:T(8,128)(2,1)}), bf16[16,2,32,128]{3,2,1,0:T(8,128)(2,1)S(1)}, u32[]{:S(2)}, u32[]{:S(2)}) async-start(bf16[16,2,32,128]{3,2,1,0:T(8,128)(2,1)} %copy.59), calls=%async_computation.2 | async-start | bytes 524288 | tf_op jit(solution)/shard_map/all_to_all | solution.py:162

commit v9 on v6

--- a/solution.py
+++ b/solution.py
@@ -56,10 +56,15 @@
 
     readings = frames.astype(jnp.float32)
     exposure = jnp.mean(readings, axis=2, keepdims=True)
-    scaled = readings * pixel_gain / exposure
-    fit_weights = jnp.einsum("rcp,ep->rce", scaled, eigen_flats, precision=lax.Precision.HIGH)
-    fitted = jnp.einsum("rce,ep->rcp", fit_weights, eigen_flats, precision=lax.Precision.HIGH)
-    flattened = (scaled - fitted).astype(jnp.bfloat16)
+    gram = jnp.dot(eigen_flats.T, eigen_flats, precision=HIGHEST, preferred_element_type=jnp.float32)
+    project = pixel_gain[:, None] * (jnp.eye(n_pix, dtype=jnp.float32) - gram)
+    project_hi = lax.reduce_precision(project, exponent_bits=8, mantissa_bits=7)
+    project_lo = (project - project_hi).astype(jnp.bfloat16)
+    rows_in = frames.reshape(local_rows * local_cols, n_pix)
+    corrected = jnp.dot(
+        rows_in, project_hi.astype(jnp.bfloat16), preferred_element_type=jnp.float32
+    ) + jnp.dot(rows_in, project_lo, preferred_element_type=jnp.float32)
+    flattened = (corrected.reshape(local_rows, local_cols, n_pix) / exposure).astype(jnp.bfloat16)
 
     gathered = lax.all_to_all(flattened, "srow", split_axis=1, concat_axis=0, tiled=True)
     cols_here = gathered.shape[1]

time: 122 us -> 130 us (1.066)
  local copies, waits for them, and re-layouts: 17.4 us -> 23.1 us
  other arithmetic: 18.1 us -> 20.8 us
    add x0 -> x1, local copies, waits for them, and re-layouts: none -> 5.61 us  [on_device(): jnp.dot(rows_in, project_hi.astype(jnp.bfloat16), preferred_element_type=...]
    convert_element_type x0 -> x1, other arithmetic: none -> 2.59 us  [on_device(): (corrected.reshape(local_rows, local_cols, n_pix) / exposure).astype(jnp....]
    dot_general x2 -> x3, matrix products: 6.99 us -> 6.17 us  [the longest x1 2.71 us: on_device(): jnp.dot(rows_in, project_lo, preferred_element_type=jnp.float32)]
where the time goes in v9:
time: 130 us; the launch traced here: 129 us
  waiting for transfers between devices  40.3 us (31%)
  local copies, waits for them, and re-layouts  23.1 us (18%)
  other arithmetic  20.8 us (16%)
  starting transfers between devices  18.9 us (15%)
  matrix products  16.5 us (13%)
  blocking collectives  8.97 us (7%)
    all_to_all x1, waiting for transfers between devices, on_device(): lax.all_to_all(flattened, 'srow', split_axis=1, concat_axis=0, tiled=True)  18.3 us
    all_to_all x1, waiting for transfers between devices, on_device(): lax.all_to_all(summed, ('scol', 'srow'), split_axis=0, concat_axis=0, til...  13.9 us
    all_to_all x1, blocking collectives, on_device(): lax.all_to_all(image.astype(jnp.bfloat16), 'srow', split_axis=0, concat_a...  8.97 us
    all_to_all x1, starting transfers between devices, on_device(): lax.all_to_all(summed, ('scol', 'srow'), split_axis=0, concat_axis=0, til...  8.8 us
    all_to_all x1, waiting for transfers between devices, on_device(): lax.all_to_all(half.astype(jnp.bfloat16), 'scol', split_axis=0, concat_ax...  8.13 us
    reshape x1, local copies, waits for them, and re-layouts, on_device(): spec = spec.reshape(n_scol, 2 * k_blk * cols_here, n_pix)  7.44 us
    all_to_all x1, starting transfers between devices, on_device(): lax.all_to_all(flattened, 'srow', split_axis=1, concat_axis=0, tiled=True)  6.56 us
    add x1, local copies, waits for them, and re-layouts, on_device(): jnp.dot(rows_in, project_hi.astype(jnp.bfloat16), preferred_element_type=...  5.61 us
  transfers between devices with their start and end apart: 3, of which 3 were waited for; matrix products, arithmetic and copies ran while one was open for 11% of the time, Pallas kernels for 0%

profile of v9, /device:TPU:0, one launch (start us, length us, event | category | flops | bytes accessed | tf_op | source)
XLA Modules:
  0.0 128.9 jit_solution(6618196249520538278)
XLA Ops:
  0.0 0.0 copy-start
  0.0 0.0 copy-start.1
  0.0 2.4 %convert_reduce_fusion = f32[64,64]{1,0:T(8,128)S(1)} fusion(bf16[64,64,256]{2,1,0:T(8,128)(2,1)} %param.8), kind=kLoop, calls=%fused_computation.8 | loop fusion | flops 2093056 | bytes 2113536 | tf_op jit(solution)/shard_map/reduce_sum | solution.py:58
  2.4 0.0 copy-done
  2.4 1.1 fusion.4
  3.5 2.4 %fusion.32 = f32[256,4096]{1,0:T(8,128)S(1)} fusion(bf16[4096,256]{1,0:T(8,128)(2,1)} %bitcast.112, f32[256,256]{1,0:T(8,128)S(1)} %fusion.4), kind=kOutput, calls=%fused_computation.66 | convolution fusion | flops 537001984 | bytes 6553600 | tf_op jit(solution)/shard_map/dot_general | solution.py:64
  5.8 0.0 copy-done.1
  5.9 2.7 %fusion = f32[4096,256]{0,1:T(8,128)} fusion(f32[256,4096]{1,0:T(8,128)S(1)} %fusion.32, bf16[4096,256]{1,0:T(8,128)(2,1)S(1)} %bitcast.113, f32[256,256]{1,0:T(8,128)S(1)} %fusion.4), kind=kOutput, calls=%fused_computation.2 | convolution fusion | flops 538116096 | bytes 10747904 | tf_op jit(solution)/shard_map/dot_general | solution.py:66
  8.6 5.6 %copy.61 = f32[4096,256]{1,0:T(8,128)} copy(f32[4096,256]{0,1:T(8,128)} %fusion) | data formatting | bytes 8388608 | tf_op jit(solution)/shard_map/add | solution.py:64
  14.2 2.6 %divide_convert_fusion = bf16[64,64,256]{2,1,0:T(8,128)(2,1)S(1)} fusion(f32[64,64,256]{2,1,0:T(8,128)} %bitcast.114, f32[64,64]{1,0:T(8,128)S(1)} %broadcast_multiply_fusion.1), kind=kLoop, calls=%fused_computation.7 | loop fusion | flops 2097152 | bytes 6307840 | tf_op jit(solution)/shard_map/convert_element_type | solution.py:67
  16.8 0.0 copy-start.6
  16.8 0.0 copy-start.7
  16.8 2.5 %copy.62 = bf16[64,64,256]{2,0,1:T(8,128)(2,1)} copy(bf16[64,64,256]{2,1,0:T(8,128)(2,1)S(1)} %divide_convert_fusion) | data formatting | bytes 4194304 | tf_op jit(solution)/shard_map/convert_element_type | solution.py:67
  19.3 0.0 copy-start.4
  19.3 0.0 copy-start.5
  19.3 6.6 %all-to-all-start = ((bf16[64,64,256]{2,0,1:T(8,128)(2,1)}), bf16[64,64,256]{2,0,1:T(8,128)(2,1)}, u32[]{:S(2)}, u32[]{:S(2)}) async-start(bf16[64,64,256]{2,0,1:T(8,128)(2,1)} %copy.62), calls=%async_computation | async-start | bytes 4194304 | tf_op jit(solution)/shard_map/all_to_all | solution.py:69
  25.9 1.0 fusion.33
  26.9 0.2 fusion.58
  27.1 0.2 copy.59
  27.2 0.1 copy.60
  27.4 0.0 copy-done.6
  27.4 0.1 iota_add_fusion.1
  27.5 0.0 copy-done.7
  27.5 1.4 %subtract_convert_fusion.1 = (bf16[512,4,128]{2,1,0:T(4,128)(2,1)S(1)}, bf16[512,4,128]{2,1,0:T(4,128)(2,1)S(1)}) fusion(f32[512,128]{1,0:T(8,128)S(1)} %get-tuple-element.31, f32[512,4]{1,0:T(8,128)S(1)} %copy.60, f32[512,128]{1,0:T(8,128)S(1)} %get-tuple-element.32, f32[512,4]{1,0:T(8,128)S(1)} %copy.59), kind=kLoop, calls=%fused_computation.28 | loop fusion | flops 2359296 | bytes 1589248 | tf_op jit(solution)/shard_map/convert.3
  28.9 0.0 copy-done.4
  28.9 0.6 dynamic_slice.3
  29.5 0.2 neg.22
  29.7 0.2 sub.159
  30.0 0.1 copy.58
  30.1 0.0 copy-done.5
  30.1 0.1 iota_add_fusion
  30.1 0.1 subtract_multiply_fusion
  30.2 0.1 subtract_multiply_fusion.1
  30.4 1.2 subtract_convert_fusion
  31.6 0.7 fusion.65
  32.3 0.3 fusion.43
  32.6 1.1 pad_maximum_fusion
  33.8 18.3 %all-to-all-done = bf16[64,64,256]{2,0,1:T(8,128)(2,1)} async-done(((bf16[64,64,256]{2,0,1:T(8,128)(2,1)}), bf16[64,64,256]{2,0,1:T(8,128)(2,1)}, u32[]{:S(2)}, u32[]{:S(2)}) %all-to-all-start) | async-done | bytes 2097184 | tf_op jit(solution)/shard_map/all_to_all | solution.py:69
  52.0 2.9 %copy.64 = bf16[8,64,8,256]{3,2,1,0:T(8,128)(2,1)S(1)} copy(bf16[8,64,8,256]{3,1,2,0:T(8,128)(2,1)} %bitcast.14) | data formatting | bytes 4194304 | tf_op jit(solution)/shard_map/all_to_all | solution.py:69
  55.0 0.7 copy.84
  55.7 0.0 copy-done.3
  55.7 4.3 %convolution_convert_fusion = bf16[1024,2048]{1,0:T(8,128)(2,1)} fusion(bf16[1024,512]{1,0:T(8,128)(2,1)S(1)} %bitcast.120, bf16[512,2048]{1,0:T(8,128)(2,1)S(1)} %bitcast.118), kind=kOutput, calls=%fused_computation.10 | convolution fusion | flops 2149580800 | bytes 7340032 | tf_op jit(solution)/shard_map/dot_general | solution.py:78
  60.0 7.4 %reshape.438 = bf16[16,512,256]{2,1,0:T(8,128)(2,1)} reshape(bf16[1024,2048]{1,0:T(8,128)(2,1)} %convolution_convert_fusion) | data formatting | bytes 8388608 | tf_op jit(solution)/shard_map/reshape | solution.py:83
  67.4 3.5 %fusion.66 = f32[16,256,512]{2,1,0:T(8,128)S(1)} fusion(bf16[16,256,256]{2,1,0:T(8,128)(2,1)S(1)} %subtract_convert_fusion, bf16[16,512,256]{2,1,0:T(8,128)(2,1)} %reshape.438), kind=kOutput, calls=%fused_computation.147 | convolution fusion | flops 1073741824 | bytes 14680064 | tf_op jit(solution)/shard_map/axp,anp->axn/dot_general | solution.py:118
  70.9 2.5 %select_reduce_fusion = bf16[16,64,512]{2,1,0:T(8,128)(2,1)} fusion(f32[16,4,64,512]{3,2,1,0:T(8,128)S(1)} %bitcast.111, pred[16,4,512]{2,1,0:T(4,128)(4,1)S(1)} %iota_compare_fusion.1), kind=kLoop, calls=%fused_computation | loop fusion | flops 3670016 | bytes 9469952 | tf_op jit(solution)/shard_map/reduce_sum | solution.py:121
  73.3 8.8 %all-to-all-start.1 = ((bf16[128,8,512]{2,1,0:T(8,128)(2,1)}), bf16[128,8,512]{2,1,0:T(8,128)(2,1)S(1)}, u32[]{:S(2)}, u32[]{:S(2)}) async-start(bf16[128,8,512]{2,1,0:T(8,128)(2,1)} %bitcast.16), calls=%async_computation.1 | async-start | bytes 2097152 | tf_op jit(solution)/shard_map/all_to_all | solution.py:124
  82.2 1.0 fusion.37
  83.2 1.0 maximum_maximum_fusion.1
  84.2 0.1 fusion.61
  84.3 2.9 %fusion.22 = (f32[128,1024]{0,1:T(8,128)S(1)}, f32[128,1024]{0,1:T(8,128)S(1)}, f32[128,1024]{0,1:T(8,128)}) fusion(s32[128]{0:T(128)S(1)} %get-tuple-element.30), kind=kLoop, calls=%fused_computation.56 | loop fusion | flops 1966080 | bytes 1573376 | tf_op jit(solution)/shard_map/sin | solution.py:16
  87.2 13.9 %all-to-all-done.1 = bf16[128,8,512]{2,1,0:T(8,128)(2,1)S(1)} async-done(((bf16[128,8,512]{2,1,0:T(8,128)(2,1)}), bf16[128,8,512]{2,1,0:T(8,128)(2,1)S(1)}, u32[]{:S(2)}, u32[]{:S(2)}) %all-to-all-start.1) | async-done | bytes 1048608 | tf_op jit(solution)/shard_map/all_to_all | solution.py:124
  101.1 1.0 copy.79
  102.1 0.0 copy-start.2
  102.1 1.2 fusion.67
  103.4 0.8 add_reduce_fusion
  104.2 0.0 copy-done.2
  104.2 0.4 fusion.3
  104.6 0.7 copy.68
  105.3 3.5 %all-to-all-start.2 = ((bf16[16,2,32,128]{3,2,1,0:T(8,128)(2,1)}), bf16[16,2,32,128]{3,2,1,0:T(8,128)(2,1)S(1)}, u32[]{:S(2)}, u32[]{:S(2)}) async-start(bf16[16,2,32,128]{3,2,1,0:T(8,128)(2,1)} %copy.68), calls=%async_computation.2 | async-start | bytes 524288 | tf_op jit(solution)/shard_map/all_to_all | solution.py:167
  108.8 1.2 maximum_maximum_fusion
  110.0 8.1 %all-to-all-done.2 = bf16[16,2,32,128]{3,2,1,0:T(8,128)(2,1)S(1)} async-done(((bf16[16,2,32,128]{3,2,1,0:T(8,128)(2,1)}), bf16[16,2,32,128]{3,2,1,0:T(8,128)(2,1)S(1)}, u32[]{:S(2)}, u32[]{:S(2)}) %all-to-all-start.2) | async-done | bytes 262176 | tf_op jit(solution)/shard_map/all_to_all | solution.py:167
  118.2 1.0 fusion.5
  119.3 9.0 %all_to_all.30 = bf16[8,32,2,128]{3,1,2,0:T(8,128)(2,1)S(1)} all-to-all(bf16[8,32,2,128]{3,1,2,0:T(8,128)(2,1)S(1)} %copy.71), channel_id=1, replica_groups=mesh['srow'=8,'scol'=16] {'srow'}, dimensions={0} | all-to-all | bytes 262144 | tf_op jit(solution)/shard_map/all_to_all | solution.py:183
  128.3 0.6 copy.73
  (21 shorter events, 0.3 us)
Async XLA Ops:
  0.0 2.4 %copy-start = (f32[16,256]{1,0:T(8,128)S(1)}, f32[16,256]{1,0:T(8,128)}, u32[]{:S(2)}) copy-start(f32[16,256]{1,0:T(8,128)} %param.10) | copy-start | bytes 49156
  0.0 5.8 %copy-start.1 = (bf16[64,64,256]{2,1,0:T(8,128)(2,1)S(1)}, bf16[64,64,256]{2,1,0:T(8,128)(2,1)}, u32[]{:S(2)}) copy-start(bf16[64,64,256]{2,1,0:T(8,128)(2,1)} %param.8) | copy-start | bytes 6291460
  16.8 10.6 %copy-start.6 = (s32[8]{0:T(128)S(1)}, s32[8]{0:T(128)}, u32[]{:S(2)}) copy-start(s32[8]{0:T(128)} %constant.179.clone) | copy-start | bytes 100
  16.8 10.7 %copy-start.7 = (s32[16]{0:T(128)S(1)}, s32[16]{0:T(128)}, u32[]{:S(2)}) copy-start(s32[16]{0:T(128)} %constant.180) | copy-start | bytes 196
  19.3 9.6 %copy-start.4 = (s32[256]{0:T(256)S(1)}, s32[256]{0:T(256)}, u32[]{:S(2)}) copy-start(s32[256]{0:T(256)} %param.11) | copy-start | bytes 3076
  19.3 10.7 %copy-start.5 = (s32[16]{0:T(128)S(1)}, s32[16]{0:T(128)}, u32[]{:S(2)}) copy-start(s32[16]{0:T(128)} %constant.178.clone) | copy-start | bytes 196
  19.3 32.7 %all-to-all-start = ((bf16[64,64,256]{2,0,1:T(8,128)(2,1)}), bf16[64,64,256]{2,0,1:T(8,128)(2,1)}, u32[]{:S(2)}, u32[]{:S(2)}) async-start(bf16[64,64,256]{2,0,1:T(8,128)(2,1)} %copy.62), calls=%async_computation | async-start | bytes 4194304 | tf_op jit(solution)/shard_map/all_to_all | solution.py:69
  52.0 3.6 %copy-start.3 = (bf16[2,16,32,512]{3,2,0,1:T(8,128)(2,1)S(1)}, bf16[2,16,32,512]{3,2,0,1:T(8,128)(2,1)}, u32[]{:S(2)}) copy-start(bf16[2,16,32,512]{3,2,0,1:T(8,128)(2,1)} %pad_maximum_fusion) | copy-start | bytes 3145732
  73.3 27.8 %all-to-all-start.1 = ((bf16[128,8,512]{2,1,0:T(8,128)(2,1)}), bf16[128,8,512]{2,1,0:T(8,128)(2,1)S(1)}, u32[]{:S(2)}, u32[]{:S(2)}) async-start(bf16[128,8,512]{2,1,0:T(8,128)(2,1)} %bitcast.16), calls=%async_computation.1 | async-start | bytes 2097152 | tf_op jit(solution)/shard_map/all_to_all | solution.py:124
  102.1 2.1 %copy-start.2 = (f32[1024,64]{1,0:T(8,128)S(1)}, f32[1024,64]{1,0:T(8,128)}, u32[]{:S(2)}) copy-start(f32[1024,64]{1,0:T(8,128)} %maximum_maximum_fusion.1) | copy-start | bytes 786436
  105.3 12.9 %all-to-all-start.2 = ((bf16[16,2,32,128]{3,2,1,0:T(8,128)(2,1)}), bf16[16,2,32,128]{3,2,1,0:T(8,128)(2,1)S(1)}, u32[]{:S(2)}, u32[]{:S(2)}) async-start(bf16[16,2,32,128]{3,2,1,0:T(8,128)(2,1)} %copy.68), calls=%async_computation.2 | async-start | bytes 524288 | tf_op jit(solution)/shard_map/all_to_all | solution.py:167

commit v10 on v6

--- a/solution.py
+++ b/solution.py
@@ -56,10 +56,10 @@
 
     readings = frames.astype(jnp.float32)
     exposure = jnp.mean(readings, axis=2, keepdims=True)
-    scaled = readings * pixel_gain / exposure
-    fit_weights = jnp.einsum("rcp,ep->rce", scaled, eigen_flats, precision=lax.Precision.HIGH)
-    fitted = jnp.einsum("rce,ep->rcp", fit_weights, eigen_flats, precision=lax.Precision.HIGH)
-    flattened = (scaled - fitted).astype(jnp.bfloat16)
+    gram = jnp.dot(eigen_flats.T, eigen_flats, precision=HIGHEST, preferred_element_type=jnp.float32)
+    project = pixel_gain[:, None] * (jnp.eye(n_pix, dtype=jnp.float32) - gram)
+    corrected = jnp.einsum("rcp,pq->rcq", readings, project, precision=lax.Precision.HIGH)
+    flattened = (corrected / exposure).astype(jnp.bfloat16)
 
     gathered = lax.all_to_all(flattened, "srow", split_axis=1, concat_axis=0, tiled=True)
     cols_here = gathered.shape[1]

time: 122 us -> 118 us (0.967)
  matrix products: 17.4 us -> 12.3 us
    dot_general x2, matrix products: 6.99 us -> 1.87 us  [the longest x1 1.46 us: on_device(): jnp.einsum('rcp,pq->rcq', readings, project, precision=lax.Precision.HIGH)]
  transfers between devices with their start and end apart: 3 -> 3, of which waited for: 3 -> 3; matrix products, arithmetic and copies ran while one was open for 11% -> 12% of each run, Pallas kernels for 0% -> 0%
where the time goes in v10:
time: 118 us; the launch traced here: 117 us
  waiting for transfers between devices  40.3 us (34%)
  starting transfers between devices  18.9 us (16%)
  other arithmetic  18.2 us (15%)
  local copies, waits for them, and re-layouts  18.1 us (15%)
  matrix products  12.3 us (10%)
  blocking collectives  8.97 us (8%)
    all_to_all x1, waiting for transfers between devices, on_device(): lax.all_to_all(flattened, 'srow', split_axis=1, concat_axis=0, tiled=True)  18.2 us
    all_to_all x1, waiting for transfers between devices, on_device(): lax.all_to_all(summed, ('scol', 'srow'), split_axis=0, concat_axis=0, til...  13.9 us
    all_to_all x1, blocking collectives, on_device(): lax.all_to_all(image.astype(jnp.bfloat16), 'srow', split_axis=0, concat_a...  8.97 us
    all_to_all x1, starting transfers between devices, on_device(): lax.all_to_all(summed, ('scol', 'srow'), split_axis=0, concat_axis=0, til...  8.79 us
    all_to_all x1, waiting for transfers between devices, on_device(): lax.all_to_all(half.astype(jnp.bfloat16), 'scol', split_axis=0, concat_ax...  8.13 us
    reshape x1, local copies, waits for them, and re-layouts, on_device(): spec = spec.reshape(n_scol, 2 * k_blk * cols_here, n_pix)  7.42 us
    all_to_all x1, starting transfers between devices, on_device(): lax.all_to_all(flattened, 'srow', split_axis=1, concat_axis=0, tiled=True)  6.58 us
    dot_general x1, matrix products, on_device(): jnp.dot(forward_rows.astype(jnp.bfloat16), gathered.reshape(row_count, co...  4.28 us
  transfers between devices with their start and end apart: 3, of which 3 were waited for; matrix products, arithmetic and copies ran while one was open for 12% of the time, Pallas kernels for 0%

profile of v10, /device:TPU:0, one launch (start us, length us, event | category | flops | bytes accessed | tf_op | source)
XLA Modules:
  0.0 117.1 jit_solution(11124761710390192674)
XLA Ops:
  0.0 0.0 copy-start
  0.0 0.0 copy-start.1
  0.0 0.0 copy-start.4
  0.0 2.4 %convert_reduce_fusion = f32[64,64]{1,0:T(8,128)S(1)} fusion(bf16[64,64,256]{2,1,0:T(8,128)(2,1)} %param.8), kind=kLoop, calls=%fused_computation.6 | loop fusion | flops 2093056 | bytes 2113536 | tf_op jit(solution)/shard_map/reduce_sum | solution.py:58
  2.4 0.0 copy-done
  2.4 0.0 copy-done.4
  2.4 0.4 fusion.5
  2.8 0.0 copy-done.1
  2.8 1.5 %fusion.2 = bf16[64,64,256]{2,1,0:T(8,128)(2,1)S(1)} fusion(f32[64,64]{1,0:T(8,128)S(1)} %broadcast_multiply_fusion.1, f32[256,256,1]{1,0,2:T(8,128)S(1)} %fusion.5, bf16[64,64,256]{2,1,0:T(8,128)(2,1)S(1)} %copy-done.1), kind=kOutput, calls=%fused_computation.10 | convolution fusion | flops 1612709888 | bytes 4472832 | tf_op jit(solution)/shard_map/rcp,pq->rcq/dot_general | solution.py:61
  4.3 2.5 %copy.54 = bf16[64,64,256]{2,0,1:T(8,128)(2,1)} copy(bf16[64,64,256]{2,1,0:T(8,128)(2,1)S(1)} %fusion.2) | data formatting | bytes 4194304 | tf_op jit(solution)/shard_map/convert_element_type | solution.py:62
  6.8 0.0 copy-start.7
  6.8 0.0 copy-start.8
  6.8 6.6 %all-to-all-start = ((bf16[64,64,256]{2,0,1:T(8,128)(2,1)}), bf16[64,64,256]{2,0,1:T(8,128)(2,1)}, u32[]{:S(2)}, u32[]{:S(2)}) async-start(bf16[64,64,256]{2,0,1:T(8,128)(2,1)} %copy.54), calls=%async_computation | async-start | bytes 4194304 | tf_op jit(solution)/shard_map/all_to_all | solution.py:64
  13.4 0.0 copy-start.5
  13.4 1.0 fusion.31
  14.5 0.2 fusion.56
  14.6 0.2 copy.52
  14.8 0.1 copy.53
  14.9 0.0 copy-done.7
  14.9 0.1 iota_add_fusion.1
  15.0 0.0 copy-done.8
  15.0 0.0 copy-start.6
  15.0 1.4 %subtract_convert_fusion.1 = (bf16[512,4,128]{2,1,0:T(4,128)(2,1)S(1)}, bf16[512,4,128]{2,1,0:T(4,128)(2,1)S(1)}) fusion(f32[512,128]{1,0:T(8,128)S(1)} %get-tuple-element.31, f32[512,4]{1,0:T(8,128)S(1)} %copy.53, f32[512,128]{1,0:T(8,128)S(1)} %get-tuple-element.32, f32[512,4]{1,0:T(8,128)S(1)} %copy.52), kind=kLoop, calls=%fused_computation.28 | loop fusion | flops 2359296 | bytes 1589248 | tf_op jit(solution)/shard_map/convert.3
  16.4 0.0 copy-done.5
  16.5 0.6 dynamic_slice.3
  17.1 0.2 neg.22
  17.3 0.2 sub.156
  17.5 0.1 copy.51
  17.6 0.0 copy-done.6
  17.6 0.1 iota_add_fusion
  17.7 0.1 subtract_multiply_fusion
  17.8 0.1 subtract_multiply_fusion.1
  17.9 1.2 %subtract_convert_fusion = bf16[16,256,256]{2,1,0:T(8,128)(2,1)S(1)} fusion(s32[256,256]{1,0:T(8,128)S(1)} %bitcast.119, s32[16,4,256]{2,1,0:T(4,128)S(1)} %get-tuple-element.12, s32[256,256]{1,0:T(8,128)S(1)} %bitcast.118, s32[16,4,256]{2,1,0:T(4,128)S(1)} %get-tuple-element.11), kind=kLoop, calls=%fused_computation.7 | loop fusion | flops 8388608 | bytes 2752512 | tf_op jit(solution)/shard_map/convert_element_type | solution.py:107
  19.2 0.7 fusion.63
  19.8 0.3 fusion.41
  20.2 1.1 pad_maximum_fusion
  21.3 18.2 %all-to-all-done = bf16[64,64,256]{2,0,1:T(8,128)(2,1)} async-done(((bf16[64,64,256]{2,0,1:T(8,128)(2,1)}), bf16[64,64,256]{2,0,1:T(8,128)(2,1)}, u32[]{:S(2)}, u32[]{:S(2)}) %all-to-all-start) | async-done | bytes 2097184 | tf_op jit(solution)/shard_map/all_to_all | solution.py:64
  39.5 2.9 %copy.55 = bf16[64,8,8,256]{3,2,0,1:T(8,128)(2,1)S(1)} copy(bf16[64,8,8,256]{3,0,2,1:T(8,128)(2,1)} %bitcast.11) | data formatting | bytes 4194304 | tf_op jit(solution)/shard_map/all_to_all | solution.py:64
  42.4 0.0 copy-start.3
  42.4 0.7 copy.74
  43.1 0.5 copy-done.3
  43.6 4.3 %convolution_convert_fusion = bf16[1024,2048]{1,0:T(8,128)(2,1)} fusion(bf16[1024,512]{1,0:T(8,128)(2,1)S(1)} %bitcast.116, bf16[512,2048]{1,0:T(8,128)(2,1)S(1)} %bitcast.114), kind=kOutput, calls=%fused_computation.8 | convolution fusion | flops 2149580800 | bytes 7340032 | tf_op jit(solution)/shard_map/dot_general | solution.py:73
  47.9 7.4 %reshape.430 = bf16[16,512,256]{2,1,0:T(8,128)(2,1)} reshape(bf16[1024,2048]{1,0:T(8,128)(2,1)} %convolution_convert_fusion) | data formatting | bytes 8388608 | tf_op jit(solution)/shard_map/reshape | solution.py:78
  55.3 3.5 %fusion.64 = f32[16,256,512]{2,1,0:T(8,128)S(1)} fusion(bf16[16,256,256]{2,1,0:T(8,128)(2,1)S(1)} %subtract_convert_fusion, bf16[16,512,256]{2,1,0:T(8,128)(2,1)} %reshape.430), kind=kOutput, calls=%fused_computation.143 | convolution fusion | flops 1073741824 | bytes 14680064 | tf_op jit(solution)/shard_map/axp,anp->axn/dot_general | solution.py:113
  58.8 2.5 %select_reduce_fusion = bf16[16,64,512]{2,1,0:T(8,128)(2,1)} fusion(f32[16,4,64,512]{3,2,1,0:T(8,128)S(1)} %bitcast.110, pred[16,4,512]{2,1,0:T(4,128)(4,1)S(1)} %iota_compare_fusion.1), kind=kLoop, calls=%fused_computation | loop fusion | flops 3670016 | bytes 9469952 | tf_op jit(solution)/shard_map/reduce_sum | solution.py:116
  61.3 8.8 %all-to-all-start.1 = ((bf16[128,8,512]{2,1,0:T(8,128)(2,1)}), bf16[128,8,512]{2,1,0:T(8,128)(2,1)S(1)}, u32[]{:S(2)}, u32[]{:S(2)}) async-start(bf16[128,8,512]{2,1,0:T(8,128)(2,1)} %bitcast.14), calls=%async_computation.1 | async-start | bytes 2097152 | tf_op jit(solution)/shard_map/all_to_all | solution.py:119
  70.1 1.0 fusion.35
  71.1 1.0 maximum_maximum_fusion.1
  72.1 0.1 fusion.59
  72.2 2.9 %fusion.22 = (f32[128,1024]{0,1:T(8,128)S(1)}, f32[128,1024]{0,1:T(8,128)S(1)}, f32[128,1024]{0,1:T(8,128)}) fusion(s32[128]{0:T(128)S(1)} %get-tuple-element.30), kind=kLoop, calls=%fused_computation.53 | loop fusion | flops 1966080 | bytes 1573376 | tf_op jit(solution)/shard_map/sin | solution.py:16
  75.1 13.9 %all-to-all-done.1 = bf16[128,8,512]{2,1,0:T(8,128)(2,1)S(1)} async-done(((bf16[128,8,512]{2,1,0:T(8,128)(2,1)}), bf16[128,8,512]{2,1,0:T(8,128)(2,1)S(1)}, u32[]{:S(2)}, u32[]{:S(2)}) %all-to-all-start.1) | async-done | bytes 1048608 | tf_op jit(solution)/shard_map/all_to_all | solution.py:119
  89.0 1.0 copy.69
  90.0 1.2 %fusion.65 = f32[8,2,32,8,2,128]{5,3,4,2,1,0:T(8,128)S(1)} fusion(bf16[8,2,32,8,128,1]{4,3,5,2,1,0:T(8,128)(2,1)S(1)} %bitcast.113, f32[2,128,128,1,1,1]{2,1,0,5,4,3:T(8,128)S(1)} %bitcast.120), kind=kOutput, calls=%fused_computation.144 | convolution fusion | flops 805306368 | bytes 5373952 | tf_op jit(solution)/shard_map/dot_general | solution.py:126
  91.3 0.0 copy-start.2
  91.3 0.8 add_reduce_fusion
  92.1 0.2 copy-done.2
  92.3 0.4 fusion.3
  92.7 0.7 copy.59
  93.4 3.5 %all-to-all-start.2 = ((bf16[16,2,32,128]{3,2,1,0:T(8,128)(2,1)}), bf16[16,2,32,128]{3,2,1,0:T(8,128)(2,1)S(1)}, u32[]{:S(2)}, u32[]{:S(2)}) async-start(bf16[16,2,32,128]{3,2,1,0:T(8,128)(2,1)} %copy.59), calls=%async_computation.2 | async-start | bytes 524288 | tf_op jit(solution)/shard_map/all_to_all | solution.py:162
  96.9 1.2 %maximum_maximum_fusion = f32[256,2048]{0,1:T(8,128)S(1)} fusion(f32[128,1024]{0,1:T(8,128)S(1)} %get-tuple-element.27, f32[128,1024]{0,1:T(8,128)} %get-tuple-element.28, f32[128,1024]{0,1:T(8,128)S(1)} %get-tuple-element.26), kind=kLoop, calls=%fused_computation.9 | loop fusion | flops 1572864 | bytes 3670016 | tf_op jit(solution)/shard_map/concatenate | solution.py:168
  98.1 8.1 %all-to-all-done.2 = bf16[16,2,32,128]{3,2,1,0:T(8,128)(2,1)S(1)} async-done(((bf16[16,2,32,128]{3,2,1,0:T(8,128)(2,1)}), bf16[16,2,32,128]{3,2,1,0:T(8,128)(2,1)S(1)}, u32[]{:S(2)}, u32[]{:S(2)}) %all-to-all-start.2) | async-done | bytes 262176 | tf_op jit(solution)/shard_map/all_to_all | solution.py:162
  106.4 1.0 fusion.6
  107.4 9.0 %all_to_all.30 = bf16[8,32,2,128]{3,1,2,0:T(8,128)(2,1)S(1)} all-to-all(bf16[8,32,2,128]{3,1,2,0:T(8,128)(2,1)S(1)} %copy.62), channel_id=1, replica_groups=mesh['srow'=8,'scol'=16] {'srow'}, dimensions={0} | all-to-all | bytes 262144 | tf_op jit(solution)/shard_map/all_to_all | solution.py:178
  116.4 0.6 copy.64
  (20 shorter events, 0.3 us)
Async XLA Ops:
  0.0 2.4 %copy-start = (f32[16,256]{1,0:T(8,128)S(1)}, f32[16,256]{1,0:T(8,128)}, u32[]{:S(2)}) copy-start(f32[16,256]{1,0:T(8,128)} %param.10) | copy-start | bytes 49156
  0.0 2.8 %copy-start.1 = (bf16[64,64,256]{2,1,0:T(8,128)(2,1)S(1)}, bf16[64,64,256]{2,1,0:T(8,128)(2,1)}, u32[]{:S(2)}) copy-start(bf16[64,64,256]{2,1,0:T(8,128)(2,1)} %param.8) | copy-start | bytes 6291460
  0.0 2.4 %copy-start.4 = (f32[256]{0:T(256)S(1)}, f32[256]{0:T(256)}, u32[]{:S(2)}) copy-start(f32[256]{0:T(256)} %param.9) | copy-start | bytes 3076
  6.8 8.1 %copy-start.7 = (s32[8]{0:T(128)S(1)}, s32[8]{0:T(128)}, u32[]{:S(2)}) copy-start(s32[8]{0:T(128)} %constant.179.clone) | copy-start | bytes 100
  6.8 8.2 %copy-start.8 = (s32[16]{0:T(128)S(1)}, s32[16]{0:T(128)}, u32[]{:S(2)}) copy-start(s32[16]{0:T(128)} %constant.180) | copy-start | bytes 196
  6.8 32.7 %all-to-all-start = ((bf16[64,64,256]{2,0,1:T(8,128)(2,1)}), bf16[64,64,256]{2,0,1:T(8,128)(2,1)}, u32[]{:S(2)}, u32[]{:S(2)}) async-start(bf16[64,64,256]{2,0,1:T(8,128)(2,1)} %copy.54), calls=%async_computation | async-start | bytes 4194304 | tf_op jit(solution)/shard_map/all_to_all | solution.py:64
  13.4 3.1 %copy-start.5 = (s32[256]{0:T(256)S(1)}, s32[256]{0:T(256)}, u32[]{:S(2)}) copy-start(s32[256]{0:T(256)} %param.11) | copy-start | bytes 3076
  15.0 2.6 %copy-start.6 = (s32[16]{0:T(128)S(1)}, s32[16]{0:T(128)}, u32[]{:S(2)}) copy-start(s32[16]{0:T(128)} %constant.178.clone) | copy-start | bytes 196
  42.4 1.2 %copy-start.3 = (bf16[2,16,32,512]{3,2,0,1:T(8,128)(2,1)S(1)}, bf16[2,16,32,512]{3,2,0,1:T(8,128)(2,1)}, u32[]{:S(2)}) copy-start(bf16[2,16,32,512]{3,2,0,1:T(8,128)(2,1)} %pad_maximum_fusion) | copy-start | bytes 3145732
  61.3 27.8 %all-to-all-start.1 = ((bf16[128,8,512]{2,1,0:T(8,128)(2,1)}), bf16[128,8,512]{2,1,0:T(8,128)(2,1)S(1)}, u32[]{:S(2)}, u32[]{:S(2)}) async-start(bf16[128,8,512]{2,1,0:T(8,128)(2,1)} %bitcast.14), calls=%async_computation.1 | async-start | bytes 2097152 | tf_op jit(solution)/shard_map/all_to_all | solution.py:119
  91.3 1.0 copy-start.2
  93.4 12.9 %all-to-all-start.2 = ((bf16[16,2,32,128]{3,2,1,0:T(8,128)(2,1)}), bf16[16,2,32,128]{3,2,1,0:T(8,128)(2,1)S(1)}, u32[]{:S(2)}, u32[]{:S(2)}) async-start(bf16[16,2,32,128]{3,2,1,0:T(8,128)(2,1)} %copy.59), calls=%async_computation.2 | async-start | bytes 524288 | tf_op jit(solution)/shard_map/all_to_all | solution.py:162

commit v11 on v10

--- a/solution.py
+++ b/solution.py
@@ -55,7 +55,8 @@
     flat_index = lax.axis_index("scol") * n_srow + lax.axis_index("srow")
 
     readings = frames.astype(jnp.float32)
-    exposure = jnp.mean(readings, axis=2, keepdims=True)
+    averaging = jnp.full((n_pix, 128), 1.0 / n_pix, dtype=jnp.bfloat16)
+    exposure = jnp.einsum("rcp,pq->rcq", frames, averaging, preferred_element_type=jnp.float32)[:, :, :1]
     gram = jnp.dot(eigen_flats.T, eigen_flats, precision=HIGHEST, preferred_element_type=jnp.float32)
     project = pixel_gain[:, None] * (jnp.eye(n_pix, dtype=jnp.float32) - gram)
     corrected = jnp.einsum("rcp,pq->rcq", readings, project, precision=lax.Precision.HIGH)

time: 118 us -> 123 us (1.042)
  waiting for transfers between devices: 40.3 us -> 33.4 us
  local copies, waits for them, and re-layouts: 18.1 us -> 22.8 us
  matrix products: 12.3 us -> 16.5 us
  other arithmetic: 18.2 us -> 21 us
    all_to_all x1, waiting for transfers between devices: 18.2 us -> 12.9 us  [on_device(): lax.all_to_all(flattened, 'srow', split_axis=1, concat_axis=0, tiled=True)]
    reduce_sum x1 -> x0, other arithmetic: 2.37 us -> none  [on_device(): exposure = jnp.mean(readings, axis=2, keepdims=True)]
    another operation x1, other arithmetic: 1.39 us -> 3.68 us
    unnamed x19 -> x23, local copies, waits for them, and re-layouts: 1.45 us -> 3.11 us
    dot_general x1, matrix products: 1.02 us -> 2.6 us  [on_device(): jnp.dot(half, inverse_cols, precision=lax.Precision.HIGH, preferred_eleme...]
    all_to_all x1, waiting for transfers between devices: 8.13 us -> 6.76 us  [on_device(): lax.all_to_all(half.astype(jnp.bfloat16), 'scol', split_axis=0, concat_ax...]
    concatenate x1, other arithmetic: 1.18 us -> 2.53 us  [on_device(): jnp.concatenate([jnp.concatenate([inv_cos, inv_sin], axis=1), jnp.concate...]
    convert_element_type x1, other arithmetic: 1.22 us -> 2.53 us  [on_device(): (upper.astype(jnp.float32) - lower.astype(jnp.float32)).astype(jnp.bfloat16)]
  transfers between devices with their start and end apart: 3 -> 3, of which waited for: 3 -> 3; matrix products, arithmetic and copies ran while one was open for 12% -> 17% of each run, Pallas kernels for 0% -> 0%
where the time goes in v11:
time: 123 us; the launch traced here: 122 us
  waiting for transfers between devices  33.4 us (27%)
  local copies, waits for them, and re-layouts  22.8 us (19%)
  other arithmetic  21 us (17%)
  starting transfers between devices  18.9 us (15%)
  matrix products  16.5 us (13%)
  blocking collectives  8.97 us (7%)
    all_to_all x1, waiting for transfers between devices, on_device(): lax.all_to_all(summed, ('scol', 'srow'), split_axis=0, concat_axis=0, til...  13.8 us
    all_to_all x1, waiting for transfers between devices, on_device(): lax.all_to_all(flattened, 'srow', split_axis=1, concat_axis=0, tiled=True)  12.9 us
    all_to_all x1, blocking collectives, on_device(): lax.all_to_all(image.astype(jnp.bfloat16), 'srow', split_axis=0, concat_a...  8.97 us
    all_to_all x1, starting transfers between devices, on_device(): lax.all_to_all(summed, ('scol', 'srow'), split_axis=0, concat_axis=0, til...  8.8 us
    reshape x1, local copies, waits for them, and re-layouts, on_device(): spec = spec.reshape(n_scol, 2 * k_blk * cols_here, n_pix)  7.38 us
    all_to_all x1, waiting for transfers between devices, on_device(): lax.all_to_all(half.astype(jnp.bfloat16), 'scol', split_axis=0, concat_ax...  6.76 us
    all_to_all x1, starting transfers between devices, on_device(): lax.all_to_all(flattened, 'srow', split_axis=1, concat_axis=0, tiled=True)  6.58 us
    dot_general x1, matrix products, on_device(): jnp.dot(forward_rows.astype(jnp.bfloat16), gathered.reshape(row_count, co...  4.31 us
  transfers between devices with their start and end apart: 3, of which 3 were waited for; matrix products, arithmetic and copies ran while one was open for 17% of the time, Pallas kernels for 0%

profile of v11, /device:TPU:0, one launch (start us, length us, event | category | flops | bytes accessed | tf_op | source)
XLA Modules:
  0.0 121.9 jit_solution(11415578403139531394)
XLA Ops:
  0.0 0.0 copy-start
  0.0 1.6 %copy-done = bf16[64,64,256]{2,1,0:T(8,128)(2,1)S(1)} copy-done((bf16[64,64,256]{2,1,0:T(8,128)(2,1)S(1)}, bf16[64,64,256]{2,1,0:T(8,128)(2,1)}, u32[]{:S(2)}) %copy-start) | copy-done | bytes 2097176
  1.6 0.7 convolution_bitcast_fusion
  2.3 0.0 copy-start.5
  2.3 0.0 copy-start.6
  2.3 0.6 slice_reduce_fusion
  2.9 0.1 copy-done.5
  3.0 0.0 copy-done.6
  3.0 0.4 fusion.5
  3.4 1.5 %fusion.2 = bf16[64,64,256]{2,1,0:T(8,128)(2,1)S(1)} fusion(f32[64,64]{1,0:T(8,128)S(1)} %slice_reduce_fusion, f32[256,256,1]{1,0,2:T(8,128)S(1)} %fusion.5, bf16[64,64,256]{2,1,0:T(8,128)(2,1)S(1)} %copy-done), kind=kOutput, calls=%fused_computation.10 | convolution fusion | flops 1612709888 | bytes 4472832 | tf_op jit(solution)/shard_map/rcp,pq->rcq/dot_general | solution.py:62
  4.9 2.5 %copy.54 = bf16[64,64,256]{2,0,1:T(8,128)(2,1)} copy(bf16[64,64,256]{2,1,0:T(8,128)(2,1)S(1)} %fusion.2) | data formatting | bytes 4194304 | tf_op jit(solution)/shard_map/convert_element_type | solution.py:63
  7.5 6.6 %all-to-all-start = ((bf16[64,64,256]{2,0,1:T(8,128)(2,1)}), bf16[64,64,256]{2,0,1:T(8,128)(2,1)}, u32[]{:S(2)}, u32[]{:S(2)}) async-start(bf16[64,64,256]{2,0,1:T(8,128)(2,1)} %copy.54), calls=%async_computation | async-start | bytes 4194304 | tf_op jit(solution)/shard_map/all_to_all | solution.py:65
  14.0 1.0 fusion.31
  15.1 0.2 fusion.57
  15.3 0.2 copy.52
  15.4 0.9 copy.53
  16.3 0.0 copy-done.9
  16.3 0.1 iota_add_fusion.1
  16.4 0.0 copy-done.10
  16.4 0.0 copy-start.8
  16.4 3.7 %subtract_convert_fusion.1 = (bf16[512,4,128]{2,1,0:T(4,128)(2,1)}, bf16[512,4,128]{2,1,0:T(4,128)(2,1)S(1)}) fusion(f32[512,128]{1,0:T(8,128)S(1)} %get-tuple-element.31, f32[512,4]{1,0:T(8,128)} %copy.53, f32[512,128]{1,0:T(8,128)S(1)} %get-tuple-element.32, f32[512,4]{1,0:T(8,128)S(1)} %copy.52), kind=kLoop, calls=%fused_computation.29 | loop fusion | flops 2359296 | bytes 1589248 | tf_op jit(solution)/shard_map/convert.3
  20.1 0.0 copy-done.7
  20.1 0.6 dynamic_slice.3
  20.7 0.2 neg.22
  20.9 1.2 %sub.156 = bf16[1,16,32,512]{3,2,0,1:T(8,128)(2,1)S(1)} reshape(bf16[512,4,128]{2,1,0:T(4,128)(2,1)} %get-tuple-element.9) | data formatting | bytes 1048576 | tf_op jit(solution)/shard_map/sub | solution.py:29
  22.2 0.1 copy.51
  22.3 0.0 copy-done.8
  22.3 0.1 iota_add_fusion
  22.3 0.1 subtract_multiply_fusion
  22.4 0.1 subtract_multiply_fusion.1
  22.6 2.5 %subtract_convert_fusion = bf16[16,256,256]{2,1,0:T(8,128)(2,1)} fusion(s32[256,256]{1,0:T(8,128)S(1)} %bitcast.122, s32[16,4,256]{2,1,0:T(4,128)S(1)} %get-tuple-element.12, s32[256,256]{1,0:T(8,128)S(1)} %bitcast.121, s32[16,4,256]{2,1,0:T(4,128)S(1)} %get-tuple-element.11), kind=kLoop, calls=%fused_computation.6 | loop fusion | flops 8388608 | bytes 2752512 | tf_op jit(solution)/shard_map/convert_element_type | solution.py:108
  25.1 0.7 fusion.64
  25.8 0.3 fusion.42
  26.2 1.1 pad_maximum_fusion
  27.3 12.9 %all-to-all-done = bf16[64,64,256]{2,0,1:T(8,128)(2,1)} async-done(((bf16[64,64,256]{2,0,1:T(8,128)(2,1)}), bf16[64,64,256]{2,0,1:T(8,128)(2,1)}, u32[]{:S(2)}, u32[]{:S(2)}) %all-to-all-start) | async-done | bytes 2097184 | tf_op jit(solution)/shard_map/all_to_all | solution.py:65
  40.2 2.9 %copy.55 = bf16[64,8,8,256]{3,2,0,1:T(8,128)(2,1)S(1)} copy(bf16[64,8,8,256]{3,0,2,1:T(8,128)(2,1)} %bitcast.12) | data formatting | bytes 4194304 | tf_op jit(solution)/shard_map/all_to_all | solution.py:65
  43.0 0.0 copy-start.4
  43.0 0.7 copy.74
  43.7 0.5 copy-done.4
  44.3 4.3 %convolution_convert_fusion = bf16[1024,2048]{1,0:T(8,128)(2,1)} fusion(bf16[1024,512]{1,0:T(8,128)(2,1)S(1)} %bitcast.119, bf16[512,2048]{1,0:T(8,128)(2,1)S(1)} %bitcast.117), kind=kOutput, calls=%fused_computation.7 | convolution fusion | flops 2149580800 | bytes 7340032 | tf_op jit(solution)/shard_map/dot_general | solution.py:74
  48.6 7.4 %reshape.426 = bf16[16,512,256]{2,1,0:T(8,128)(2,1)} reshape(bf16[1024,2048]{1,0:T(8,128)(2,1)} %convolution_convert_fusion) | data formatting | bytes 8388608 | tf_op jit(solution)/shard_map/reshape | solution.py:79
  56.0 4.1 %fusion.66 = f32[16,256,512]{2,1,0:T(8,128)S(1)} fusion(bf16[16,256,256]{2,1,0:T(8,128)(2,1)} %subtract_convert_fusion, bf16[16,512,256]{2,1,0:T(8,128)(2,1)} %reshape.426), kind=kOutput, calls=%fused_computation.145 | convolution fusion | flops 1073741824 | bytes 14680064 | tf_op jit(solution)/shard_map/axp,anp->axn/dot_general | solution.py:114
  60.1 2.5 %select_reduce_fusion = bf16[16,64,512]{2,1,0:T(8,128)(2,1)} fusion(f32[16,4,64,512]{3,2,1,0:T(8,128)S(1)} %bitcast.113, pred[16,4,512]{2,1,0:T(4,128)(4,1)S(1)} %iota_compare_fusion.1), kind=kLoop, calls=%fused_computation | loop fusion | flops 3670016 | bytes 9469952 | tf_op jit(solution)/shard_map/reduce_sum | solution.py:117
  62.5 8.8 %all-to-all-start.1 = ((bf16[128,8,512]{2,1,0:T(8,128)(2,1)}), bf16[128,8,512]{2,1,0:T(8,128)(2,1)S(1)}, u32[]{:S(2)}, u32[]{:S(2)}) async-start(bf16[128,8,512]{2,1,0:T(8,128)(2,1)} %bitcast.15), calls=%async_computation.1 | async-start | bytes 2097152 | tf_op jit(solution)/shard_map/all_to_all | solution.py:120
  71.4 1.0 fusion.35
  72.4 1.0 maximum_maximum_fusion.1
  73.4 0.1 fusion.60
  73.5 3.1 %fusion.22 = (f32[128,1024]{0,1:T(8,128)}, f32[128,1024]{0,1:T(8,128)}, f32[128,1024]{0,1:T(8,128)}) fusion(s32[128]{0:T(128)S(1)} %get-tuple-element.30), kind=kLoop, calls=%fused_computation.54 | loop fusion | flops 1966080 | bytes 1573376 | tf_op jit(solution)/shard_map/sin | solution.py:16
  76.5 13.8 %all-to-all-done.1 = bf16[128,8,512]{2,1,0:T(8,128)(2,1)S(1)} async-done(((bf16[128,8,512]{2,1,0:T(8,128)(2,1)}), bf16[128,8,512]{2,1,0:T(8,128)(2,1)S(1)}, u32[]{:S(2)}, u32[]{:S(2)}) %all-to-all-start.1) | async-done | bytes 1048608 | tf_op jit(solution)/shard_map/all_to_all | solution.py:120
  90.3 1.7 %copy.69 = bf16[128,8,512]{0,2,1:T(8,128)(2,1)} copy(bf16[128,8,512]{2,1,0:T(8,128)(2,1)S(1)} %all-to-all-done.1) | data formatting | bytes 2097152 | tf_op jit(solution)/shard_map/reshape | solution.py:128
  92.0 2.5 %fusion.67 = f32[8,2,32,8,2,128]{5,3,4,2,1,0:T(8,128)S(1)} fusion(bf16[8,2,32,8,128,1]{4,3,5,2,1,0:T(8,128)(2,1)} %bitcast.116, f32[2,128,128,1,1,1]{2,1,0,5,4,3:T(8,128)S(1)} %bitcast.123), kind=kOutput, calls=%fused_computation.146 | convolution fusion | flops 805306368 | bytes 5373952 | tf_op jit(solution)/shard_map/dot_general | solution.py:127
  94.5 0.0 copy-start.3
  94.5 0.8 add_reduce_fusion
  95.3 0.0 copy-start.1
  95.3 0.0 copy-start.2
  95.4 0.2 copy-done.3
  95.5 0.4 fusion.3
  95.9 0.7 copy.59
  96.6 3.5 %all-to-all-start.2 = ((bf16[16,2,32,128]{3,2,1,0:T(8,128)(2,1)}), bf16[16,2,32,128]{3,2,1,0:T(8,128)(2,1)S(1)}, u32[]{:S(2)}, u32[]{:S(2)}) async-start(bf16[16,2,32,128]{3,2,1,0:T(8,128)(2,1)} %copy.59), calls=%async_computation.2 | async-start | bytes 524288 | tf_op jit(solution)/shard_map/all_to_all | solution.py:163
  100.2 2.5 %maximum_maximum_fusion = f32[256,2048]{0,1:T(8,128)} fusion(f32[128,1024]{0,1:T(8,128)S(1)} %copy-done.2, f32[128,1024]{0,1:T(8,128)} %get-tuple-element.28, f32[128,1024]{0,1:T(8,128)S(1)} %copy-done.1), kind=kLoop, calls=%fused_computation.9 | loop fusion | flops 1572864 | bytes 3670016 | tf_op jit(solution)/shard_map/concatenate | solution.py:169
  102.7 6.8 %all-to-all-done.2 = bf16[16,2,32,128]{3,2,1,0:T(8,128)(2,1)S(1)} async-done(((bf16[16,2,32,128]{3,2,1,0:T(8,128)(2,1)}), bf16[16,2,32,128]{3,2,1,0:T(8,128)(2,1)S(1)}, u32[]{:S(2)}, u32[]{:S(2)}) %all-to-all-start.2) | async-done | bytes 262176 | tf_op jit(solution)/shard_map/all_to_all | solution.py:163
  109.6 2.6 %fusion.6 = bf16[8,32,2,128]{3,1,0,2:T(8,128)(2,1)S(1)} fusion(f32[2,8,128,256]{3,2,1,0:T(8,128)} %bitcast.114, f32[32,256,1,1]{1,0,2,3:T(8,128)S(1)} %reshape.436), kind=kOutput, calls=%fused_computation.18 | convolution fusion | flops 100728832 | bytes 2260992 | tf_op jit(solution)/shard_map/dot_general | solution.py:177
  112.2 9.0 %all_to_all.30 = bf16[8,32,2,128]{3,1,2,0:T(8,128)(2,1)S(1)} all-to-all(bf16[8,32,2,128]{3,1,2,0:T(8,128)(2,1)S(1)} %copy.62), channel_id=1, replica_groups=mesh['srow'=8,'scol'=16] {'srow'}, dimensions={0} | all-to-all | bytes 262144 | tf_op jit(solution)/shard_map/all_to_all | solution.py:179
  121.2 0.6 copy.64
  (24 shorter events, 0.3 us)
Async XLA Ops:
  0.0 1.6 %copy-start = (bf16[64,64,256]{2,1,0:T(8,128)(2,1)S(1)}, bf16[64,64,256]{2,1,0:T(8,128)(2,1)}, u32[]{:S(2)}) copy-start(bf16[64,64,256]{2,1,0:T(8,128)(2,1)} %param.8) | copy-start | bytes 6291460
  2.3 0.7 copy-start.5
  2.3 0.7 copy-start.6
  7.5 8.8 %copy-start.9 = (s32[8]{0:T(128)S(1)}, s32[8]{0:T(128)}, u32[]{:S(2)}) copy-start(s32[8]{0:T(128)} %constant.178.clone) | copy-start | bytes 100
  7.5 8.9 %copy-start.10 = (s32[16]{0:T(128)S(1)}, s32[16]{0:T(128)}, u32[]{:S(2)}) copy-start(s32[16]{0:T(128)} %constant.179) | copy-start | bytes 196
  7.5 32.7 %all-to-all-start = ((bf16[64,64,256]{2,0,1:T(8,128)(2,1)}), bf16[64,64,256]{2,0,1:T(8,128)(2,1)}, u32[]{:S(2)}, u32[]{:S(2)}) async-start(bf16[64,64,256]{2,0,1:T(8,128)(2,1)} %copy.54), calls=%async_computation | async-start | bytes 4194304 | tf_op jit(solution)/shard_map/all_to_all | solution.py:65
  14.0 6.1 %copy-start.7 = (s32[256]{0:T(256)S(1)}, s32[256]{0:T(256)}, u32[]{:S(2)}) copy-start(s32[256]{0:T(256)} %param.11) | copy-start | bytes 3076
  16.4 5.9 %copy-start.8 = (s32[16]{0:T(128)S(1)}, s32[16]{0:T(128)}, u32[]{:S(2)}) copy-start(s32[16]{0:T(128)} %constant.177.clone) | copy-start | bytes 196
  43.0 1.2 %copy-start.4 = (bf16[2,16,32,512]{3,2,0,1:T(8,128)(2,1)S(1)}, bf16[2,16,32,512]{3,2,0,1:T(8,128)(2,1)}, u32[]{:S(2)}) copy-start(bf16[2,16,32,512]{3,2,0,1:T(8,128)(2,1)} %pad_maximum_fusion) | copy-start | bytes 3145732
  62.5 27.8 %all-to-all-start.1 = ((bf16[128,8,512]{2,1,0:T(8,128)(2,1)}), bf16[128,8,512]{2,1,0:T(8,128)(2,1)S(1)}, u32[]{:S(2)}, u32[]{:S(2)}) async-start(bf16[128,8,512]{2,1,0:T(8,128)(2,1)} %bitcast.15), calls=%async_computation.1 | async-start | bytes 2097152 | tf_op jit(solution)/shard_map/all_to_all | solution.py:120
  94.5 1.0 copy-start.3
  95.3 4.9 %copy-start.1 = (f32[128,1024]{0,1:T(8,128)S(1)}, f32[128,1024]{0,1:T(8,128)}, u32[]{:S(2)}) copy-start(f32[128,1024]{0,1:T(8,128)} %get-tuple-element.26) | copy-start | bytes 1572868
  95.3 4.9 %copy-start.2 = (f32[128,1024]{0,1:T(8,128)S(1)}, f32[128,1024]{0,1:T(8,128)}, u32[]{:S(2)}) copy-start(f32[128,1024]{0,1:T(8,128)} %get-tuple-element.27) | copy-start | bytes 1572868
  96.6 12.9 %all-to-all-start.2 = ((bf16[16,2,32,128]{3,2,1,0:T(8,128)(2,1)}), bf16[16,2,32,128]{3,2,1,0:T(8,128)(2,1)S(1)}, u32[]{:S(2)}, u32[]{:S(2)}) async-start(bf16[16,2,32,128]{3,2,1,0:T(8,128)(2,1)} %copy.59), calls=%async_computation.2 | async-start | bytes 524288 | tf_op jit(solution)/shard_map/all_to_all | solution.py:163

commit v12 on v10

--- a/solution.py
+++ b/solution.py
@@ -110,10 +110,10 @@
     dx_of_n = jnp.broadcast_to(own_dx[:, None, :, None], (n_scol, 2, k_blk, cols_here))
     dx_of_n = dx_of_n.reshape(n_scol, 1, 2 * k_blk * cols_here)
     weight = weight.transpose(0, 3, 1, 2, 4).reshape(n_scol, n_dx * n_srow * n_dyl, n_pix)
-    every_dx = jnp.einsum("axp,anp->axn", weight, spec, preferred_element_type=jnp.float32)
+    every_dx = jnp.einsum("axp,anp->axn", weight, spec, preferred_element_type=jnp.bfloat16)
     every_dx = every_dx.reshape(n_scol, n_dx, n_srow * n_dyl, 2 * k_blk * cols_here)
     dx_pick = dx_of_n[:, None, :, :] == jnp.arange(n_dx, dtype=jnp.int32)[None, :, None, None]
-    summed = jnp.sum(jnp.where(dx_pick, every_dx, 0.0), axis=1)
+    summed = jnp.sum(jnp.where(dx_pick, every_dx, jnp.zeros((), jnp.bfloat16)), axis=1)
     summed = summed.reshape(n_dev, n_dyl, 2 * k_blk * cols_here).astype(jnp.bfloat16)
 
     summed = lax.all_to_all(summed, ("scol", "srow"), split_axis=0, concat_axis=0, tiled=True)

time: 118 us -> 117 us (level)
  no operation moved by 1% of the time
where the time goes in v12:
time: 117 us
  waiting for transfers between devices  40.3 us (34%)
  starting transfers between devices  18.9 us (16%)
  local copies, waits for them, and re-layouts  18.1 us (15%)
  other arithmetic  17.7 us (15%)
  matrix products  12.3 us (11%)
  blocking collectives  8.97 us (8%)
    all_to_all x1, waiting for transfers between devices, on_device(): lax.all_to_all(flattened, 'srow', split_axis=1, concat_axis=0, tiled=True)  18.2 us
    all_to_all x1, waiting for transfers between devices, on_device(): lax.all_to_all(summed, ('scol', 'srow'), split_axis=0, concat_axis=0, til...  13.9 us
    all_to_all x1, blocking collectives, on_device(): lax.all_to_all(image.astype(jnp.bfloat16), 'srow', split_axis=0, concat_a...  8.97 us
    all_to_all x1, starting transfers between devices, on_device(): lax.all_to_all(summed, ('scol', 'srow'), split_axis=0, concat_axis=0, til...  8.79 us
    all_to_all x1, waiting for transfers between devices, on_device(): lax.all_to_all(half.astype(jnp.bfloat16), 'scol', split_axis=0, concat_ax...  8.13 us
    reshape x1, local copies, waits for them, and re-layouts, on_device(): spec = spec.reshape(n_scol, 2 * k_blk * cols_here, n_pix)  7.42 us
    all_to_all x1, starting transfers between devices, on_device(): lax.all_to_all(flattened, 'srow', split_axis=1, concat_axis=0, tiled=True)  6.58 us
    dot_general x1, matrix products, on_device(): jnp.dot(forward_rows.astype(jnp.bfloat16), gathered.reshape(row_count, co...  4.28 us
  transfers between devices with their start and end apart: 3, of which 3 were waited for; matrix products, arithmetic and copies ran while one was open for 12% of the time, Pallas kernels for 0%

profile of v12, /device:TPU:0, one launch (start us, length us, event | category | flops | bytes accessed | tf_op | source)
XLA Modules:
  0.0 116.6 jit_solution(1721541616890834971)
XLA Ops:
  0.0 0.0 copy-start
  0.0 0.0 copy-start.1
  0.0 0.0 copy-start.4
  0.0 2.4 %convert_reduce_fusion = f32[64,64]{1,0:T(8,128)S(1)} fusion(bf16[64,64,256]{2,1,0:T(8,128)(2,1)} %param.8), kind=kLoop, calls=%fused_computation.6 | loop fusion | flops 2093056 | bytes 2113536 | tf_op jit(solution)/shard_map/reduce_sum | solution.py:58
  2.4 0.0 copy-done
  2.4 0.0 copy-done.4
  2.4 0.4 fusion.5
  2.8 0.0 copy-done.1
  2.8 1.5 %fusion.2 = bf16[64,64,256]{2,1,0:T(8,128)(2,1)S(1)} fusion(f32[64,64]{1,0:T(8,128)S(1)} %broadcast_multiply_fusion.1, f32[256,256,1]{1,0,2:T(8,128)S(1)} %fusion.5, bf16[64,64,256]{2,1,0:T(8,128)(2,1)S(1)} %copy-done.1), kind=kOutput, calls=%fused_computation.10 | convolution fusion | flops 1612709888 | bytes 4472832 | tf_op jit(solution)/shard_map/rcp,pq->rcq/dot_general | solution.py:61
  4.3 2.5 %copy.54 = bf16[64,64,256]{2,0,1:T(8,128)(2,1)} copy(bf16[64,64,256]{2,1,0:T(8,128)(2,1)S(1)} %fusion.2) | data formatting | bytes 4194304 | tf_op jit(solution)/shard_map/convert_element_type | solution.py:62
  6.8 0.0 copy-start.7
  6.8 0.0 copy-start.8
  6.8 6.6 %all-to-all-start = ((bf16[64,64,256]{2,0,1:T(8,128)(2,1)}), bf16[64,64,256]{2,0,1:T(8,128)(2,1)}, u32[]{:S(2)}, u32[]{:S(2)}) async-start(bf16[64,64,256]{2,0,1:T(8,128)(2,1)} %copy.54), calls=%async_computation | async-start | bytes 4194304 | tf_op jit(solution)/shard_map/all_to_all | solution.py:64
  13.4 0.0 copy-start.5
  13.4 1.0 fusion.31
  14.5 0.2 fusion.56
  14.6 0.2 copy.52
  14.8 0.1 copy.53
  14.9 0.0 copy-done.7
  14.9 0.1 iota_add_fusion.1
  15.0 0.0 copy-done.8
  15.0 0.0 copy-start.6
  15.0 1.4 %subtract_convert_fusion.1 = (bf16[512,4,128]{2,1,0:T(4,128)(2,1)S(1)}, bf16[512,4,128]{2,1,0:T(4,128)(2,1)S(1)}) fusion(f32[512,128]{1,0:T(8,128)S(1)} %get-tuple-element.31, f32[512,4]{1,0:T(8,128)S(1)} %copy.53, f32[512,128]{1,0:T(8,128)S(1)} %get-tuple-element.32, f32[512,4]{1,0:T(8,128)S(1)} %copy.52), kind=kLoop, calls=%fused_computation.28 | loop fusion | flops 2359296 | bytes 1589248 | tf_op jit(solution)/shard_map/convert.4
  16.4 0.0 copy-done.5
  16.5 0.6 dynamic_slice.3
  17.1 0.2 neg.22
  17.3 0.2 sub.156
  17.5 0.1 copy.51
  17.6 0.0 copy-done.6
  17.6 0.1 iota_add_fusion
  17.7 0.1 subtract_multiply_fusion
  17.8 0.1 subtract_multiply_fusion.1
  17.9 1.2 %subtract_convert_fusion = bf16[16,256,256]{2,1,0:T(8,128)(2,1)S(1)} fusion(s32[256,256]{1,0:T(8,128)S(1)} %bitcast.119, s32[16,4,256]{2,1,0:T(4,128)S(1)} %get-tuple-element.12, s32[256,256]{1,0:T(8,128)S(1)} %bitcast.118, s32[16,4,256]{2,1,0:T(4,128)S(1)} %get-tuple-element.11), kind=kLoop, calls=%fused_computation.7 | loop fusion | flops 8388608 | bytes 2752512 | tf_op jit(solution)/shard_map/convert_element_type | solution.py:107
  19.2 0.7 fusion.63
  19.8 0.3 fusion.41
  20.2 1.1 pad_maximum_fusion
  21.3 18.2 %all-to-all-done = bf16[64,64,256]{2,0,1:T(8,128)(2,1)} async-done(((bf16[64,64,256]{2,0,1:T(8,128)(2,1)}), bf16[64,64,256]{2,0,1:T(8,128)(2,1)}, u32[]{:S(2)}, u32[]{:S(2)}) %all-to-all-start) | async-done | bytes 2097184 | tf_op jit(solution)/shard_map/all_to_all | solution.py:64
  39.5 2.9 %copy.55 = bf16[64,8,8,256]{3,2,0,1:T(8,128)(2,1)S(1)} copy(bf16[64,8,8,256]{3,0,2,1:T(8,128)(2,1)} %bitcast.11) | data formatting | bytes 4194304 | tf_op jit(solution)/shard_map/all_to_all | solution.py:64
  42.4 0.0 copy-start.3
  42.4 0.7 copy.74
  43.1 0.5 copy-done.3
  43.6 4.3 %convolution_convert_fusion = bf16[1024,2048]{1,0:T(8,128)(2,1)} fusion(bf16[1024,512]{1,0:T(8,128)(2,1)S(1)} %bitcast.116, bf16[512,2048]{1,0:T(8,128)(2,1)S(1)} %bitcast.114), kind=kOutput, calls=%fused_computation.8 | convolution fusion | flops 2149580800 | bytes 7340032 | tf_op jit(solution)/shard_map/dot_general | solution.py:73
  47.9 7.4 %reshape.431 = bf16[16,512,256]{2,1,0:T(8,128)(2,1)} reshape(bf16[1024,2048]{1,0:T(8,128)(2,1)} %convolution_convert_fusion) | data formatting | bytes 8388608 | tf_op jit(solution)/shard_map/reshape | solution.py:78
  55.3 3.5 %fusion.64 = bf16[16,256,512]{2,1,0:T(8,128)(2,1)S(1)} fusion(bf16[16,256,256]{2,1,0:T(8,128)(2,1)S(1)} %subtract_convert_fusion, bf16[16,512,256]{2,1,0:T(8,128)(2,1)} %reshape.431), kind=kOutput, calls=%fused_computation.143 | convolution fusion | flops 1073741824 | bytes 10485760 | tf_op jit(solution)/shard_map/axp,anp->axn/dot_general | solution.py:113
  58.8 2.0 %select_reduce_fusion = bf16[16,64,512]{2,1,0:T(8,128)(2,1)} fusion(bf16[16,4,64,512]{3,2,1,0:T(8,128)(2,1)S(1)} %bitcast.110, pred[16,4,512]{2,1,0:T(4,128)(4,1)S(1)} %iota_compare_fusion.1), kind=kLoop, calls=%fused_computation.4 | loop fusion | flops 3670016 | bytes 5275648 | tf_op jit(solution)/shard_map/reduce_sum | solution.py:116
  60.8 8.8 %all-to-all-start.1 = ((bf16[128,8,512]{2,1,0:T(8,128)(2,1)}), bf16[128,8,512]{2,1,0:T(8,128)(2,1)S(1)}, u32[]{:S(2)}, u32[]{:S(2)}) async-start(bf16[128,8,512]{2,1,0:T(8,128)(2,1)} %bitcast.14), calls=%async_computation.1 | async-start | bytes 2097152 | tf_op jit(solution)/shard_map/all_to_all | solution.py:119
  69.6 1.0 fusion.35
  70.6 1.0 maximum_maximum_fusion.1
  71.6 0.1 fusion.59
  71.7 2.9 %fusion.22 = (f32[128,1024]{0,1:T(8,128)S(1)}, f32[128,1024]{0,1:T(8,128)S(1)}, f32[128,1024]{0,1:T(8,128)}) fusion(s32[128]{0:T(128)S(1)} %get-tuple-element.30), kind=kLoop, calls=%fused_computation.53 | loop fusion | flops 1966080 | bytes 1573376 | tf_op jit(solution)/shard_map/sin | solution.py:16
  74.6 13.9 %all-to-all-done.1 = bf16[128,8,512]{2,1,0:T(8,128)(2,1)S(1)} async-done(((bf16[128,8,512]{2,1,0:T(8,128)(2,1)}), bf16[128,8,512]{2,1,0:T(8,128)(2,1)S(1)}, u32[]{:S(2)}, u32[]{:S(2)}) %all-to-all-start.1) | async-done | bytes 1048608 | tf_op jit(solution)/shard_map/all_to_all | solution.py:119
  88.5 1.0 copy.69
  89.5 1.2 %fusion.65 = f32[8,2,32,8,2,128]{5,3,4,2,1,0:T(8,128)S(1)} fusion(bf16[8,2,32,8,128,1]{4,3,5,2,1,0:T(8,128)(2,1)S(1)} %bitcast.113, f32[2,128,128,1,1,1]{2,1,0,5,4,3:T(8,128)S(1)} %bitcast.120), kind=kOutput, calls=%fused_computation.144 | convolution fusion | flops 805306368 | bytes 5373952 | tf_op jit(solution)/shard_map/dot_general | solution.py:126
  90.8 0.0 copy-start.2
  90.8 0.8 add_reduce_fusion
  91.6 0.2 copy-done.2
  91.8 0.4 fusion.3
  92.2 0.7 copy.59
  92.9 3.5 %all-to-all-start.2 = ((bf16[16,2,32,128]{3,2,1,0:T(8,128)(2,1)}), bf16[16,2,32,128]{3,2,1,0:T(8,128)(2,1)S(1)}, u32[]{:S(2)}, u32[]{:S(2)}) async-start(bf16[16,2,32,128]{3,2,1,0:T(8,128)(2,1)} %copy.59), calls=%async_computation.2 | async-start | bytes 524288 | tf_op jit(solution)/shard_map/all_to_all | solution.py:162
  96.4 1.2 %maximum_maximum_fusion = f32[256,2048]{0,1:T(8,128)S(1)} fusion(f32[128,1024]{0,1:T(8,128)S(1)} %get-tuple-element.27, f32[128,1024]{0,1:T(8,128)} %get-tuple-element.28, f32[128,1024]{0,1:T(8,128)S(1)} %get-tuple-element.26), kind=kLoop, calls=%fused_computation.9 | loop fusion | flops 1572864 | bytes 3670016 | tf_op jit(solution)/shard_map/concatenate | solution.py:168
  97.6 8.1 %all-to-all-done.2 = bf16[16,2,32,128]{3,2,1,0:T(8,128)(2,1)S(1)} async-done(((bf16[16,2,32,128]{3,2,1,0:T(8,128)(2,1)}), bf16[16,2,32,128]{3,2,1,0:T(8,128)(2,1)S(1)}, u32[]{:S(2)}, u32[]{:S(2)}) %all-to-all-start.2) | async-done | bytes 262176 | tf_op jit(solution)/shard_map/all_to_all | solution.py:162
  105.9 1.0 fusion.6
  106.9 9.0 %all_to_all.30 = bf16[8,32,2,128]{3,1,2,0:T(8,128)(2,1)S(1)} all-to-all(bf16[8,32,2,128]{3,1,2,0:T(8,128)(2,1)S(1)} %copy.62), channel_id=1, replica_groups=mesh['srow'=8,'scol'=16] {'srow'}, dimensions={0} | all-to-all | bytes 262144 | tf_op jit(solution)/shard_map/all_to_all | solution.py:178
  115.9 0.6 copy.64
  (20 shorter events, 0.3 us)
Async XLA Ops:
  0.0 2.4 %copy-start = (f32[16,256]{1,0:T(8,128)S(1)}, f32[16,256]{1,0:T(8,128)}, u32[]{:S(2)}) copy-start(f32[16,256]{1,0:T(8,128)} %param.10) | copy-start | bytes 49156
  0.0 2.8 %copy-start.1 = (bf16[64,64,256]{2,1,0:T(8,128)(2,1)S(1)}, bf16[64,64,256]{2,1,0:T(8,128)(2,1)}, u32[]{:S(2)}) copy-start(bf16[64,64,256]{2,1,0:T(8,128)(2,1)} %param.8) | copy-start | bytes 6291460
  0.0 2.4 %copy-start.4 = (f32[256]{0:T(256)S(1)}, f32[256]{0:T(256)}, u32[]{:S(2)}) copy-start(f32[256]{0:T(256)} %param.9) | copy-start | bytes 3076
  6.8 8.1 %copy-start.7 = (s32[8]{0:T(128)S(1)}, s32[8]{0:T(128)}, u32[]{:S(2)}) copy-start(s32[8]{0:T(128)} %constant.182.clone) | copy-start | bytes 100
  6.8 8.2 %copy-start.8 = (s32[16]{0:T(128)S(1)}, s32[16]{0:T(128)}, u32[]{:S(2)}) copy-start(s32[16]{0:T(128)} %constant.183) | copy-start | bytes 196
  6.8 32.7 %all-to-all-start = ((bf16[64,64,256]{2,0,1:T(8,128)(2,1)}), bf16[64,64,256]{2,0,1:T(8,128)(2,1)}, u32[]{:S(2)}, u32[]{:S(2)}) async-start(bf16[64,64,256]{2,0,1:T(8,128)(2,1)} %copy.54), calls=%async_computation | async-start | bytes 4194304 | tf_op jit(solution)/shard_map/all_to_all | solution.py:64
  13.4 3.1 %copy-start.5 = (s32[256]{0:T(256)S(1)}, s32[256]{0:T(256)}, u32[]{:S(2)}) copy-start(s32[256]{0:T(256)} %param.11) | copy-start | bytes 3076
  15.0 2.6 %copy-start.6 = (s32[16]{0:T(128)S(1)}, s32[16]{0:T(128)}, u32[]{:S(2)}) copy-start(s32[16]{0:T(128)} %constant.181.clone) | copy-start | bytes 196
  42.4 1.2 %copy-start.3 = (bf16[2,16,32,512]{3,2,0,1:T(8,128)(2,1)S(1)}, bf16[2,16,32,512]{3,2,0,1:T(8,128)(2,1)}, u32[]{:S(2)}) copy-start(bf16[2,16,32,512]{3,2,0,1:T(8,128)(2,1)} %pad_maximum_fusion) | copy-start | bytes 3145732
  60.8 27.8 %all-to-all-start.1 = ((bf16[128,8,512]{2,1,0:T(8,128)(2,1)}), bf16[128,8,512]{2,1,0:T(8,128)(2,1)S(1)}, u32[]{:S(2)}, u32[]{:S(2)}) async-start(bf16[128,8,512]{2,1,0:T(8,128)(2,1)} %bitcast.14), calls=%async_computation.1 | async-start | bytes 2097152 | tf_op jit(solution)/shard_map/all_to_all | solution.py:119
  90.8 1.0 copy-start.2
  92.9 12.9 %all-to-all-start.2 = ((bf16[16,2,32,128]{3,2,1,0:T(8,128)(2,1)}), bf16[16,2,32,128]{3,2,1,0:T(8,128)(2,1)S(1)}, u32[]{:S(2)}, u32[]{:S(2)}) async-start(bf16[16,2,32,128]{3,2,1,0:T(8,128)(2,1)} %copy.59), calls=%async_computation.2 | async-start | bytes 524288 | tf_op jit(solution)/shard_map/all_to_all | solution.py:162

commit v13 on v12

--- a/solution.py
+++ b/solution.py
@@ -156,9 +156,11 @@
         ],
         axis=0,
     )
+    inverse_rows = inverse_rows.reshape(2, n_scol, row_count // n_scol, 2 * k_blk).transpose(1, 0, 2, 3)
+    inverse_rows = inverse_rows.reshape(2 * row_count, 2 * k_blk)
     psi = psi.transpose(1, 0, 2).reshape(2 * k_blk, j_blk)
     half = jnp.dot(inverse_rows, psi, precision=lax.Precision.HIGH, preferred_element_type=jnp.float32)
-    half = half.reshape(2, n_scol, row_count // n_scol, j_blk).transpose(1, 0, 2, 3)
+    half = half.reshape(n_scol, 2, row_count // n_scol, j_blk)
     half = lax.all_to_all(half.astype(jnp.bfloat16), "scol", split_axis=0, concat_axis=0, tiled=True)
     half = jnp.sum(half.astype(jnp.float32), axis=0)
     out_rows = half.shape[1]

time: 117 us -> 117 us (level)
  no operation moved by 1% of the time
where the time goes in v13:
time: 117 us
  waiting for transfers between devices  40.3 us (34%)
  starting transfers between devices  18.9 us (16%)
  other arithmetic  17.7 us (15%)
  local copies, waits for them, and re-layouts  17.4 us (15%)
  matrix products  12.9 us (11%)
  blocking collectives  8.97 us (8%)
    all_to_all x1, waiting for transfers between devices, on_device(): lax.all_to_all(flattened, 'srow', split_axis=1, concat_axis=0, tiled=True)  18.2 us
    all_to_all x1, waiting for transfers between devices, on_device(): lax.all_to_all(summed, ('scol', 'srow'), split_axis=0, concat_axis=0, til...  13.9 us
    all_to_all x1, blocking collectives, on_device(): lax.all_to_all(image.astype(jnp.bfloat16), 'srow', split_axis=0, concat_a...  8.97 us
    all_to_all x1, starting transfers between devices, on_device(): lax.all_to_all(summed, ('scol', 'srow'), split_axis=0, concat_axis=0, til...  8.79 us
    all_to_all x1, waiting for transfers between devices, on_device(): lax.all_to_all(half.astype(jnp.bfloat16), 'scol', split_axis=0, concat_ax...  8.13 us
    reshape x1, local copies, waits for them, and re-layouts, on_device(): spec = spec.reshape(n_scol, 2 * k_blk * cols_here, n_pix)  7.42 us
    all_to_all x1, starting transfers between devices, on_device(): lax.all_to_all(flattened, 'srow', split_axis=1, concat_axis=0, tiled=True)  6.58 us
    dot_general x1, matrix products, on_device(): jnp.dot(forward_rows.astype(jnp.bfloat16), gathered.reshape(row_count, co...  4.28 us
  transfers between devices with their start and end apart: 3, of which 3 were waited for; matrix products, arithmetic and copies ran while one was open for 12% of the time, Pallas kernels for 0%

profile of v13, /device:TPU:0, one launch (start us, length us, event | category | flops | bytes accessed | tf_op | source)
XLA Modules:
  0.0 116.5 jit_solution(5382474700457479184)
XLA Ops:
  0.0 0.0 copy-start
  0.0 0.0 copy-start.1
  0.0 0.0 copy-start.4
  0.0 2.4 %convert_reduce_fusion = f32[64,64]{1,0:T(8,128)S(1)} fusion(bf16[64,64,256]{2,1,0:T(8,128)(2,1)} %param.8), kind=kLoop, calls=%fused_computation.6 | loop fusion | flops 2093056 | bytes 2113536 | tf_op jit(solution)/shard_map/reduce_sum | solution.py:58
  2.4 0.0 copy-done
  2.4 0.0 copy-done.4
  2.4 0.4 fusion.4
  2.8 0.0 copy-done.1
  2.8 1.5 %fusion.2 = bf16[64,64,256]{2,1,0:T(8,128)(2,1)S(1)} fusion(f32[64,64]{1,0:T(8,128)S(1)} %broadcast_multiply_fusion.1, f32[256,256,1]{1,0,2:T(8,128)S(1)} %fusion.4, bf16[64,64,256]{2,1,0:T(8,128)(2,1)S(1)} %copy-done.1), kind=kOutput, calls=%fused_computation.10 | convolution fusion | flops 1612709888 | bytes 4472832 | tf_op jit(solution)/shard_map/rcp,pq->rcq/dot_general | solution.py:61
  4.3 2.5 %copy.53 = bf16[64,64,256]{2,0,1:T(8,128)(2,1)} copy(bf16[64,64,256]{2,1,0:T(8,128)(2,1)S(1)} %fusion.2) | data formatting | bytes 4194304 | tf_op jit(solution)/shard_map/convert_element_type | solution.py:62
  6.8 0.0 copy-start.7
  6.8 0.0 copy-start.8
  6.8 6.6 %all-to-all-start = ((bf16[64,64,256]{2,0,1:T(8,128)(2,1)}), bf16[64,64,256]{2,0,1:T(8,128)(2,1)}, u32[]{:S(2)}, u32[]{:S(2)}) async-start(bf16[64,64,256]{2,0,1:T(8,128)(2,1)} %copy.53), calls=%async_computation | async-start | bytes 4194304 | tf_op jit(solution)/shard_map/all_to_all | solution.py:64
  13.4 0.0 copy-start.5
  13.4 1.0 fusion.32
  14.5 0.2 fusion.57
  14.6 0.2 copy.51
  14.8 0.1 copy.52
  14.9 0.0 copy-done.7
  14.9 0.1 iota_add_fusion.1
  15.0 0.0 copy-done.8
  15.0 0.0 copy-start.6
  15.0 1.4 %subtract_convert_fusion.1 = (bf16[512,4,128]{2,1,0:T(4,128)(2,1)S(1)}, bf16[512,4,128]{2,1,0:T(4,128)(2,1)S(1)}) fusion(f32[512,128]{1,0:T(8,128)S(1)} %get-tuple-element.31, f32[512,4]{1,0:T(8,128)S(1)} %copy.52, f32[512,128]{1,0:T(8,128)S(1)} %get-tuple-element.32, f32[512,4]{1,0:T(8,128)S(1)} %copy.51), kind=kLoop, calls=%fused_computation.27 | loop fusion | flops 2359296 | bytes 1589248 | tf_op jit(solution)/shard_map/convert.4
  16.4 0.0 copy-done.5
  16.5 0.6 dynamic_slice.3
  17.1 0.2 neg.22
  17.3 0.2 sub.156
  17.5 0.1 copy.50
  17.6 0.0 copy-done.6
  17.6 0.1 iota_add_fusion
  17.7 0.1 subtract_multiply_fusion
  17.8 0.1 subtract_multiply_fusion.1
  17.9 1.2 %subtract_convert_fusion = bf16[16,256,256]{2,1,0:T(8,128)(2,1)S(1)} fusion(s32[256,256]{1,0:T(8,128)S(1)} %bitcast.119, s32[16,4,256]{2,1,0:T(4,128)S(1)} %get-tuple-element.12, s32[256,256]{1,0:T(8,128)S(1)} %bitcast.118, s32[16,4,256]{2,1,0:T(4,128)S(1)} %get-tuple-element.11), kind=kLoop, calls=%fused_computation.7 | loop fusion | flops 8388608 | bytes 2752512 | tf_op jit(solution)/shard_map/convert_element_type | solution.py:107
  19.2 0.7 fusion.64
  19.8 0.3 fusion.42
  20.2 1.1 pad_maximum_fusion
  21.3 18.2 %all-to-all-done = bf16[64,64,256]{2,0,1:T(8,128)(2,1)} async-done(((bf16[64,64,256]{2,0,1:T(8,128)(2,1)}), bf16[64,64,256]{2,0,1:T(8,128)(2,1)}, u32[]{:S(2)}, u32[]{:S(2)}) %all-to-all-start) | async-done | bytes 2097184 | tf_op jit(solution)/shard_map/all_to_all | solution.py:64
  39.5 2.9 %copy.54 = bf16[64,8,8,256]{3,2,0,1:T(8,128)(2,1)S(1)} copy(bf16[64,8,8,256]{3,0,2,1:T(8,128)(2,1)} %bitcast.12) | data formatting | bytes 4194304 | tf_op jit(solution)/shard_map/all_to_all | solution.py:64
  42.4 0.0 copy-start.3
  42.4 0.7 copy.70
  43.1 0.5 copy-done.3
  43.6 4.3 %convolution_convert_fusion = bf16[1024,2048]{1,0:T(8,128)(2,1)} fusion(bf16[1024,512]{1,0:T(8,128)(2,1)S(1)} %bitcast.116, bf16[512,2048]{1,0:T(8,128)(2,1)S(1)} %bitcast.114), kind=kOutput, calls=%fused_computation.8 | convolution fusion | flops 2149580800 | bytes 7340032 | tf_op jit(solution)/shard_map/dot_general | solution.py:73
  47.9 7.4 %reshape.437 = bf16[16,512,256]{2,1,0:T(8,128)(2,1)} reshape(bf16[1024,2048]{1,0:T(8,128)(2,1)} %convolution_convert_fusion) | data formatting | bytes 8388608 | tf_op jit(solution)/shard_map/reshape | solution.py:78
  55.3 3.5 %fusion.65 = bf16[16,256,512]{2,1,0:T(8,128)(2,1)S(1)} fusion(bf16[16,256,256]{2,1,0:T(8,128)(2,1)S(1)} %subtract_convert_fusion, bf16[16,512,256]{2,1,0:T(8,128)(2,1)} %reshape.437), kind=kOutput, calls=%fused_computation.144 | convolution fusion | flops 1073741824 | bytes 10485760 | tf_op jit(solution)/shard_map/axp,anp->axn/dot_general | solution.py:113
  58.8 2.0 %select_reduce_fusion = bf16[16,64,512]{2,1,0:T(8,128)(2,1)} fusion(bf16[16,4,64,512]{3,2,1,0:T(8,128)(2,1)S(1)} %bitcast.110, pred[16,4,512]{2,1,0:T(4,128)(4,1)S(1)} %iota_compare_fusion.1), kind=kLoop, calls=%fused_computation.4 | loop fusion | flops 3670016 | bytes 5275648 | tf_op jit(solution)/shard_map/reduce_sum | solution.py:116
  60.8 8.8 %all-to-all-start.1 = ((bf16[128,8,512]{2,1,0:T(8,128)(2,1)}), bf16[128,8,512]{2,1,0:T(8,128)(2,1)S(1)}, u32[]{:S(2)}, u32[]{:S(2)}) async-start(bf16[128,8,512]{2,1,0:T(8,128)(2,1)} %bitcast.15), calls=%async_computation.1 | async-start | bytes 2097152 | tf_op jit(solution)/shard_map/all_to_all | solution.py:119
  69.6 1.0 fusion.36
  70.6 1.0 maximum_maximum_fusion.1
  71.6 0.1 fusion.60
  71.7 2.9 %fusion.23 = (f32[128,1024]{0,1:T(8,128)S(1)}, f32[128,1024]{0,1:T(8,128)S(1)}, f32[128,1024]{0,1:T(8,128)}) fusion(s32[128]{0:T(128)S(1)} %get-tuple-element.30), kind=kLoop, calls=%fused_computation.54 | loop fusion | flops 1966080 | bytes 1573376 | tf_op jit(solution)/shard_map/sin | solution.py:16
  74.6 13.9 %all-to-all-done.1 = bf16[128,8,512]{2,1,0:T(8,128)(2,1)S(1)} async-done(((bf16[128,8,512]{2,1,0:T(8,128)(2,1)}), bf16[128,8,512]{2,1,0:T(8,128)(2,1)S(1)}, u32[]{:S(2)}, u32[]{:S(2)}) %all-to-all-start.1) | async-done | bytes 1048608 | tf_op jit(solution)/shard_map/all_to_all | solution.py:119
  88.5 1.0 copy.66
  89.5 1.2 %fusion.66 = f32[8,2,32,8,2,128]{5,3,4,2,1,0:T(8,128)S(1)} fusion(bf16[8,2,32,8,128,1]{4,3,5,2,1,0:T(8,128)(2,1)S(1)} %bitcast.113, f32[2,128,128,1,1,1]{2,1,0,5,4,3:T(8,128)S(1)} %bitcast.120), kind=kOutput, calls=%fused_computation.145 | convolution fusion | flops 805306368 | bytes 5373952 | tf_op jit(solution)/shard_map/dot_general | solution.py:126
  90.8 0.0 copy-start.2
  90.8 0.8 add_reduce_fusion
  91.6 0.2 copy-done.2
  91.8 1.1 convolution_convert_fusion.1
  92.9 3.5 %all-to-all-start.2 = ((bf16[16,2,32,128]{3,2,1,0:T(8,128)(2,1)}), bf16[16,2,32,128]{3,2,1,0:T(8,128)(2,1)S(1)}, u32[]{:S(2)}, u32[]{:S(2)}) async-start(bf16[16,2,32,128]{3,2,1,0:T(8,128)(2,1)} %convolution_convert_fusion.1), calls=%async_computation.2 | async-start | bytes 524288 | tf_op jit(solution)/shard_map/all_to_all | solution.py:164
  96.4 1.2 %maximum_maximum_fusion = f32[256,2048]{0,1:T(8,128)S(1)} fusion(f32[128,1024]{0,1:T(8,128)S(1)} %get-tuple-element.27, f32[128,1024]{0,1:T(8,128)} %get-tuple-element.28, f32[128,1024]{0,1:T(8,128)S(1)} %get-tuple-element.26), kind=kLoop, calls=%fused_computation.9 | loop fusion | flops 1572864 | bytes 3670016 | tf_op jit(solution)/shard_map/concatenate | solution.py:170
  97.6 8.1 %all-to-all-done.2 = bf16[16,2,32,128]{3,2,1,0:T(8,128)(2,1)S(1)} async-done(((bf16[16,2,32,128]{3,2,1,0:T(8,128)(2,1)}), bf16[16,2,32,128]{3,2,1,0:T(8,128)(2,1)S(1)}, u32[]{:S(2)}, u32[]{:S(2)}) %all-to-all-start.2) | async-done | bytes 262176 | tf_op jit(solution)/shard_map/all_to_all | solution.py:164
  105.8 1.0 fusion.5
  106.9 9.0 %all_to_all.30 = bf16[8,32,2,128]{3,1,2,0:T(8,128)(2,1)S(1)} all-to-all(bf16[8,32,2,128]{3,1,2,0:T(8,128)(2,1)S(1)} %copy.59), channel_id=1, replica_groups=mesh['srow'=8,'scol'=16] {'srow'}, dimensions={0} | all-to-all | bytes 262144 | tf_op jit(solution)/shard_map/all_to_all | solution.py:180
  115.9 0.6 copy.61
  (20 shorter events, 0.3 us)
Async XLA Ops:
  0.0 2.4 %copy-start = (f32[16,256]{1,0:T(8,128)S(1)}, f32[16,256]{1,0:T(8,128)}, u32[]{:S(2)}) copy-start(f32[16,256]{1,0:T(8,128)} %param.10) | copy-start | bytes 49156
  0.0 2.8 %copy-start.1 = (bf16[64,64,256]{2,1,0:T(8,128)(2,1)S(1)}, bf16[64,64,256]{2,1,0:T(8,128)(2,1)}, u32[]{:S(2)}) copy-start(bf16[64,64,256]{2,1,0:T(8,128)(2,1)} %param.8) | copy-start | bytes 6291460
  0.0 2.4 %copy-start.4 = (f32[256]{0:T(256)S(1)}, f32[256]{0:T(256)}, u32[]{:S(2)}) copy-start(f32[256]{0:T(256)} %param.9) | copy-start | bytes 3076
  6.8 8.1 %copy-start.7 = (s32[8]{0:T(128)S(1)}, s32[8]{0:T(128)}, u32[]{:S(2)}) copy-start(s32[8]{0:T(128)} %constant.182.clone) | copy-start | bytes 100
  6.8 8.2 %copy-start.8 = (s32[16]{0:T(128)S(1)}, s32[16]{0:T(128)}, u32[]{:S(2)}) copy-start(s32[16]{0:T(128)} %constant.183) | copy-start | bytes 196
  6.8 32.7 %all-to-all-start = ((bf16[64,64,256]{2,0,1:T(8,128)(2,1)}), bf16[64,64,256]{2,0,1:T(8,128)(2,1)}, u32[]{:S(2)}, u32[]{:S(2)}) async-start(bf16[64,64,256]{2,0,1:T(8,128)(2,1)} %copy.53), calls=%async_computation | async-start | bytes 4194304 | tf_op jit(solution)/shard_map/all_to_all | solution.py:64
  13.4 3.1 %copy-start.5 = (s32[256]{0:T(256)S(1)}, s32[256]{0:T(256)}, u32[]{:S(2)}) copy-start(s32[256]{0:T(256)} %param.11) | copy-start | bytes 3076
  15.0 2.6 %copy-start.6 = (s32[16]{0:T(128)S(1)}, s32[16]{0:T(128)}, u32[]{:S(2)}) copy-start(s32[16]{0:T(128)} %constant.181.clone) | copy-start | bytes 196
  42.4 1.2 %copy-start.3 = (bf16[2,16,32,512]{3,2,0,1:T(8,128)(2,1)S(1)}, bf16[2,16,32,512]{3,2,0,1:T(8,128)(2,1)}, u32[]{:S(2)}) copy-start(bf16[2,16,32,512]{3,2,0,1:T(8,128)(2,1)} %pad_maximum_fusion) | copy-start | bytes 3145732
  60.8 27.8 %all-to-all-start.1 = ((bf16[128,8,512]{2,1,0:T(8,128)(2,1)}), bf16[128,8,512]{2,1,0:T(8,128)(2,1)S(1)}, u32[]{:S(2)}, u32[]{:S(2)}) async-start(bf16[128,8,512]{2,1,0:T(8,128)(2,1)} %bitcast.15), calls=%async_computation.1 | async-start | bytes 2097152 | tf_op jit(solution)/shard_map/all_to_all | solution.py:119
  90.8 1.0 copy-start.2
  92.9 12.9 %all-to-all-start.2 = ((bf16[16,2,32,128]{3,2,1,0:T(8,128)(2,1)}), bf16[16,2,32,128]{3,2,1,0:T(8,128)(2,1)S(1)}, u32[]{:S(2)}, u32[]{:S(2)}) async-start(bf16[16,2,32,128]{3,2,1,0:T(8,128)(2,1)} %convolution_convert_fusion.1), calls=%async_computation.2 | async-start | bytes 524288 | tf_op jit(solution)/shard_map/all_to_all | solution.py:164

commit v14 on v12

--- a/solution.py
+++ b/solution.py
@@ -123,11 +123,13 @@
     col_ids = jnp.arange(col_count, dtype=jnp.int32)
     my_j = b_idx * j_blk + jnp.arange(j_blk, dtype=jnp.int32)
     src_cos, src_sin = waves(jnp.arange(n_dev, dtype=jnp.int32) * cols_here, my_j, col_count)
-    by_source = jnp.dot(
-        summed.reshape(n_dev, -1).T.astype(jnp.float32),
-        jnp.concatenate([src_cos, src_sin], axis=1),
-        precision=lax.Precision.HIGH,
-        preferred_element_type=jnp.float32,
+    src_table = jnp.concatenate([src_cos, src_sin], axis=1)
+    table_hi = lax.reduce_precision(src_table, exponent_bits=8, mantissa_bits=7)
+    table_lo = (src_table - table_hi).astype(jnp.bfloat16)
+    received = summed.reshape(n_dev, -1).T
+    by_source = (
+        jnp.dot(received, table_hi.astype(jnp.bfloat16), preferred_element_type=jnp.float32)
+        + jnp.dot(received, table_lo, preferred_element_type=jnp.float32)
     ).reshape(n_dyl, 2, k_blk, cols_here, 2, j_blk)
     part_re = by_source[:, 0, :, :, 0] + by_source[:, 1, :, :, 1]
     part_im = by_source[:, 1, :, :, 0] - by_source[:, 0, :, :, 1]

time: 117 us -> 118 us (level)
  matrix products: 12.3 us -> 14.6 us
    all_to_all x1, waiting for transfers between devices: 13.9 us -> 15.8 us  [on_device(): lax.all_to_all(summed, ('scol', 'srow'), split_axis=0, concat_axis=0, til...]
    all_to_all x1, waiting for transfers between devices: 18.2 us -> 16.6 us  [on_device(): lax.all_to_all(flattened, 'srow', split_axis=1, concat_axis=0, tiled=True)]
    dot_general x1, matrix products: 1.46 us -> 2.85 us  [on_device(): jnp.einsum('rcp,pq->rcq', readings, project, precision=lax.Precision.HIGH)]
where the time goes in v14:
time: 118 us; the launch traced here: 117 us
  waiting for transfers between devices  40.5 us (34%)
  starting transfers between devices  18.7 us (16%)
  local copies, waits for them, and re-layouts  17.6 us (15%)
  other arithmetic  16.7 us (14%)
  matrix products  14.6 us (12%)
  blocking collectives  8.97 us (8%)
    all_to_all x1, waiting for transfers between devices, on_device(): lax.all_to_all(flattened, 'srow', split_axis=1, concat_axis=0, tiled=True)  16.6 us
    all_to_all x1, waiting for transfers between devices, on_device(): lax.all_to_all(summed, ('scol', 'srow'), split_axis=0, concat_axis=0, til...  15.8 us
    all_to_all x1, blocking collectives, on_device(): lax.all_to_all(image.astype(jnp.bfloat16), 'srow', split_axis=0, concat_a...  8.97 us
    all_to_all x1, starting transfers between devices, on_device(): lax.all_to_all(summed, ('scol', 'srow'), split_axis=0, concat_axis=0, til...  8.58 us
    all_to_all x1, waiting for transfers between devices, on_device(): lax.all_to_all(half.astype(jnp.bfloat16), 'scol', split_axis=0, concat_ax...  8.13 us
    reshape x1, local copies, waits for them, and re-layouts, on_device(): spec = spec.reshape(n_scol, 2 * k_blk * cols_here, n_pix)  7.44 us
    all_to_all x1, starting transfers between devices, on_device(): lax.all_to_all(flattened, 'srow', split_axis=1, concat_axis=0, tiled=True)  6.57 us
    dot_general x1, matrix products, on_device(): jnp.dot(forward_rows.astype(jnp.bfloat16), gathered.reshape(row_count, co...  4.28 us
  transfers between devices with their start and end apart: 3, of which 3 were waited for; matrix products, arithmetic and copies ran while one was open for 12% of the time, Pallas kernels for 0%

profile of v14, /device:TPU:0, one launch (start us, length us, event | category | flops | bytes accessed | tf_op | source)
XLA Modules:
  0.0 117.5 jit_solution(10055165902922367257)
XLA Ops:
  0.0 0.0 copy-start
  0.0 2.2 %convert_reduce_fusion = f32[64,64]{1,0:T(8,128)S(1)} fusion(bf16[64,64,256]{2,1,0:T(8,128)(2,1)} %param.8), kind=kLoop, calls=%fused_computation.7 | loop fusion | flops 2093056 | bytes 2113536 | tf_op jit(solution)/shard_map/reduce_sum | solution.py:58
  2.2 0.0 copy-done
  2.2 1.1 fusion.5
  3.3 2.9 %fusion.2 = bf16[64,64,256]{2,1,0:T(8,128)(2,1)S(1)} fusion(f32[64,64]{1,0:T(8,128)S(1)} %broadcast_multiply_fusion.1, f32[256,256,1]{1,0,2:T(8,128)S(1)} %fusion.5, bf16[64,64,256]{2,1,0:T(8,128)(2,1)} %param.8), kind=kOutput, calls=%fused_computation.11 | convolution fusion | flops 1612709888 | bytes 4472832 | tf_op jit(solution)/shard_map/rcp,pq->rcq/dot_general | solution.py:61
  6.2 0.0 copy-start.6
  6.2 2.5 %copy.50 = bf16[64,64,256]{2,0,1:T(8,128)(2,1)} copy(bf16[64,64,256]{2,1,0:T(8,128)(2,1)S(1)} %fusion.2) | data formatting | bytes 4194304 | tf_op jit(solution)/shard_map/convert_element_type | solution.py:62
  8.7 0.0 copy-start.5
  8.7 0.0 copy-start.3
  8.7 0.0 copy-start.4
  8.7 6.6 %all-to-all-start = ((bf16[64,64,256]{2,0,1:T(8,128)(2,1)}), bf16[64,64,256]{2,0,1:T(8,128)(2,1)}, u32[]{:S(2)}, u32[]{:S(2)}) async-start(bf16[64,64,256]{2,0,1:T(8,128)(2,1)} %copy.50), calls=%async_computation | async-start | bytes 4194304 | tf_op jit(solution)/shard_map/all_to_all | solution.py:64
  15.3 1.0 fusion.32
  16.4 0.0 copy-done.6
  16.4 0.1 iota_add_fusion.1
  16.4 0.6 dynamic_slice.3
  17.0 0.2 fusion.59
  17.2 0.2 copy.48
  17.3 0.1 copy.49
  17.5 1.4 %subtract_convert_fusion.1 = (bf16[512,4,128]{2,1,0:T(4,128)(2,1)S(1)}, bf16[512,4,128]{2,1,0:T(4,128)(2,1)S(1)}) fusion(f32[512,128]{1,0:T(8,128)S(1)} %get-tuple-element.31, f32[512,4]{1,0:T(8,128)S(1)} %copy.49, f32[512,128]{1,0:T(8,128)S(1)} %get-tuple-element.32, f32[512,4]{1,0:T(8,128)S(1)} %copy.48), kind=kLoop, calls=%fused_computation.29 | loop fusion | flops 2359296 | bytes 1589248 | tf_op jit(solution)/shard_map/convert.4
  18.9 0.2 neg.22
  19.1 1.0 sub.159
  20.1 0.0 copy-done.5
  20.1 0.1 copy.47
  20.2 0.0 copy-done.3
  20.2 0.0 copy-start.1
  20.3 0.0 copy-done.4
  20.3 0.1 iota_add_fusion
  20.3 0.1 subtract_multiply_fusion
  20.4 0.1 subtract_multiply_fusion.1
  20.6 1.2 %subtract_convert_fusion = bf16[16,256,256]{2,1,0:T(8,128)(2,1)S(1)} fusion(s32[256,256]{1,0:T(8,128)S(1)} %bitcast.109, s32[16,4,256]{2,1,0:T(4,128)S(1)} %get-tuple-element.12, s32[256,256]{1,0:T(8,128)S(1)} %bitcast.108, s32[16,4,256]{2,1,0:T(4,128)S(1)} %get-tuple-element.11), kind=kLoop, calls=%fused_computation.8 | loop fusion | flops 8388608 | bytes 2752512 | tf_op jit(solution)/shard_map/convert_element_type | solution.py:107
  21.8 0.7 fusion.66
  22.5 1.0 fusion.36
  23.5 0.2 maximum_maximum_fusion.1
  23.7 0.0 copy-done.1
  23.7 1.1 pad_maximum_fusion
  24.9 16.6 %all-to-all-done = bf16[64,64,256]{2,0,1:T(8,128)(2,1)} async-done(((bf16[64,64,256]{2,0,1:T(8,128)(2,1)}), bf16[64,64,256]{2,0,1:T(8,128)(2,1)}, u32[]{:S(2)}, u32[]{:S(2)}) %all-to-all-start) | async-done | bytes 2097184 | tf_op jit(solution)/shard_map/all_to_all | solution.py:64
  41.4 0.0 copy-start.2
  41.4 2.9 %copy.51 = bf16[64,8,8,256]{3,2,0,1:T(8,128)(2,1)S(1)} copy(bf16[64,8,8,256]{3,0,2,1:T(8,128)(2,1)} %bitcast.11) | data formatting | bytes 4194304 | tf_op jit(solution)/shard_map/all_to_all | solution.py:64
  44.4 0.7 copy.66
  45.1 0.0 copy-done.2
  45.1 4.3 %convolution_convert_fusion = bf16[1024,2048]{1,0:T(8,128)(2,1)} fusion(bf16[1024,512]{1,0:T(8,128)(2,1)S(1)} %bitcast.106, bf16[512,2048]{1,0:T(8,128)(2,1)S(1)} %bitcast.104), kind=kOutput, calls=%fused_computation.9 | convolution fusion | flops 2149580800 | bytes 7340032 | tf_op jit(solution)/shard_map/dot_general | solution.py:73
  49.4 7.4 %reshape.431 = bf16[16,512,256]{2,1,0:T(8,128)(2,1)} reshape(bf16[1024,2048]{1,0:T(8,128)(2,1)} %convolution_convert_fusion) | data formatting | bytes 8388608 | tf_op jit(solution)/shard_map/reshape | solution.py:78
  56.8 3.5 %fusion.69 = bf16[16,256,512]{2,1,0:T(8,128)(2,1)S(1)} fusion(bf16[16,256,256]{2,1,0:T(8,128)(2,1)S(1)} %subtract_convert_fusion, bf16[16,512,256]{2,1,0:T(8,128)(2,1)} %reshape.431), kind=kOutput, calls=%fused_computation.150 | convolution fusion | flops 1073741824 | bytes 10485760 | tf_op jit(solution)/shard_map/axp,anp->axn/dot_general | solution.py:113
  60.3 2.0 %select_reduce_fusion = bf16[16,64,512]{2,1,0:T(8,128)(2,1)} fusion(bf16[16,4,64,512]{3,2,1,0:T(8,128)(2,1)S(1)} %bitcast.98, pred[16,4,512]{2,1,0:T(4,128)(4,1)S(1)} %iota_compare_fusion.1), kind=kLoop, calls=%fused_computation.5 | loop fusion | flops 3670016 | bytes 5275648 | tf_op jit(solution)/shard_map/reduce_sum | solution.py:116
  62.2 8.6 %all-to-all-start.1 = ((bf16[128,8,512]{2,1,0:T(8,128)(2,1)}), bf16[128,8,512]{2,1,0:T(8,128)(2,1)S(1)}, u32[]{:S(2)}, u32[]{:S(2)}) async-start(bf16[128,8,512]{2,1,0:T(8,128)(2,1)} %bitcast.14), calls=%async_computation.1 | async-start | bytes 2097152 | tf_op jit(solution)/shard_map/all_to_all | solution.py:119
  70.9 0.1 fusion.62
  70.9 0.3 fusion.44
  71.3 2.9 %fusion.22 = (f32[128,1024]{0,1:T(8,128)S(1)}, f32[128,1024]{0,1:T(8,128)S(1)}, f32[128,1024]{0,1:T(8,128)}) fusion(s32[128]{0:T(128)S(1)} %get-tuple-element.30), kind=kLoop, calls=%fused_computation.54 | loop fusion | flops 1966080 | bytes 1573376 | tf_op jit(solution)/shard_map/sin | solution.py:16
  74.2 15.8 %all-to-all-done.1 = bf16[128,8,512]{2,1,0:T(8,128)(2,1)S(1)} async-done(((bf16[128,8,512]{2,1,0:T(8,128)(2,1)}), bf16[128,8,512]{2,1,0:T(8,128)(2,1)S(1)}, u32[]{:S(2)}, u32[]{:S(2)}) %all-to-all-start.1) | async-done | bytes 1048608 | tf_op jit(solution)/shard_map/all_to_all | solution.py:119
  90.0 0.4 copy.67
  90.4 0.7 fusion.41
  91.2 0.7 convolution_add_fusion
  91.9 0.8 add_reduce_fusion
  92.7 0.4 fusion.3
  93.1 0.7 copy.54
  93.8 3.5 %all-to-all-start.2 = ((bf16[16,2,32,128]{3,2,1,0:T(8,128)(2,1)}), bf16[16,2,32,128]{3,2,1,0:T(8,128)(2,1)S(1)}, u32[]{:S(2)}, u32[]{:S(2)}) async-start(bf16[16,2,32,128]{3,2,1,0:T(8,128)(2,1)} %copy.54), calls=%async_computation.2 | async-start | bytes 524288 | tf_op jit(solution)/shard_map/all_to_all | solution.py:164
  97.3 1.2 %maximum_maximum_fusion = f32[256,2048]{0,1:T(8,128)S(1)} fusion(f32[128,1024]{0,1:T(8,128)S(1)} %get-tuple-element.27, f32[128,1024]{0,1:T(8,128)} %get-tuple-element.28, f32[128,1024]{0,1:T(8,128)S(1)} %get-tuple-element.26), kind=kLoop, calls=%fused_computation.10 | loop fusion | flops 1572864 | bytes 3670016 | tf_op jit(solution)/shard_map/concatenate | solution.py:170
  98.5 8.1 %all-to-all-done.2 = bf16[16,2,32,128]{3,2,1,0:T(8,128)(2,1)S(1)} async-done(((bf16[16,2,32,128]{3,2,1,0:T(8,128)(2,1)}), bf16[16,2,32,128]{3,2,1,0:T(8,128)(2,1)S(1)}, u32[]{:S(2)}, u32[]{:S(2)}) %all-to-all-start.2) | async-done | bytes 262176 | tf_op jit(solution)/shard_map/all_to_all | solution.py:164
  106.8 1.0 fusion.6
  107.8 9.0 %all_to_all.30 = bf16[8,32,2,128]{3,1,2,0:T(8,128)(2,1)S(1)} all-to-all(bf16[8,32,2,128]{3,1,2,0:T(8,128)(2,1)S(1)} %copy.57), channel_id=1, replica_groups=mesh['srow'=8,'scol'=16] {'srow'}, dimensions={0} | all-to-all | bytes 262144 | tf_op jit(solution)/shard_map/all_to_all | solution.py:180
  116.8 0.6 copy.59
  (19 shorter events, 0.3 us)
Async XLA Ops:
  0.0 2.2 %copy-start = (f32[16,256]{1,0:T(8,128)S(1)}, f32[16,256]{1,0:T(8,128)}, u32[]{:S(2)}) copy-start(f32[16,256]{1,0:T(8,128)} %param.10) | copy-start | bytes 49156
  6.2 10.1 %copy-start.6 = (s32[8]{0:T(128)S(1)}, s32[8]{0:T(128)}, u32[]{:S(2)}) copy-start(s32[8]{0:T(128)} %constant.182.clone) | copy-start | bytes 100
  8.7 11.4 %copy-start.5 = (s32[16]{0:T(128)S(1)}, s32[16]{0:T(128)}, u32[]{:S(2)}) copy-start(s32[16]{0:T(128)} %constant.183) | copy-start | bytes 196
  8.7 11.5 %copy-start.3 = (s32[256]{0:T(256)S(1)}, s32[256]{0:T(256)}, u32[]{:S(2)}) copy-start(s32[256]{0:T(256)} %param.11) | copy-start | bytes 3076
  8.7 11.5 %copy-start.4 = (s32[16]{0:T(128)S(1)}, s32[16]{0:T(128)}, u32[]{:S(2)}) copy-start(s32[16]{0:T(128)} %constant.181.clone) | copy-start | bytes 196
  8.7 32.7 %all-to-all-start = ((bf16[64,64,256]{2,0,1:T(8,128)(2,1)}), bf16[64,64,256]{2,0,1:T(8,128)(2,1)}, u32[]{:S(2)}, u32[]{:S(2)}) async-start(bf16[64,64,256]{2,0,1:T(8,128)(2,1)} %copy.50), calls=%async_computation | async-start | bytes 4194304 | tf_op jit(solution)/shard_map/all_to_all | solution.py:64
  20.2 3.5 %copy-start.1 = (bf16[1,16,32,512]{3,2,0,1:T(8,128)(2,1)S(1)}, bf16[1,16,32,512]{3,2,0,1:T(8,128)(2,1)}, u32[]{:S(2)}) copy-start(bf16[1,16,32,512]{3,2,0,1:T(8,128)(2,1)} %sub.159) | copy-start | bytes 1572868
  41.4 3.6 %copy-start.2 = (bf16[2,16,32,512]{3,2,0,1:T(8,128)(2,1)S(1)}, bf16[2,16,32,512]{3,2,0,1:T(8,128)(2,1)}, u32[]{:S(2)}) copy-start(bf16[2,16,32,512]{3,2,0,1:T(8,128)(2,1)} %pad_maximum_fusion) | copy-start | bytes 3145732
  62.2 27.8 %all-to-all-start.1 = ((bf16[128,8,512]{2,1,0:T(8,128)(2,1)}), bf16[128,8,512]{2,1,0:T(8,128)(2,1)S(1)}, u32[]{:S(2)}, u32[]{:S(2)}) async-start(bf16[128,8,512]{2,1,0:T(8,128)(2,1)} %bitcast.14), calls=%async_computation.1 | async-start | bytes 2097152 | tf_op jit(solution)/shard_map/all_to_all | solution.py:119
  93.8 12.9 %all-to-all-start.2 = ((bf16[16,2,32,128]{3,2,1,0:T(8,128)(2,1)}), bf16[16,2,32,128]{3,2,1,0:T(8,128)(2,1)S(1)}, u32[]{:S(2)}, u32[]{:S(2)}) async-start(bf16[16,2,32,128]{3,2,1,0:T(8,128)(2,1)} %copy.54), calls=%async_computation.2 | async-start | bytes 524288 | tf_op jit(solution)/shard_map/all_to_all | solution.py:164
